TPU v7x, 512 devices: a whole 4x8x8 slice. The times are simulated.
512 devices in a mesh: area: 128 (over z, y, core), blk: 4 (over x).
Axes of the slice: x: 4, y: 8, z: 8, core: 2. Of those that a mesh axis runs over, the one named last changes fastest.
Arguments:
- activity: float32 [1024, 4, 64, 128], P('area', 'blk'), may hold values from -8 to 8
- ext_input: bfloat16 [1024, 4, 64, 128], P('area', 'blk'), may hold values from -5 to 5
- weights: bfloat16 [384, 4, 128, 512], P('area', 'blk'), may hold values from -0.25 to 0.25
- slot_dst: int32 [384], P('area'), may hold values from 0 to 7
- slot_src: int32 [384], P('area'), may hold values from 0 to 1023, as said below
- slot_count: int32 [128], P('area'), may hold values from 3 to 3, as said below
- hebb_mask: int32 [384], P('area'), may hold values 0 or 1
Outputs:
- final_activity: float32 [1024, 4, 64, 128], P('area', 'blk')
- plasticity: bfloat16 [384, 4, 128, 512], P('area', 'blk')
Inputs may be any that keep to these rules, and one draw needn't show every extreme that they name: Index i of area holds area i // 4; sources lie in areas listed for it by a connectome over the areas that always lists the area itself, the areas beside it on both sides (counted round) and the opposite one. Slots 0, 1 and 2 of index i of area have their source sub-blocks held by indices (i - 1) mod 128, (i + 1) mod 128 and (i + 64) mod 128. Among the occupied slots of one index of area, at most 1 have source sub-blocks held by one index of area (slot_src // 8); some index of area reaches 1. `slot_count`: some index of area has all 3 slots occupied.
All inputs are finite; a program needn't handle non-finite values. No bound on the sum of `hebb_mask` on one device may be relied on, other than what follows from the above.
Results may differ from a plain program's by a relative error of at most 0.014.
Values may be sent and summed in bfloat16 or wider, within the bound.
No kernel may reach another device: no remote copies, remote signals or barrier semaphores. Data moves between devices by JAX's collectives and lax.ppermute only.
A program may use at most 64 MiB of HBM per device.

v0:
```python
import jax
import jax.numpy as jnp
from jax import lax
from jax.sharding import PartitionSpec as P

STEPS = 4


euler_step = 0.5


def request_rosters(src_rows, count_now, sub_dev, n_areas, link_cap):
    slot_cap = src_rows.shape[0]
    slot_ids = jnp.arange(slot_cap)
    occupied = slot_ids < count_now
    owner_idx = src_rows // sub_dev
    local_idx = src_rows % sub_dev
    earlier = (
        (owner_idx[:, None] == owner_idx[None, :])
        & occupied[None, :]
        & (slot_ids[None, :] < slot_ids[:, None])
    )
    link_idx = jnp.minimum(jnp.sum(earlier.astype(jnp.int32), axis=1), link_cap - 1)
    matches = (
        occupied[:, None, None]
        & (owner_idx[:, None, None] == jnp.arange(n_areas)[None, :, None])
        & (link_idx[:, None, None] == jnp.arange(link_cap)[None, None, :])
    )
    request_table = jnp.sum(jnp.where(matches, (local_idx + 1)[:, None, None], 0), axis=0)
    return (occupied, owner_idx, link_idx, request_table)


def body(activity, ext_input, weights, slot_dst, slot_src, slot_count, hebb_mask):
    n_areas = lax.axis_size("area")
    my_blk = lax.axis_index("blk")
    sub_dev = activity.shape[0]
    trials = activity.shape[2]
    quarter = activity.shape[3]
    slot_cap = slot_src.shape[0]
    sub_width = weights.shape[3]
    link_cap = (slot_cap + n_areas - 1) // n_areas
    occupied, owner_idx, link_idx, request_table = request_rosters(
        slot_src, slot_count[0], sub_dev, n_areas, link_cap
    )
    needed_rows = lax.all_to_all(request_table, "area", split_axis=0, concat_axis=0, tiled=True)
    is_valid = needed_rows > 0
    pick_idx = jnp.maximum(needed_rows - 1, 0)
    select = ((slot_dst[:, None] == jnp.arange(sub_dev)[None, :]) & occupied[:, None]).astype(
        jnp.float32
    )
    slot_weights = weights[:, 0]
    pre_list = []
    post_list = []
    full_act, full_ext = (
        lax.all_gather(activity.astype(jnp.bfloat16), "blk", axis=1, tiled=True).astype(
            activity.dtype
        ),
        lax.all_gather(
            ext_input.astype(jnp.float32).astype(jnp.bfloat16), "blk", axis=1, tiled=True
        ).astype(jnp.float32),
    )
    current = full_act.transpose(0, 2, 1, 3).reshape(sub_dev, trials, sub_width)
    drive_in = full_ext.transpose(0, 2, 1, 3).reshape(sub_dev, trials, sub_width)
    rate_full = jnp.tanh(current).astype(jnp.bfloat16)
    for step_idx in range(STEPS):
        rates_own = lax.dynamic_slice_in_dim(rate_full, my_blk * quarter, quarter, 2)
        outbound_rates = jnp.where(
            is_valid[:, :, None, None], rates_own[pick_idx], jnp.zeros((), jnp.bfloat16)
        )
        presynaptic_rates = lax.all_to_all(
            outbound_rates, "area", split_axis=0, concat_axis=0, tiled=True
        )[owner_idx, link_idx]
        input_contribution = jnp.einsum(
            "xvy,xye->xve", presynaptic_rates, slot_weights, preferred_element_type=jnp.float32
        )
        partial_value = jnp.einsum(
            "kd,kts->dts", select, input_contribution, precision=lax.Precision.HIGHEST
        )
        partial_value, presynaptic_rates = (partial_value, presynaptic_rates)
        summed = lax.psum(partial_value.astype(jnp.bfloat16), "blk").astype(jnp.float32)
        current = current + euler_step * (summed - current + drive_in)
        rate_full = jnp.tanh(current).astype(jnp.bfloat16)
        pre_list.append(presynaptic_rates)
        post_list.append(rate_full)
    final_state = lax.dynamic_slice_in_dim(current, my_blk * quarter, quarter, 2)[:, None]
    pre_all = jnp.stack(pre_list, axis=1).astype(jnp.float32)
    pre_centered = (pre_all - jnp.mean(pre_all, axis=2, keepdims=True)).astype(jnp.bfloat16)
    pre_centered = pre_centered.reshape(slot_cap, STEPS * trials, quarter)
    post_all = jnp.stack(post_list, axis=1).astype(jnp.float32)
    post_centered = (post_all - jnp.mean(post_all, axis=2, keepdims=True)).astype(jnp.bfloat16)
    post_slot = post_centered[slot_dst].reshape(slot_cap, STEPS * trials, sub_width)
    change = jnp.einsum("knq,kns->kqs", pre_centered, post_slot, preferred_element_type=jnp.float32)
    gate_on = (occupied & (hebb_mask == 1)).astype(jnp.float32)
    norm_scale = (STEPS * trials) ** (-0.5)
    plasticity = (change * gate_on[:, None, None] * norm_scale).astype(jnp.bfloat16)[:, None]
    return (final_state, plasticity)


def solution(mesh):
    in_specs = (
        P("area", "blk", None, None),
        P("area", "blk", None, None),
        P("area", "blk", None, None),
        P("area"),
        P("area"),
        P("area"),
        P("area"),
    )
    out_specs = (P("area", "blk", None, None), P("area", "blk", None, None))
    return jax.shard_map(body, mesh=mesh, in_specs=in_specs, out_specs=out_specs, check_vma=False)
```

profile of v0, /device:TPU:6, one launch (start us, length us, event | category | flops | bytes accessed | tf_op | source)
XLA Modules:
  0.0 564.3 jit_solution(8893313728588876898)
XLA Ops:
  11.3 17.8 %all-to-all-start = ((s32[128,1,1]{2,1,0:T(1,128)}), s32[128,1,1]{2,1,0:T(1,128)S(1)}, u32[]{:S(2)}, u32[]{:S(2)}) async-start(s32[128,1,1]{2,1,0:T(1,128)} %copy.91), calls=%async_computation | async-start | bytes 131072 | tf_op jit(solution)/shard_map/all_to_all | solution.py:45
  30.2 13.4 %all_gather.6 = bf16[8,4,64,128]{3,2,1,0:T(8,128)(2,1)S(1)} all-gather(bf16[8,1,64,128]{3,2,1,0:T(8,128)(2,1)S(1)} %convert_element_type.74), channel_id=1, replica_groups=mesh['area'=128,'blk'=4] {'blk'}, dimensions={1}, use_global_device_ids=true | all-gather | bytes 655360 | tf_op jit(solution)/shard_map/all_gather | solution.py:55
  44.3 2.4 maximum_reduce_fusion
  46.7 2.2 gather_fusion
  48.9 2.4 compare_reduce_fusion
  51.2 3.2 fusion.4
  54.4 13.8 %all-to-all-start.1 = ((bf16[128,1,64,128]{3,2,1,0:T(8,128)(2,1)}), bf16[128,1,64,128]{3,2,1,0:T(8,128)(2,1)S(1)}, u32[]{:S(2)}, u32[]{:S(2)}) async-start(bf16[128,1,64,128]{3,2,1,0:T(8,128)(2,1)} %fusion.4), calls=%async_computation.1 | async-start | bytes 4194304 | tf_op jit(solution)/shard_map/all_to_all | solution.py:70
  69.7 51.1 %all-to-all-done.1 = bf16[128,1,64,128]{3,2,1,0:T(8,128)(2,1)S(1)} async-done(((bf16[128,1,64,128]{3,2,1,0:T(8,128)(2,1)}), bf16[128,1,64,128]{3,2,1,0:T(8,128)(2,1)S(1)}, u32[]{:S(2)}, u32[]{:S(2)}) %all-to-all-start.1) | async-done | bytes 2097184 | tf_op jit(solution)/shard_map/all_to_all | solution.py:70
  124.8 13.3 %all_gather.7 = bf16[8,4,64,128]{3,2,1,0:T(8,128)(2,1)S(1)} all-gather(bf16[8,1,64,128]{3,2,1,0:T(8,128)(2,1)S(1)} %copy-done.10), channel_id=1, replica_groups=mesh['area'=128,'blk'=4] {'blk'}, dimensions={1}, use_global_device_ids=true | all-gather | bytes 655360 | tf_op jit(solution)/shard_map/all_gather | solution.py:58
  138.2 33.5 %all-reduce.5.cloned.1.call-done = bf16[8,64,512]{2,0,1:T(8,128)(2,1)} async-done(((bf16[8,64,512]{2,0,1:T(8,128)(2,1)}), bf16[8,64,512]{2,0,1:T(8,128)(2,1)}) %all-reduce.5.cloned.1.call-update) | async-done | bytes 524304 | tf_op jit(solution)/shard_map/psum | solution.py:80
  171.7 2.2 tanh_convert_fusion.3
  178.7 67.0 %all_to_all.29 = bf16[128,1,64,128]{3,2,1,0:T(8,128)(2,1)} all-to-all(bf16[128,1,64,128]{3,2,1,0:T(8,128)(2,1)S(1)} %fusion.3), channel_id=1, replica_groups=mesh['area'=128,'blk'=4] {'area'}, dimensions={0} | all-to-all | bytes 4194304 | tf_op jit(solution)/shard_map/all_to_all | solution.py:70
  245.7 2.2 gather_fusion.3
  249.9 47.4 %all-reduce.7.cloned.1.call-done = bf16[8,64,512]{2,0,1:T(8,128)(2,1)} async-done(((bf16[8,64,512]{2,0,1:T(8,128)(2,1)}), bf16[8,64,512]{2,0,1:T(8,128)(2,1)}) %all-reduce.7.cloned.1.call-update) | async-done | bytes 524304 | tf_op jit(solution)/shard_map/psum | solution.py:80
  297.3 2.3 tanh_convert_fusion.2
  300.5 2.2 gather_fusion.4
  304.5 67.0 %all_to_all.30 = bf16[128,1,64,128]{3,2,1,0:T(8,128)(2,1)} all-to-all(bf16[128,1,64,128]{3,2,1,0:T(8,128)(2,1)S(1)} %fusion.2), channel_id=1, replica_groups=mesh['area'=128,'blk'=4] {'area'}, dimensions={0} | all-to-all | bytes 4194304 | tf_op jit(solution)/shard_map/all_to_all | solution.py:70
  375.5 47.5 %all-reduce.9.cloned.1.call-done = bf16[8,64,512]{2,0,1:T(8,128)(2,1)} async-done(((bf16[8,64,512]{2,0,1:T(8,128)(2,1)}), bf16[8,64,512]{2,0,1:T(8,128)(2,1)}) %all-reduce.9.cloned.1.call-update) | async-done | bytes 524304 | tf_op jit(solution)/shard_map/psum | solution.py:80
  423.0 2.6 tanh_convert_fusion.1
  428.5 3.1 fusion.1
  431.6 15.4 %all-to-all-start.4 = ((bf16[128,1,64,128]{3,2,1,0:T(8,128)(2,1)}), bf16[128,1,64,128]{3,2,1,0:T(8,128)(2,1)}, u32[]{:S(2)}, u32[]{:S(2)}) async-start(bf16[128,1,64,128]{3,2,1,0:T(8,128)(2,1)} %fusion.1), calls=%async_computation.4 | async-start | bytes 4194304 | tf_op jit(solution)/shard_map/all_to_all | solution.py:70
  447.1 52.0 %all-to-all-done.4 = bf16[128,1,64,128]{3,2,1,0:T(8,128)(2,1)} async-done(((bf16[128,1,64,128]{3,2,1,0:T(8,128)(2,1)}), bf16[128,1,64,128]{3,2,1,0:T(8,128)(2,1)}, u32[]{:S(2)}, u32[]{:S(2)}) %all-to-all-start.4) | async-done | bytes 2097184 | tf_op jit(solution)/shard_map/all_to_all | solution.py:70
  504.1 46.6 %all-reduce.11.cloned.1.call-done = bf16[8,64,512]{2,0,1:T(8,128)(2,1)} async-done(((bf16[8,64,512]{2,0,1:T(8,128)(2,1)}), bf16[8,64,512]{2,0,1:T(8,128)(2,1)}) %all-reduce.11.cloned.1.call-update) | async-done | bytes 524304 | tf_op jit(solution)/shard_map/psum | solution.py:80
  550.7 3.0 fusion.16
  (89 shorter events, 36.0 us)
Async XLA Ops:
  7.2 114.8 %copy-start = (bf16[3,1,128,512]{3,2,1,0:T(8,128)(2,1)S(1)}, bf16[3,1,128,512]{3,2,1,0:T(8,128)(2,1)}, u32[]{:S(2)}) copy-start(bf16[3,1,128,512]{3,2,1,0:T(8,128)(2,1)} %param.9) | copy-start | bytes 1179652
  9.7 19.4 %copy-start.11 = (pred[3]{0:T(512)(128)(4,1)}, pred[3]{0:T(512)(128)(4,1)S(1)}, u32[]{:S(2)}) copy-start(pred[3]{0:T(512)(128)(4,1)S(1)} %get-tuple-element.19) | copy-start | bytes 13
  9.9 0.6 copy-start.13
  11.3 33.0 %all-to-all-start = ((s32[128,1,1]{2,1,0:T(1,128)}), s32[128,1,1]{2,1,0:T(1,128)S(1)}, u32[]{:S(2)}, u32[]{:S(2)}) async-start(s32[128,1,1]{2,1,0:T(1,128)} %copy.91), calls=%async_computation | async-start | bytes 131072 | tf_op jit(solution)/shard_map/all_to_all | solution.py:45
  54.4 66.4 %all-to-all-start.1 = ((bf16[128,1,64,128]{3,2,1,0:T(8,128)(2,1)}), bf16[128,1,64,128]{3,2,1,0:T(8,128)(2,1)S(1)}, u32[]{:S(2)}, u32[]{:S(2)}) async-start(bf16[128,1,64,128]{3,2,1,0:T(8,128)(2,1)} %fusion.4), calls=%async_computation.1 | async-start | bytes 4194304 | tf_op jit(solution)/shard_map/all_to_all | solution.py:70
  68.2 103.5 %all-reduce.5.cloned.1.call-start = ((), (), s32[]{:S(2)}) async-start(), calls=%async_computation.5 | async-start | bytes 1048576 | tf_op jit(solution)/shard_map/psum | solution.py:80
  122.0 2.8 copy-start.10
  124.7 172.6 %all-reduce.7.cloned.1.call-start = ((), (), s32[]{:S(2)}) async-start(), calls=%async_computation.6 | async-start | bytes 1048576 | tf_op jit(solution)/shard_map/psum | solution.py:80
  173.9 0.8 copy-start.4
  245.7 51.6 %copy-start.1 = (bf16[8,64,512]{2,0,1:T(8,128)(2,1)S(1)}, bf16[8,64,512]{2,0,1:T(8,128)(2,1)}, u32[]{:S(2)}) copy-start(bf16[8,64,512]{2,0,1:T(8,128)(2,1)} %all-reduce.5.cloned.1.call-done) | copy-start | bytes 1572868
  249.8 173.1 %all-reduce.9.cloned.1.call-start = ((), (), s32[]{:S(2)}) async-start(), calls=%async_computation.7 | async-start | bytes 1048576 | tf_op jit(solution)/shard_map/psum | solution.py:80
  299.6 0.8 copy-start.2
  425.5 0.8 copy-start.6
  431.6 15.5 %copy-start.14 = (s32[3]{0:T(128)S(1)}, s32[3]{0:T(128)}, u32[]{:S(2)}) copy-start(s32[3]{0:T(128)} %param.10) | copy-start | bytes 40
  431.6 67.5 %all-to-all-start.4 = ((bf16[128,1,64,128]{3,2,1,0:T(8,128)(2,1)}), bf16[128,1,64,128]{3,2,1,0:T(8,128)(2,1)}, u32[]{:S(2)}, u32[]{:S(2)}) async-start(bf16[128,1,64,128]{3,2,1,0:T(8,128)(2,1)} %fusion.1), calls=%async_computation.4 | async-start | bytes 4194304 | tf_op jit(solution)/shard_map/all_to_all | solution.py:70
  447.0 56.2 %copy-start.9 = (bf16[3,64,128]{2,1,0:T(8,128)(2,1)S(1)}, bf16[3,64,128]{2,1,0:T(8,128)(2,1)}, u32[]{:S(2)}) copy-start(bf16[3,64,128]{2,1,0:T(8,128)(2,1)} %gather_fusion.1) | copy-start | bytes 147460
  447.1 103.7 %all-reduce.11.cloned.1.call-start = ((), (), s32[]{:S(2)}) async-start(), calls=%async_computation.8 | async-start | bytes 1048576 | tf_op jit(solution)/shard_map/psum | solution.py:80
  550.7 3.0 copy-start.3
  550.7 3.0 copy-start.5
  550.7 3.0 copy-start.7
  555.2 1.4 copy-start.8
  555.2 1.4 copy-start.12
Sparse Core Ops, SparseCore 0:
  124.8 46.8 all-reduce.4
  250.0 47.3 all-reduce.6
  375.6 47.3 all-reduce.8
  503.3 47.3 all-reduce.10
where the time goes:
time: 566 us; the launch traced here: 564 us
  waiting for transfers between devices  278 us (49%)
  blocking collectives  161 us (28%)
  starting transfers between devices  47.2 us (8%)
  other arithmetic  30.4 us (5%)
  local copies, waits for them, and re-layouts  23.6 us (4%)
  between operations  14.9 us (3%)
  matrix products  9.37 us (2%)
    psum x4, waiting for transfers between devices, body(): lax.psum(partial_value.astype(jnp.bfloat16), 'blk').astype(jnp.float32)  175 us
    all_to_all x2, blocking collectives, body(): lax.all_to_all(outbound_rates, 'area', split_axis=0, concat_axis=0, tiled...  134 us
    all_to_all x2, waiting for transfers between devices, body(): lax.all_to_all(outbound_rates, 'area', split_axis=0, concat_axis=0, tiled...  103 us
    all_to_all x2, starting transfers between devices, body(): lax.all_to_all(outbound_rates, 'area', split_axis=0, concat_axis=0, tiled...  29.2 us
    all_to_all x1, starting transfers between devices, body(): lax.all_to_all(request_table, 'area', split_axis=0, concat_axis=0, tiled=...  17.8 us
    all_gather x1, blocking collectives, body(): lax.all_gather(activity.astype(jnp.bfloat16), 'blk', axis=1, tiled=True)  13.4 us
    all_gather x1, blocking collectives, body(): lax.all_gather(ext_input.astype(jnp.float32).astype(jnp.bfloat16), 'blk',...  13.3 us
  transfers between devices with their start and end apart: 7, of which 6 were waited for; matrix products, arithmetic and copies ran while one was open for 1% of the time, Pallas kernels for 0%

commit v1 on v0

v1 whole, which is shorter than its diff:
```python
import jax
import jax.numpy as jnp
from jax import lax
from jax.sharding import PartitionSpec as P

STEPS = 4


euler_step = 0.5


def centre(x):
    xf = x.astype(jnp.float32)
    return (xf - jnp.mean(xf, axis=-2, keepdims=True)).astype(jnp.bfloat16)


def body(activity, ext_input, weights, slot_dst, slot_src, slot_count, hebb_mask):
    n_areas = lax.axis_size("area")
    n_blk = lax.axis_size("blk")
    my_blk = lax.axis_index("blk")
    sub_dev = activity.shape[0]
    trials = activity.shape[2]
    quarter = activity.shape[3]
    slot_cap = slot_src.shape[0]
    sub_width = weights.shape[3]
    offsets = (-1, 1, n_areas // 2)

    occupied = jnp.arange(slot_cap) < slot_count[0]
    select = ((slot_dst[:, None] == jnp.arange(sub_dev)[None, :]) & occupied[:, None]).astype(jnp.float32)

    wanted = jnp.clip(slot_src % sub_dev, 0, sub_dev - 1).astype(jnp.int32)
    provide = []
    for k in range(slot_cap):
        perm = [(i, (i + offsets[k]) % n_areas) for i in range(n_areas)]
        provide.append(lax.ppermute(wanted[k], "area", perm))

    w_split = weights[:, 0].reshape(slot_cap, quarter, n_blk, quarter)
    w_parts = lax.all_to_all(w_split, "blk", split_axis=2, concat_axis=2, tiled=True)
    part_of_shift = (my_blk - jnp.arange(n_blk)) % n_blk
    w_shift = jnp.take(w_parts, part_of_shift, axis=2).transpose(0, 2, 1, 3)

    def n_of(area_idx, blk_idx):
        return area_idx * n_blk + blk_idx

    def exchange(rate_own):
        got = []
        for k in range(slot_cap):
            payload = lax.dynamic_index_in_dim(rate_own, provide[k], 0, keepdims=False)
            per_shift = []
            for s in range(n_blk):
                perm = [
                    (n_of(i, b), n_of((i - offsets[k]) % n_areas, (b + s) % n_blk))
                    for i in range(n_areas)
                    for b in range(n_blk)
                ]
                per_shift.append(lax.ppermute(payload, ("area", "blk"), perm))
            got.append(jnp.stack(per_shift))
        return jnp.stack(got)

    current = activity[:, 0]
    drive_in = ext_input[:, 0].astype(jnp.float32)
    rate_own = jnp.tanh(current).astype(jnp.bfloat16)
    pre_list = []
    post_list = []
    for step_idx in range(STEPS):
        presyn = exchange(rate_own)
        contrib = jnp.einsum("ksnq,ksqv->ksnv", presyn, w_shift, preferred_element_type=jnp.float32)
        partial_value = jnp.einsum("kd,ksnv->sdnv", select, contrib, precision=lax.Precision.HIGHEST)
        summed = jnp.sum(partial_value.astype(jnp.bfloat16).astype(jnp.float32), axis=0)
        current = current + euler_step * (summed - current + drive_in)
        rate_own = jnp.tanh(current).astype(jnp.bfloat16)
        pre_list.append(presyn[:, 0])
        post_list.append(rate_own)
    final_state = current[:, None]

    pre_centered = centre(jnp.stack(pre_list, axis=1))
    post_centered = centre(jnp.stack(post_list, axis=0))
    post_sel = jnp.take(post_centered, slot_dst, axis=1).transpose(1, 0, 2, 3)
    post_whole = lax.all_gather(post_sel, "blk", axis=3, tiled=True)
    change = jnp.einsum("ktnq,ktnu->kqu", pre_centered, post_whole, preferred_element_type=jnp.float32)
    gate_on = (occupied & (hebb_mask == 1)).astype(jnp.float32)
    norm_scale = (STEPS * trials) ** (-0.5)
    plasticity = (change * gate_on[:, None, None] * norm_scale).astype(jnp.bfloat16)[:, None]
    return (final_state, plasticity)


def solution(mesh):
    in_specs = (
        P("area", "blk", None, None),
        P("area", "blk", None, None),
        P("area", "blk", None, None),
        P("area"),
        P("area"),
        P("area"),
        P("area"),
    )
    out_specs = (P("area", "blk", None, None), P("area", "blk", None, None))
    return jax.shard_map(body, mesh=mesh, in_specs=in_specs, out_specs=out_specs, check_vma=False)
```

time: 566 us -> 272 us (0.48)
  waiting for transfers between devices: 278 us -> 5.56 us
  starting transfers between devices: 47.2 us -> 227 us
  blocking collectives: 161 us -> 15.4 us
  other arithmetic: 30.4 us -> 3.04 us
  local copies, waits for them, and re-layouts: 23.6 us -> 4.86 us
  between operations: 14.9 us -> 7.84 us
    ppermute x0 -> x51, starting transfers between devices: none -> 222 us  [the longest x48 205 us: exchange(): per_shift.append(lax.ppermute(payload, ('area', 'blk'), perm))]
    psum x4 -> x0, waiting for transfers between devices: 175 us -> none  [body(): lax.psum(partial_value.astype(jnp.bfloat16), 'blk').astype(jnp.float32)]
    all_to_all x2 -> x0, blocking collectives: 134 us -> none  [body(): lax.all_to_all(outbound_rates, 'area', split_axis=0, concat_axis=0, tiled...]
    all_to_all x3 -> x1, waiting for transfers between devices: 103 us -> 0.01 us  [body(): lax.all_to_all(w_split, 'blk', split_axis=2, concat_axis=2, tiled=True)]
    all_to_all x3 -> x1, starting transfers between devices: 47 us -> 4.9 us  [body(): lax.all_to_all(w_split, 'blk', split_axis=2, concat_axis=2, tiled=True)]
    gather x9 -> x2, local copies, waits for them, and re-layouts: 16.9 us -> 1.21 us  [the longest x1 0.62 us: body(): w_shift = jnp.take(w_parts, part_of_shift, axis=2).transpose(0, 2, 1, 3)]
    all_gather x2 -> x1, blocking collectives: 26.7 us -> 15.4 us  [body(): post_whole = lax.all_gather(post_sel, 'blk', axis=3, tiled=True)]
    select_n x5 -> x3, other arithmetic: 9.92 us -> 0.79 us  [the longest x2 0.77 us: body(): post_sel = jnp.take(post_centered, slot_dst, axis=1).transpose(1, 0, 2, 3)]
  transfers between devices with their start and end apart: 7 -> 52, of which waited for: 6 -> 4; matrix products, arithmetic and copies ran while one was open for 1% -> 1% of each run, Pallas kernels for 0% -> 0%
where the time goes in v1:
time: 272 us; the launch traced here: 269 us
  starting transfers between devices  227 us (83%)
  blocking collectives  15.4 us (6%)
  between operations  7.84 us (3%)
  waiting for transfers between devices  5.56 us (2%)
  matrix products  5.43 us (2%)
  local copies, waits for them, and re-layouts  4.86 us (2%)
  other arithmetic  3.04 us (1%)
    ppermute x48, starting transfers between devices, exchange(): per_shift.append(lax.ppermute(payload, ('area', 'blk'), perm))  205 us
    ppermute x3, starting transfers between devices, body(): provide.append(lax.ppermute(wanted[k], 'area', perm))  17.1 us
    all_gather x1, blocking collectives, body(): post_whole = lax.all_gather(post_sel, 'blk', axis=3, tiled=True)  15.4 us
    ppermute x48, waiting for transfers between devices, exchange(): per_shift.append(lax.ppermute(payload, ('area', 'blk'), perm))  5.55 us
  transfers between devices with their start and end apart: 52, of which 4 were waited for; matrix products, arithmetic and copies ran while one was open for 1% of the time, Pallas kernels for 0%

profile of v1, /device:TPU:6, one launch (start us, length us, event | category | flops | bytes accessed | tf_op | source)
XLA Modules:
  0.0 269.5 jit_solution(7294866537927108117)
XLA Ops:
  2.0 13.3 %collective-permute-start = (s32[]{:T(128)}, s32[]{:T(128)}, u32[]{:S(2)}, u32[]{:S(2)}) collective-permute-start(s32[]{:T(128)} %bitcast.2), channel_id=1, source_target_pairs={{0,508},{4,0},{8,4},{12,8},{16,12},{20,16},{24,20},{28,24},{32,28}... | collective-permute-start | bytes 20 | tf_op jit(solution)/shard_map/ppermute | solution.py:35
  21.3 4.9 %all-to-all-start = ((bf16[3,128,4,128]{3,1,0,2:T(8,128)(2,1)}), bf16[3,128,4,128]{3,1,0,2:T(8,128)(2,1)S(1)}, u32[]{:S(2)}, u32[]{:S(2)}) async-start(bf16[3,128,4,128]{3,1,0,2:T(8,128)(2,1)} %copy.71), calls=%async_computation | async-start | bytes 786432 | tf_op jit(solution)/shard_map/all_to_all | solution.py:38
  37.0 5.1 %collective-permute-start.2 = (bf16[64,128]{1,0:T(8,128)(2,1)S(1)}, bf16[64,128]{1,0:T(8,128)(2,1)S(1)}, u32[]{:S(2)}, u32[]{:S(2)}) collective-permute-start(bf16[64,128]{1,0:T(8,128)(2,1)S(1)} %get-tuple-element.28), channel_id=1, source_target_pairs={{0,5},{1,6},{2,7},{3,4},{4,9},{5,10},{6,11},{7,8},{8,13},{9,14},{1... | collective-permute-start | bytes 49160 | tf_op jit(solution)/shard_map/ppermute | solution.py:56
  44.6 4.4 %collective-permute-start.14 = (bf16[64,128]{1,0:T(8,128)(2,1)S(1)}, bf16[64,128]{1,0:T(8,128)(2,1)S(1)}, u32[]{:S(2)}, u32[]{:S(2)}) collective-permute-start(bf16[64,128]{1,0:T(8,128)(2,1)S(1)} %get-tuple-element.29), channel_id=1, source_target_pairs={{0,259},{1,256},{2,257},{3,258},{4,263},{5,260},{6,261},{7,262},{8... | collective-permute-start | bytes 49160 | tf_op jit(solution)/shard_map/ppermute | solution.py:56
  49.0 6.6 %collective-permute-start.13 = (bf16[64,128]{1,0:T(8,128)(2,1)S(1)}, bf16[64,128]{1,0:T(8,128)(2,1)S(1)}, u32[]{:S(2)}, u32[]{:S(2)}) collective-permute-start(bf16[64,128]{1,0:T(8,128)(2,1)S(1)} %get-tuple-element.29), channel_id=1, source_target_pairs={{0,258},{1,259},{2,256},{3,257},{4,262},{5,263},{6,260},{7,261},{8... | collective-permute-start | bytes 49160 | tf_op jit(solution)/shard_map/ppermute | solution.py:56
  55.6 5.3 %collective-permute-start.12 = (bf16[64,128]{1,0:T(8,128)(2,1)S(1)}, bf16[64,128]{1,0:T(8,128)(2,1)S(1)}, u32[]{:S(2)}, u32[]{:S(2)}) collective-permute-start(bf16[64,128]{1,0:T(8,128)(2,1)S(1)} %get-tuple-element.29), channel_id=1, source_target_pairs={{0,257},{1,258},{2,259},{3,256},{4,261},{5,262},{6,263},{7,260},{8... | collective-permute-start | bytes 49160 | tf_op jit(solution)/shard_map/ppermute | solution.py:56
  60.9 6.3 %collective-permute-start.11 = (bf16[64,128]{1,0:T(8,128)(2,1)S(1)}, bf16[64,128]{1,0:T(8,128)(2,1)S(1)}, u32[]{:S(2)}, u32[]{:S(2)}) collective-permute-start(bf16[64,128]{1,0:T(8,128)(2,1)S(1)} %get-tuple-element.29), channel_id=1, source_target_pairs={{0,256},{1,257},{2,258},{3,259},{4,260},{5,261},{6,262},{7,263},{8... | collective-permute-start | bytes 49160 | tf_op jit(solution)/shard_map/ppermute | solution.py:56
  75.9 4.9 %collective-permute-start.7 = (bf16[64,128]{1,0:T(8,128)(2,1)S(1)}, bf16[64,128]{1,0:T(8,128)(2,1)S(1)}, u32[]{:S(2)}, u32[]{:S(2)}) collective-permute-start(bf16[64,128]{1,0:T(8,128)(2,1)S(1)} %get-tuple-element.30), channel_id=1, source_target_pairs={{0,509},{1,510},{2,511},{3,508},{4,1},{5,2},{6,3},{7,0},{8,5},{9,6... | collective-permute-start | bytes 49160 | tf_op jit(solution)/shard_map/ppermute | solution.py:56
  97.7 8.1 %collective-permute-start.26 = (bf16[64,128]{1,0:T(8,128)(2,1)S(1)}, bf16[64,128]{1,0:T(8,128)(2,1)S(1)}, u32[]{:S(2)}, u32[]{:S(2)}) collective-permute-start(bf16[64,128]{1,0:T(8,128)(2,1)S(1)} %get-tuple-element.26), channel_id=1, source_target_pairs={{0,259},{1,256},{2,257},{3,258},{4,263},{5,260},{6,261},{7,262},{8... | collective-permute-start | bytes 49160 | tf_op jit(solution)/shard_map/ppermute | solution.py:56
  108.8 8.3 %collective-permute-start.24 = (bf16[64,128]{1,0:T(8,128)(2,1)S(1)}, bf16[64,128]{1,0:T(8,128)(2,1)S(1)}, u32[]{:S(2)}, u32[]{:S(2)}) collective-permute-start(bf16[64,128]{1,0:T(8,128)(2,1)S(1)} %get-tuple-element.26), channel_id=1, source_target_pairs={{0,257},{1,258},{2,259},{3,256},{4,261},{5,262},{6,263},{7,260},{8... | collective-permute-start | bytes 49160 | tf_op jit(solution)/shard_map/ppermute | solution.py:56
  119.7 6.4 %collective-permute-start.22 = (bf16[64,128]{1,0:T(8,128)(2,1)S(1)}, bf16[64,128]{1,0:T(8,128)(2,1)S(1)}, u32[]{:S(2)}, u32[]{:S(2)}) collective-permute-start(bf16[64,128]{1,0:T(8,128)(2,1)S(1)} %get-tuple-element.27), channel_id=1, source_target_pairs={{0,511},{1,508},{2,509},{3,510},{4,3},{5,0},{6,1},{7,2},{8,7},{9,4... | collective-permute-start | bytes 49160 | tf_op jit(solution)/shard_map/ppermute | solution.py:56
  126.2 5.1 %collective-permute-start.21 = (bf16[64,128]{1,0:T(8,128)(2,1)S(1)}, bf16[64,128]{1,0:T(8,128)(2,1)S(1)}, u32[]{:S(2)}, u32[]{:S(2)}) collective-permute-start(bf16[64,128]{1,0:T(8,128)(2,1)S(1)} %get-tuple-element.27), channel_id=1, source_target_pairs={{0,510},{1,511},{2,508},{3,509},{4,2},{5,3},{6,0},{7,1},{8,6},{9,7... | collective-permute-start | bytes 49160 | tf_op jit(solution)/shard_map/ppermute | solution.py:56
  131.3 4.8 %collective-permute-start.20 = (bf16[64,128]{1,0:T(8,128)(2,1)S(1)}, bf16[64,128]{1,0:T(8,128)(2,1)S(1)}, u32[]{:S(2)}, u32[]{:S(2)}) collective-permute-start(bf16[64,128]{1,0:T(8,128)(2,1)S(1)} %get-tuple-element.27), channel_id=1, source_target_pairs={{0,509},{1,510},{2,511},{3,508},{4,1},{5,2},{6,3},{7,0},{8,5},{9,6... | collective-permute-start | bytes 49160 | tf_op jit(solution)/shard_map/ppermute | solution.py:56
  151.8 8.0 %collective-permute-start.38 = (bf16[64,128]{1,0:T(8,128)(2,1)S(1)}, bf16[64,128]{1,0:T(8,128)(2,1)S(1)}, u32[]{:S(2)}, u32[]{:S(2)}) collective-permute-start(bf16[64,128]{1,0:T(8,128)(2,1)S(1)} %get-tuple-element.23), channel_id=1, source_target_pairs={{0,259},{1,256},{2,257},{3,258},{4,263},{5,260},{6,261},{7,262},{8... | collective-permute-start | bytes 49160 | tf_op jit(solution)/shard_map/ppermute | solution.py:56
  163.3 7.8 %collective-permute-start.36 = (bf16[64,128]{1,0:T(8,128)(2,1)S(1)}, bf16[64,128]{1,0:T(8,128)(2,1)S(1)}, u32[]{:S(2)}, u32[]{:S(2)}) collective-permute-start(bf16[64,128]{1,0:T(8,128)(2,1)S(1)} %get-tuple-element.23), channel_id=1, source_target_pairs={{0,257},{1,258},{2,259},{3,256},{4,261},{5,262},{6,263},{7,260},{8... | collective-permute-start | bytes 49160 | tf_op jit(solution)/shard_map/ppermute | solution.py:56
  173.7 7.0 %collective-permute-start.34 = (bf16[64,128]{1,0:T(8,128)(2,1)S(1)}, bf16[64,128]{1,0:T(8,128)(2,1)S(1)}, u32[]{:S(2)}, u32[]{:S(2)}) collective-permute-start(bf16[64,128]{1,0:T(8,128)(2,1)S(1)} %get-tuple-element.24), channel_id=1, source_target_pairs={{0,511},{1,508},{2,509},{3,510},{4,3},{5,0},{6,1},{7,2},{8,7},{9,4... | collective-permute-start | bytes 49160 | tf_op jit(solution)/shard_map/ppermute | solution.py:56
  180.8 4.5 %collective-permute-start.33 = (bf16[64,128]{1,0:T(8,128)(2,1)S(1)}, bf16[64,128]{1,0:T(8,128)(2,1)S(1)}, u32[]{:S(2)}, u32[]{:S(2)}) collective-permute-start(bf16[64,128]{1,0:T(8,128)(2,1)S(1)} %get-tuple-element.24), channel_id=1, source_target_pairs={{0,510},{1,511},{2,508},{3,509},{4,2},{5,3},{6,0},{7,1},{8,6},{9,7... | collective-permute-start | bytes 49160 | tf_op jit(solution)/shard_map/ppermute | solution.py:56
  185.3 4.9 %collective-permute-start.32 = (bf16[64,128]{1,0:T(8,128)(2,1)S(1)}, bf16[64,128]{1,0:T(8,128)(2,1)S(1)}, u32[]{:S(2)}, u32[]{:S(2)}) collective-permute-start(bf16[64,128]{1,0:T(8,128)(2,1)S(1)} %get-tuple-element.24), channel_id=1, source_target_pairs={{0,509},{1,510},{2,511},{3,508},{4,1},{5,2},{6,3},{7,0},{8,5},{9,6... | collective-permute-start | bytes 49160 | tf_op jit(solution)/shard_map/ppermute | solution.py:56
  206.5 8.1 %collective-permute-start.50 = (bf16[64,128]{1,0:T(8,128)(2,1)S(1)}, bf16[64,128]{1,0:T(8,128)(2,1)S(1)}, u32[]{:S(2)}, u32[]{:S(2)}) collective-permute-start(bf16[64,128]{1,0:T(8,128)(2,1)S(1)} %get-tuple-element.20), channel_id=1, source_target_pairs={{0,259},{1,256},{2,257},{3,258},{4,263},{5,260},{6,261},{7,262},{8... | collective-permute-start | bytes 49160 | tf_op jit(solution)/shard_map/ppermute | solution.py:56
  217.6 8.3 %collective-permute-start.48 = (bf16[64,128]{1,0:T(8,128)(2,1)S(1)}, bf16[64,128]{1,0:T(8,128)(2,1)S(1)}, u32[]{:S(2)}, u32[]{:S(2)}) collective-permute-start(bf16[64,128]{1,0:T(8,128)(2,1)S(1)} %get-tuple-element.20), channel_id=1, source_target_pairs={{0,257},{1,258},{2,259},{3,256},{4,261},{5,262},{6,263},{7,260},{8... | collective-permute-start | bytes 49160 | tf_op jit(solution)/shard_map/ppermute | solution.py:56
  228.5 6.4 %collective-permute-start.46 = (bf16[64,128]{1,0:T(8,128)(2,1)S(1)}, bf16[64,128]{1,0:T(8,128)(2,1)S(1)}, u32[]{:S(2)}, u32[]{:S(2)}) collective-permute-start(bf16[64,128]{1,0:T(8,128)(2,1)S(1)} %get-tuple-element.21), channel_id=1, source_target_pairs={{0,511},{1,508},{2,509},{3,510},{4,3},{5,0},{6,1},{7,2},{8,7},{9,4... | collective-permute-start | bytes 49160 | tf_op jit(solution)/shard_map/ppermute | solution.py:56
  234.9 5.1 %collective-permute-start.45 = (bf16[64,128]{1,0:T(8,128)(2,1)S(1)}, bf16[64,128]{1,0:T(8,128)(2,1)S(1)}, u32[]{:S(2)}, u32[]{:S(2)}) collective-permute-start(bf16[64,128]{1,0:T(8,128)(2,1)S(1)} %get-tuple-element.21), channel_id=1, source_target_pairs={{0,510},{1,511},{2,508},{3,509},{4,2},{5,3},{6,0},{7,1},{8,6},{9,7... | collective-permute-start | bytes 49160 | tf_op jit(solution)/shard_map/ppermute | solution.py:56
  240.0 4.8 %collective-permute-start.44 = (bf16[64,128]{1,0:T(8,128)(2,1)S(1)}, bf16[64,128]{1,0:T(8,128)(2,1)S(1)}, u32[]{:S(2)}, u32[]{:S(2)}) collective-permute-start(bf16[64,128]{1,0:T(8,128)(2,1)S(1)} %get-tuple-element.21), channel_id=1, source_target_pairs={{0,509},{1,510},{2,511},{3,508},{4,1},{5,2},{6,3},{7,0},{8,5},{9,6... | collective-permute-start | bytes 49160 | tf_op jit(solution)/shard_map/ppermute | solution.py:56
  253.0 15.4 %all_gather.3 = bf16[3,4,64,512]{3,2,1,0:T(8,128)(2,1)S(1)} all-gather(bf16[3,4,64,128]{3,2,1,0:T(8,128)(2,1)S(1)} %broadcast_select_fusion), channel_id=1, replica_groups=mesh['area'=128,'blk'=4] {'blk'}, dimensions={3}, use_global_device_ids=true | all-gather | bytes 983040 | tf_op jit(solution)/shard_map/all_gather | solution.py:79
  (142 shorter events, 98.0 us)
Async XLA Ops:
  2.0 25.7 %collective-permute-start = (s32[]{:T(128)}, s32[]{:T(128)}, u32[]{:S(2)}, u32[]{:S(2)}) collective-permute-start(s32[]{:T(128)} %bitcast.2), channel_id=1, source_target_pairs={{0,508},{4,0},{8,4},{12,8},{16,12},{20,16},{24,20},{28,24},{32,28}... | collective-permute-start | bytes 20 | tf_op jit(solution)/shard_map/ppermute | solution.py:35
  21.3 64.5 %all-to-all-start = ((bf16[3,128,4,128]{3,1,0,2:T(8,128)(2,1)}), bf16[3,128,4,128]{3,1,0,2:T(8,128)(2,1)S(1)}, u32[]{:S(2)}, u32[]{:S(2)}) async-start(bf16[3,128,4,128]{3,1,0,2:T(8,128)(2,1)} %copy.71), calls=%async_computation | async-start | bytes 786432 | tf_op jit(solution)/shard_map/all_to_all | solution.py:38
  37.0 23.9 %collective-permute-start.2 = (bf16[64,128]{1,0:T(8,128)(2,1)S(1)}, bf16[64,128]{1,0:T(8,128)(2,1)S(1)}, u32[]{:S(2)}, u32[]{:S(2)}) collective-permute-start(bf16[64,128]{1,0:T(8,128)(2,1)S(1)} %get-tuple-element.28), channel_id=1, source_target_pairs={{0,5},{1,6},{2,7},{3,4},{4,9},{5,10},{6,11},{7,8},{8,13},{9,14},{1... | collective-permute-start | bytes 49160 | tf_op jit(solution)/shard_map/ppermute | solution.py:56
  42.1 25.1 %collective-permute-start.1 = (bf16[64,128]{1,0:T(8,128)(2,1)S(1)}, bf16[64,128]{1,0:T(8,128)(2,1)S(1)}, u32[]{:S(2)}, u32[]{:S(2)}) collective-permute-start(bf16[64,128]{1,0:T(8,128)(2,1)S(1)} %get-tuple-element.28), channel_id=1, source_target_pairs={{0,4},{1,5},{2,6},{3,7},{4,8},{5,9},{6,10},{7,11},{8,12},{9,13},{1... | collective-permute-start | bytes 49160 | tf_op jit(solution)/shard_map/ppermute | solution.py:56
  44.6 26.9 %collective-permute-start.14 = (bf16[64,128]{1,0:T(8,128)(2,1)S(1)}, bf16[64,128]{1,0:T(8,128)(2,1)S(1)}, u32[]{:S(2)}, u32[]{:S(2)}) collective-permute-start(bf16[64,128]{1,0:T(8,128)(2,1)S(1)} %get-tuple-element.29), channel_id=1, source_target_pairs={{0,259},{1,256},{2,257},{3,258},{4,263},{5,260},{6,261},{7,262},{8... | collective-permute-start | bytes 49160 | tf_op jit(solution)/shard_map/ppermute | solution.py:56
  49.0 26.9 %collective-permute-start.13 = (bf16[64,128]{1,0:T(8,128)(2,1)S(1)}, bf16[64,128]{1,0:T(8,128)(2,1)S(1)}, u32[]{:S(2)}, u32[]{:S(2)}) collective-permute-start(bf16[64,128]{1,0:T(8,128)(2,1)S(1)} %get-tuple-element.29), channel_id=1, source_target_pairs={{0,258},{1,259},{2,256},{3,257},{4,262},{5,263},{6,260},{7,261},{8... | collective-permute-start | bytes 49160 | tf_op jit(solution)/shard_map/ppermute | solution.py:56
  55.6 25.2 %collective-permute-start.12 = (bf16[64,128]{1,0:T(8,128)(2,1)S(1)}, bf16[64,128]{1,0:T(8,128)(2,1)S(1)}, u32[]{:S(2)}, u32[]{:S(2)}) collective-permute-start(bf16[64,128]{1,0:T(8,128)(2,1)S(1)} %get-tuple-element.29), channel_id=1, source_target_pairs={{0,257},{1,258},{2,259},{3,256},{4,261},{5,262},{6,263},{7,260},{8... | collective-permute-start | bytes 49160 | tf_op jit(solution)/shard_map/ppermute | solution.py:56
  60.9 23.4 %collective-permute-start.11 = (bf16[64,128]{1,0:T(8,128)(2,1)S(1)}, bf16[64,128]{1,0:T(8,128)(2,1)S(1)}, u32[]{:S(2)}, u32[]{:S(2)}) collective-permute-start(bf16[64,128]{1,0:T(8,128)(2,1)S(1)} %get-tuple-element.29), channel_id=1, source_target_pairs={{0,256},{1,257},{2,258},{3,259},{4,260},{5,261},{6,262},{7,263},{8... | collective-permute-start | bytes 49160 | tf_op jit(solution)/shard_map/ppermute | solution.py:56
  92.7 24.4 %collective-permute-start.16 = (bf16[64,128]{1,0:T(8,128)(2,1)S(1)}, bf16[64,128]{1,0:T(8,128)(2,1)S(1)}, u32[]{:S(2)}, u32[]{:S(2)}) collective-permute-start(bf16[64,128]{1,0:T(8,128)(2,1)S(1)} %get-tuple-element.25), channel_id=1, source_target_pairs={{0,5},{1,6},{2,7},{3,4},{4,9},{5,10},{6,11},{7,8},{8,13},{9,14},{1... | collective-permute-start | bytes 49160 | tf_op jit(solution)/shard_map/ppermute | solution.py:56
  95.8 23.9 %collective-permute-start.15 = (bf16[64,128]{1,0:T(8,128)(2,1)S(1)}, bf16[64,128]{1,0:T(8,128)(2,1)S(1)}, u32[]{:S(2)}, u32[]{:S(2)}) collective-permute-start(bf16[64,128]{1,0:T(8,128)(2,1)S(1)} %get-tuple-element.25), channel_id=1, source_target_pairs={{0,4},{1,5},{2,6},{3,7},{4,8},{5,9},{6,10},{7,11},{8,12},{9,13},{1... | collective-permute-start | bytes 49160 | tf_op jit(solution)/shard_map/ppermute | solution.py:56
  97.7 28.4 %collective-permute-start.26 = (bf16[64,128]{1,0:T(8,128)(2,1)S(1)}, bf16[64,128]{1,0:T(8,128)(2,1)S(1)}, u32[]{:S(2)}, u32[]{:S(2)}) collective-permute-start(bf16[64,128]{1,0:T(8,128)(2,1)S(1)} %get-tuple-element.26), channel_id=1, source_target_pairs={{0,259},{1,256},{2,257},{3,258},{4,263},{5,260},{6,261},{7,262},{8... | collective-permute-start | bytes 49160 | tf_op jit(solution)/shard_map/ppermute | solution.py:56
  105.9 25.4 %collective-permute-start.25 = (bf16[64,128]{1,0:T(8,128)(2,1)S(1)}, bf16[64,128]{1,0:T(8,128)(2,1)S(1)}, u32[]{:S(2)}, u32[]{:S(2)}) collective-permute-start(bf16[64,128]{1,0:T(8,128)(2,1)S(1)} %get-tuple-element.26), channel_id=1, source_target_pairs={{0,258},{1,259},{2,256},{3,257},{4,262},{5,263},{6,260},{7,261},{8... | collective-permute-start | bytes 49160 | tf_op jit(solution)/shard_map/ppermute | solution.py:56
  108.8 27.2 %collective-permute-start.24 = (bf16[64,128]{1,0:T(8,128)(2,1)S(1)}, bf16[64,128]{1,0:T(8,128)(2,1)S(1)}, u32[]{:S(2)}, u32[]{:S(2)}) collective-permute-start(bf16[64,128]{1,0:T(8,128)(2,1)S(1)} %get-tuple-element.26), channel_id=1, source_target_pairs={{0,257},{1,258},{2,259},{3,256},{4,261},{5,262},{6,263},{7,260},{8... | collective-permute-start | bytes 49160 | tf_op jit(solution)/shard_map/ppermute | solution.py:56
  147.2 23.9 %collective-permute-start.28 = (bf16[64,128]{1,0:T(8,128)(2,1)S(1)}, bf16[64,128]{1,0:T(8,128)(2,1)S(1)}, u32[]{:S(2)}, u32[]{:S(2)}) collective-permute-start(bf16[64,128]{1,0:T(8,128)(2,1)S(1)} %get-tuple-element.22), channel_id=1, source_target_pairs={{0,5},{1,6},{2,7},{3,4},{4,9},{5,10},{6,11},{7,8},{8,13},{9,14},{1... | collective-permute-start | bytes 49160 | tf_op jit(solution)/shard_map/ppermute | solution.py:56
  149.9 23.8 %collective-permute-start.27 = (bf16[64,128]{1,0:T(8,128)(2,1)S(1)}, bf16[64,128]{1,0:T(8,128)(2,1)S(1)}, u32[]{:S(2)}, u32[]{:S(2)}) collective-permute-start(bf16[64,128]{1,0:T(8,128)(2,1)S(1)} %get-tuple-element.22), channel_id=1, source_target_pairs={{0,4},{1,5},{2,6},{3,7},{4,8},{5,9},{6,10},{7,11},{8,12},{9,13},{1... | collective-permute-start | bytes 49160 | tf_op jit(solution)/shard_map/ppermute | solution.py:56
  151.8 28.9 %collective-permute-start.38 = (bf16[64,128]{1,0:T(8,128)(2,1)S(1)}, bf16[64,128]{1,0:T(8,128)(2,1)S(1)}, u32[]{:S(2)}, u32[]{:S(2)}) collective-permute-start(bf16[64,128]{1,0:T(8,128)(2,1)S(1)} %get-tuple-element.23), channel_id=1, source_target_pairs={{0,259},{1,256},{2,257},{3,258},{4,263},{5,260},{6,261},{7,262},{8... | collective-permute-start | bytes 49160 | tf_op jit(solution)/shard_map/ppermute | solution.py:56
  159.9 25.4 %collective-permute-start.37 = (bf16[64,128]{1,0:T(8,128)(2,1)S(1)}, bf16[64,128]{1,0:T(8,128)(2,1)S(1)}, u32[]{:S(2)}, u32[]{:S(2)}) collective-permute-start(bf16[64,128]{1,0:T(8,128)(2,1)S(1)} %get-tuple-element.23), channel_id=1, source_target_pairs={{0,258},{1,259},{2,256},{3,257},{4,262},{5,263},{6,260},{7,261},{8... | collective-permute-start | bytes 49160 | tf_op jit(solution)/shard_map/ppermute | solution.py:56
  163.3 26.9 %collective-permute-start.36 = (bf16[64,128]{1,0:T(8,128)(2,1)S(1)}, bf16[64,128]{1,0:T(8,128)(2,1)S(1)}, u32[]{:S(2)}, u32[]{:S(2)}) collective-permute-start(bf16[64,128]{1,0:T(8,128)(2,1)S(1)} %get-tuple-element.23), channel_id=1, source_target_pairs={{0,257},{1,258},{2,259},{3,256},{4,261},{5,262},{6,263},{7,260},{8... | collective-permute-start | bytes 49160 | tf_op jit(solution)/shard_map/ppermute | solution.py:56
  201.4 24.5 %collective-permute-start.40 = (bf16[64,128]{1,0:T(8,128)(2,1)S(1)}, bf16[64,128]{1,0:T(8,128)(2,1)S(1)}, u32[]{:S(2)}, u32[]{:S(2)}) collective-permute-start(bf16[64,128]{1,0:T(8,128)(2,1)S(1)} %get-tuple-element.19), channel_id=1, source_target_pairs={{0,5},{1,6},{2,7},{3,4},{4,9},{5,10},{6,11},{7,8},{8,13},{9,14},{1... | collective-permute-start | bytes 49160 | tf_op jit(solution)/shard_map/ppermute | solution.py:56
  204.4 24.1 %collective-permute-start.39 = (bf16[64,128]{1,0:T(8,128)(2,1)S(1)}, bf16[64,128]{1,0:T(8,128)(2,1)S(1)}, u32[]{:S(2)}, u32[]{:S(2)}) collective-permute-start(bf16[64,128]{1,0:T(8,128)(2,1)S(1)} %get-tuple-element.19), channel_id=1, source_target_pairs={{0,4},{1,5},{2,6},{3,7},{4,8},{5,9},{6,10},{7,11},{8,12},{9,13},{1... | collective-permute-start | bytes 49160 | tf_op jit(solution)/shard_map/ppermute | solution.py:56
  206.5 28.4 %collective-permute-start.50 = (bf16[64,128]{1,0:T(8,128)(2,1)S(1)}, bf16[64,128]{1,0:T(8,128)(2,1)S(1)}, u32[]{:S(2)}, u32[]{:S(2)}) collective-permute-start(bf16[64,128]{1,0:T(8,128)(2,1)S(1)} %get-tuple-element.20), channel_id=1, source_target_pairs={{0,259},{1,256},{2,257},{3,258},{4,263},{5,260},{6,261},{7,262},{8... | collective-permute-start | bytes 49160 | tf_op jit(solution)/shard_map/ppermute | solution.py:56
  214.7 25.4 %collective-permute-start.49 = (bf16[64,128]{1,0:T(8,128)(2,1)S(1)}, bf16[64,128]{1,0:T(8,128)(2,1)S(1)}, u32[]{:S(2)}, u32[]{:S(2)}) collective-permute-start(bf16[64,128]{1,0:T(8,128)(2,1)S(1)} %get-tuple-element.20), channel_id=1, source_target_pairs={{0,258},{1,259},{2,256},{3,257},{4,262},{5,263},{6,260},{7,261},{8... | collective-permute-start | bytes 49160 | tf_op jit(solution)/shard_map/ppermute | solution.py:56
  217.6 27.2 %collective-permute-start.48 = (bf16[64,128]{1,0:T(8,128)(2,1)S(1)}, bf16[64,128]{1,0:T(8,128)(2,1)S(1)}, u32[]{:S(2)}, u32[]{:S(2)}) collective-permute-start(bf16[64,128]{1,0:T(8,128)(2,1)S(1)} %get-tuple-element.20), channel_id=1, source_target_pairs={{0,257},{1,258},{2,259},{3,256},{4,261},{5,262},{6,263},{7,260},{8... | collective-permute-start | bytes 49160 | tf_op jit(solution)/shard_map/ppermute | solution.py:56
  225.9 22.5 %collective-permute-start.47 = (bf16[64,128]{1,0:T(8,128)(2,1)S(1)}, bf16[64,128]{1,0:T(8,128)(2,1)S(1)}, u32[]{:S(2)}, u32[]{:S(2)}) collective-permute-start(bf16[64,128]{1,0:T(8,128)(2,1)S(1)} %get-tuple-element.20), channel_id=1, source_target_pairs={{0,256},{1,257},{2,258},{3,259},{4,260},{5,261},{6,262},{7,263},{8... | collective-permute-start | bytes 49160 | tf_op jit(solution)/shard_map/ppermute | solution.py:56
  (32 other events, 420.2 us)

commit v2 on v1

v2 whole, which is shorter than its diff:
```python
import jax
import jax.numpy as jnp
from jax import lax
from jax.sharding import PartitionSpec as P

STEPS = 4


euler_step = 0.5


def centre(x):
    xf = x.astype(jnp.float32)
    return (xf - jnp.mean(xf, axis=-2, keepdims=True)).astype(jnp.bfloat16)


def body(activity, ext_input, weights, slot_dst, slot_src, slot_count, hebb_mask):
    n_areas = lax.axis_size("area")
    my_blk = lax.axis_index("blk")
    sub_dev = activity.shape[0]
    trials = activity.shape[2]
    quarter = activity.shape[3]
    slot_cap = slot_src.shape[0]
    sub_width = weights.shape[3]
    n_parts = sub_width // quarter
    offsets = (-1, 1, n_areas // 2)

    occupied = jnp.arange(slot_cap) < slot_count[0]
    select = ((slot_dst[:, None] == jnp.arange(sub_dev)[None, :]) & occupied[:, None]).astype(jnp.float32)

    wanted = jnp.clip(slot_src % sub_dev, 0, sub_dev - 1).astype(jnp.int32)
    provide = []
    for k in range(slot_cap):
        perm = [(i, (i + offsets[k]) % n_areas) for i in range(n_areas)]
        provide.append(lax.ppermute(wanted[k], "area", perm))

    w_full = lax.all_gather(weights[:, 0], "blk", axis=1, tiled=False)
    act_full = lax.all_gather(activity[:, 0], "blk", axis=1, tiled=False)
    ext_full = lax.all_gather(ext_input[:, 0], "blk", axis=1, tiled=False)
    current = act_full.transpose(0, 2, 1, 3).reshape(sub_dev, trials, sub_width)
    drive_in = ext_full.transpose(0, 2, 1, 3).reshape(sub_dev, trials, sub_width).astype(jnp.float32)

    def exchange(rate_full):
        got = []
        for k in range(slot_cap):
            payload = lax.dynamic_index_in_dim(rate_full, provide[k], 0, keepdims=False)
            perm = [(i, (i - offsets[k]) % n_areas) for i in range(n_areas)]
            got.append(lax.ppermute(payload, "area", perm))
        return jnp.stack(got)

    rate_full = jnp.tanh(current).astype(jnp.bfloat16)
    pre_list = []
    post_list = []
    for step_idx in range(STEPS):
        presyn = exchange(rate_full)
        presyn_parts = presyn.reshape(slot_cap, trials, n_parts, quarter)
        contrib = jnp.einsum("knjq,kjqv->kjnv", presyn_parts, w_full, preferred_element_type=jnp.float32)
        partial_value = jnp.einsum("kd,kjnv->jdnv", select, contrib, precision=lax.Precision.HIGHEST)
        summed = jnp.sum(partial_value.astype(jnp.bfloat16).astype(jnp.float32), axis=0)
        current = current + euler_step * (summed - current + drive_in)
        rate_full = jnp.tanh(current).astype(jnp.bfloat16)
        pre_list.append(lax.dynamic_slice_in_dim(presyn, my_blk * quarter, quarter, 2))
        post_list.append(rate_full)
    final_state = lax.dynamic_slice_in_dim(current, my_blk * quarter, quarter, 2)[:, None]

    pre_centered = centre(jnp.stack(pre_list, axis=1))
    post_centered = centre(jnp.stack(post_list, axis=0))
    post_sel = jnp.take(post_centered, slot_dst, axis=1).transpose(1, 0, 2, 3)
    change = jnp.einsum("ktnq,ktnu->kqu", pre_centered, post_sel, preferred_element_type=jnp.float32)
    gate_on = (occupied & (hebb_mask == 1)).astype(jnp.float32)
    norm_scale = (STEPS * trials) ** (-0.5)
    plasticity = (change * gate_on[:, None, None] * norm_scale).astype(jnp.bfloat16)[:, None]
    return (final_state, plasticity)


def solution(mesh):
    in_specs = (
        P("area", "blk", None, None),
        P("area", "blk", None, None),
        P("area", "blk", None, None),
        P("area"),
        P("area"),
        P("area"),
        P("area"),
    )
    out_specs = (P("area", "blk", None, None), P("area", "blk", None, None))
    return jax.shard_map(body, mesh=mesh, in_specs=in_specs, out_specs=out_specs, check_vma=False)
```

time: 272 us -> 178 us (0.65)
  starting transfers between devices: 227 us -> 82.6 us
  matrix products: 5.43 us -> 19.3 us
  between operations: 7.84 us -> 21.3 us
  other arithmetic: 3.04 us -> 16.3 us
  local copies, waits for them, and re-layouts: 4.86 us -> 10.5 us
  waiting for transfers between devices: 5.56 us -> 11.1 us
    ppermute x48 -> x12, starting transfers between devices: 205 us -> 65.4 us  [exchange(): got.append(lax.ppermute(payload, 'area', perm))]
    dot_general x9, matrix products: 5.43 us -> 19.3 us  [the longest x4 11.4 us: body(): jnp.einsum('kd,kjnv->jdnv', select, contrib, precision=lax.Precision.HIGH...]
    convert_element_type x6 -> x7, other arithmetic: 0.75 us -> 11.4 us  [the longest x6 11.2 us: body(): rate_full = jnp.tanh(current).astype(jnp.bfloat16)]
    all_to_all x1 -> x0, starting transfers between devices: 4.9 us -> none  [body(): lax.all_to_all(w_split, 'blk', split_axis=2, concat_axis=2, tiled=True)]
    all_gather x0 -> x2, waiting for transfers between devices: none -> 4.33 us  [the longest x1 4.31 us: body(): w_full = lax.all_gather(weights[:, 0], 'blk', axis=1, tiled=False)]
    convert_element_type x0 -> x3, local copies, waits for them, and re-layouts: none -> 3.21 us  [body(): ext_full.transpose(0, 2, 1, 3).reshape(sub_dev, trials, sub_width)]
    ppermute x48 -> x12, waiting for transfers between devices: 5.55 us -> 5.43 us  [exchange(): got.append(lax.ppermute(payload, 'area', perm))]
  transfers between devices with their start and end apart: 52 -> 17, of which waited for: 4 -> 4; matrix products, arithmetic and copies ran while one was open for 1% -> 7% of each run, Pallas kernels for 0% -> 0%
where the time goes in v2:
time: 178 us; the launch traced here: 177 us
  starting transfers between devices  82.6 us (46%)
  between operations  21.3 us (12%)
  matrix products  19.3 us (11%)
  other arithmetic  16.3 us (9%)
  blocking collectives  15.6 us (9%)
  waiting for transfers between devices  11.1 us (6%)
  local copies, waits for them, and re-layouts  10.5 us (6%)
    ppermute x12, starting transfers between devices, exchange(): got.append(lax.ppermute(payload, 'area', perm))  65.4 us
    ppermute x3, starting transfers between devices, body(): provide.append(lax.ppermute(wanted[k], 'area', perm))  17.1 us
    all_gather x1, blocking collectives, body(): ext_full = lax.all_gather(ext_input[:, 0], 'blk', axis=1, tiled=False)  15.6 us
    dot_general x4, matrix products, body(): jnp.einsum('kd,kjnv->jdnv', select, contrib, precision=lax.Precision.HIGH...  11.4 us
    convert_element_type x6, other arithmetic, body(): rate_full = jnp.tanh(current).astype(jnp.bfloat16)  11.2 us
    dot_general x4, matrix products, body(): jnp.einsum('knjq,kjqv->kjnv', presyn_parts, w_full, preferred_element_typ...  5.66 us
    ppermute x12, waiting for transfers between devices, exchange(): got.append(lax.ppermute(payload, 'area', perm))  5.43 us
    all_gather x1, waiting for transfers between devices, body(): w_full = lax.all_gather(weights[:, 0], 'blk', axis=1, tiled=False)  4.31 us
  transfers between devices with their start and end apart: 17, of which 4 were waited for; matrix products, arithmetic and copies ran while one was open for 7% of the time, Pallas kernels for 0%

profile of v2, /device:TPU:6, one launch (start us, length us, event | category | flops | bytes accessed | tf_op | source)
XLA Modules:
  0.0 176.7 jit_solution(12189536708232827035)
XLA Ops:
  9.9 13.3 %collective-permute-start = (s32[]{:T(128)}, s32[]{:T(128)}, u32[]{:S(2)}, u32[]{:S(2)}) collective-permute-start(s32[]{:T(128)} %bitcast.1), channel_id=1, source_target_pairs={{0,508},{4,0},{8,4},{12,8},{16,12},{20,16},{24,20},{28,24},{32,28}... | collective-permute-start | bytes 20 | tf_op jit(solution)/shard_map/ppermute | solution.py:35
  23.2 1.9 %collective-permute-start.2 = (s32[]{:T(128)}, s32[]{:T(128)}, u32[]{:S(2)}, u32[]{:S(2)}) collective-permute-start(s32[]{:T(128)} %bitcast.3), channel_id=1, source_target_pairs={{0,4},{4,8},{8,12},{12,16},{16,20},{20,24},{24,28},{28,32},{32,36}... | collective-permute-start | bytes 20 | tf_op jit(solution)/shard_map/ppermute | solution.py:35
  25.1 1.9 %collective-permute-start.4 = (s32[]{:T(128)}, s32[]{:T(128)}, u32[]{:S(2)}, u32[]{:S(2)}) collective-permute-start(s32[]{:T(128)} %bitcast.5), channel_id=1, source_target_pairs={{0,256},{4,260},{8,264},{12,268},{16,272},{20,276},{24,280},{28,28... | collective-permute-start | bytes 20 | tf_op jit(solution)/shard_map/ppermute | solution.py:35
  27.7 15.6 %all_gather.11 = bf16[8,4,64,128]{3,2,1,0:T(8,128)(2,1)S(1)} all-gather(bf16[8,1,64,128]{3,2,1,0:T(8,128)(2,1)} %param.8), channel_id=1, replica_groups=mesh['area'=128,'blk'=4] {'blk'}, dimensions={1}, use_global_device_ids=true | all-gather | bytes 655360 | tf_op jit(solution)/shard_map/all_gather | solution.py:39
  54.3 1.9 %collective-permute-start.1 = (bf16[64,512]{1,0:T(8,128)(2,1)S(1)}, bf16[64,512]{1,0:T(8,128)(2,1)S(1)}, u32[]{:S(2)}, u32[]{:S(2)}) collective-permute-start(bf16[64,512]{1,0:T(8,128)(2,1)S(1)} %get-tuple-element.28), channel_id=1, source_target_pairs={{0,4},{4,8},{8,12},{12,16},{16,20},{20,24},{24,28},{28,32},{32,36}... | collective-permute-start | bytes 196616 | tf_op jit(solution)/shard_map/ppermute | solution.py:48
  56.2 7.0 %collective-permute-start.3 = (bf16[64,512]{1,0:T(8,128)(2,1)S(1)}, bf16[64,512]{1,0:T(8,128)(2,1)S(1)}, u32[]{:S(2)}, u32[]{:S(2)}) collective-permute-start(bf16[64,512]{1,0:T(8,128)(2,1)S(1)} %get-tuple-element.30), channel_id=1, source_target_pairs={{0,508},{4,0},{8,4},{12,8},{16,12},{20,16},{24,20},{28,24},{32,28}... | collective-permute-start | bytes 196616 | tf_op jit(solution)/shard_map/ppermute | solution.py:48
  63.2 7.1 %collective-permute-start.5 = (bf16[64,512]{1,0:T(8,128)(2,1)S(1)}, bf16[64,512]{1,0:T(8,128)(2,1)S(1)}, u32[]{:S(2)}, u32[]{:S(2)}) collective-permute-start(bf16[64,512]{1,0:T(8,128)(2,1)S(1)} %get-tuple-element.29), channel_id=1, source_target_pairs={{0,256},{4,260},{8,264},{12,268},{16,272},{20,276},{24,280},{28,28... | collective-permute-start | bytes 196616 | tf_op jit(solution)/shard_map/ppermute | solution.py:48
  73.3 4.3 %all-gather.5.cloned.1.call-done = bf16[3,4,128,512]{3,2,1,0:T(8,128)(2,1)} async-done(((bf16[3,1,128,512]{3,2,1,0:T(8,128)(2,1)}), bf16[3,4,128,512]{3,2,1,0:T(8,128)(2,1)}) %all-gather.5.cloned.1.call-update) | async-done | bytes 1572880 | tf_op jit(solution)/shard_map/all_gather | solution.py:37
  79.4 2.9 %convert_reduce_fusion.4 = f32[64,512,8]{1,2,0:T(8,128)S(1)} fusion(pred[3,8,1,1]{1,0,3,2:T(4,128)(4,1)S(1)} %fusion.90, f32[3,4,64,512]{3,2,1,0:T(8,128)S(1)} %fusion.52), kind=kOutput, calls=%fused_computation.7 | convolution fusion | flops 40632320 | bytes 2621464 | tf_op jit(solution)/shard_map/kd,kjnv->jdnv/dot_general | solution.py:58
  83.7 1.9 %collective-permute-start.6 = (bf16[64,512]{1,0:T(8,128)(2,1)S(1)}, bf16[64,512]{1,0:T(8,128)(2,1)S(1)}, u32[]{:S(2)}, u32[]{:S(2)}) collective-permute-start(bf16[64,512]{1,0:T(8,128)(2,1)S(1)} %get-tuple-element.25), channel_id=1, source_target_pairs={{0,4},{4,8},{8,12},{12,16},{16,20},{20,24},{24,28},{28,32},{32,36}... | collective-permute-start | bytes 196616 | tf_op jit(solution)/shard_map/ppermute | solution.py:48
  85.6 7.0 %collective-permute-start.7 = (bf16[64,512]{1,0:T(8,128)(2,1)}, bf16[64,512]{1,0:T(8,128)(2,1)S(1)}, u32[]{:S(2)}, u32[]{:S(2)}) collective-permute-start(bf16[64,512]{1,0:T(8,128)(2,1)} %get-tuple-element.27), channel_id=1, source_target_pairs={{0,508},{4,0},{8,4},{12,8},{16,12},{20,16},{24,20},{28,24},{32,28}... | collective-permute-start | bytes 196616 | tf_op jit(solution)/shard_map/ppermute | solution.py:48
  92.6 8.2 %collective-permute-start.8 = (bf16[64,512]{1,0:T(8,128)(2,1)}, bf16[64,512]{1,0:T(8,128)(2,1)S(1)}, u32[]{:S(2)}, u32[]{:S(2)}) collective-permute-start(bf16[64,512]{1,0:T(8,128)(2,1)} %get-tuple-element.26), channel_id=1, source_target_pairs={{0,256},{4,260},{8,264},{12,268},{16,272},{20,276},{24,280},{28,28... | collective-permute-start | bytes 196616 | tf_op jit(solution)/shard_map/ppermute | solution.py:48
  105.0 2.9 %convert_reduce_fusion.3 = f32[64,512,8]{1,2,0:T(8,128)S(1)} fusion(pred[3,8,1,1]{1,0,3,2:T(4,128)(4,1)S(1)} %fusion.90, f32[3,4,64,512]{3,2,1,0:T(8,128)S(1)} %fusion.58), kind=kOutput, calls=%fused_computation.6 | convolution fusion | flops 40632320 | bytes 2621464 | tf_op jit(solution)/shard_map/kd,kjnv->jdnv/dot_general | solution.py:58
  111.9 7.0 %collective-permute-start.10 = (bf16[64,512]{1,0:T(8,128)(2,1)}, bf16[64,512]{1,0:T(8,128)(2,1)S(1)}, u32[]{:S(2)}, u32[]{:S(2)}) collective-permute-start(bf16[64,512]{1,0:T(8,128)(2,1)} %get-tuple-element.24), channel_id=1, source_target_pairs={{0,508},{4,0},{8,4},{12,8},{16,12},{20,16},{24,20},{28,24},{32,28}... | collective-permute-start | bytes 196616 | tf_op jit(solution)/shard_map/ppermute | solution.py:48
  118.9 8.0 %collective-permute-start.11 = (bf16[64,512]{1,0:T(8,128)(2,1)}, bf16[64,512]{1,0:T(8,128)(2,1)S(1)}, u32[]{:S(2)}, u32[]{:S(2)}) collective-permute-start(bf16[64,512]{1,0:T(8,128)(2,1)} %get-tuple-element.23), channel_id=1, source_target_pairs={{0,256},{4,260},{8,264},{12,268},{16,272},{20,276},{24,280},{28,28... | collective-permute-start | bytes 196616 | tf_op jit(solution)/shard_map/ppermute | solution.py:48
  126.9 3.0 %tanh_convert_fusion.1 = (bf16[1,8,64,512]{3,2,1,0:T(8,128)(2,1)}, f32[1,8,64,512]{3,2,1,0:T(8,128)}, bf16[1,8,64,512]{3,2,1,0:T(8,128)(2,1)}) fusion(f32[1,8,64,512]{3,2,1,0:T(8,128)S(1)} %copy-done.4, f32[64,512,8]{1,2,0:T(8,128)S(1)} %convert_reduce_fusion.3, f32[1,8,64,512]{3,2,1,0:T(8,128)S(1)} %copy-done.11, f32[64,512,8]{1,2,0:T(8,128)S(1)} %convert_reduce_fusion.4), kind=kLoop, calls=%fused_computation.58 | loop fusion | flops 2621440 | bytes 6291456 | tf_op jit(solution)/shard_map/convert_element_type | solution.py:61
  132.5 2.9 %convert_reduce_fusion.2 = f32[64,512,8]{1,2,0:T(8,128)S(1)} fusion(pred[3,8,1,1]{1,0,3,2:T(4,128)(4,1)S(1)} %fusion.90, f32[3,4,64,512]{3,2,1,0:T(8,128)S(1)} %fusion.64), kind=kOutput, calls=%fused_computation.5 | convolution fusion | flops 40632320 | bytes 2621464 | tf_op jit(solution)/shard_map/kd,kjnv->jdnv/dot_general | solution.py:58
  135.4 3.0 %tanh_convert_fusion.3 = (bf16[8,64,512]{2,1,0:T(8,128)(2,1)S(1)}, f32[8,64,512]{2,1,0:T(8,128)}) fusion(f32[64,512,8]{1,2,0:T(8,128)S(1)} %convert_reduce_fusion.2, f32[64,512,8]{1,2,0:T(8,128)S(1)} %copy-done.3, f32[8,4,8,8,128]{4,3,2,1,0:T(8,128)S(1)} %get-tuple-element.18, f32[64,512,8]{1,2,0:T(8,128)S(1)} %convert_reduce_fusion.4, ...), kind=kLoop, calls=%fused_computation.60 | loop fusion | flops 3407872 | bytes 6815744 | tf_op jit(solution)/shard_map/convert_element_type | solution.py:61
  138.5 2.1 %collective-permute-start.12 = (bf16[64,512]{1,0:T(8,128)(2,1)S(1)}, bf16[64,512]{1,0:T(8,128)(2,1)S(1)}, u32[]{:S(2)}, u32[]{:S(2)}) collective-permute-start(bf16[64,512]{1,0:T(8,128)(2,1)S(1)} %get-tuple-element.19), channel_id=1, source_target_pairs={{0,4},{4,8},{8,12},{12,16},{16,20},{20,24},{24,28},{28,32},{32,36}... | collective-permute-start | bytes 196616 | tf_op jit(solution)/shard_map/ppermute | solution.py:48
  140.5 7.0 %collective-permute-start.13 = (bf16[64,512]{1,0:T(8,128)(2,1)S(1)}, bf16[64,512]{1,0:T(8,128)(2,1)S(1)}, u32[]{:S(2)}, u32[]{:S(2)}) collective-permute-start(bf16[64,512]{1,0:T(8,128)(2,1)S(1)} %get-tuple-element.21), channel_id=1, source_target_pairs={{0,508},{4,0},{8,4},{12,8},{16,12},{20,16},{24,20},{28,24},{32,28}... | collective-permute-start | bytes 196616 | tf_op jit(solution)/shard_map/ppermute | solution.py:48
  147.5 6.5 %collective-permute-start.14 = (bf16[64,512]{1,0:T(8,128)(2,1)S(1)}, bf16[64,512]{1,0:T(8,128)(2,1)S(1)}, u32[]{:S(2)}, u32[]{:S(2)}) collective-permute-start(bf16[64,512]{1,0:T(8,128)(2,1)S(1)} %get-tuple-element.20), channel_id=1, source_target_pairs={{0,256},{4,260},{8,264},{12,268},{16,272},{20,276},{24,280},{28,28... | collective-permute-start | bytes 196616 | tf_op jit(solution)/shard_map/ppermute | solution.py:48
  154.1 3.5 %collective-permute-done.14 = bf16[64,512]{1,0:T(8,128)(2,1)S(1)} collective-permute-done((bf16[64,512]{1,0:T(8,128)(2,1)S(1)}, bf16[64,512]{1,0:T(8,128)(2,1)S(1)}, u32[]{:S(2)}, u32[]{:S(2)}) %collective-permute-start.14) | collective-permute-done | bytes 65568 | tf_op jit(solution)/shard_map/ppermute | solution.py:48
  158.2 2.9 %convert_reduce_fusion.1 = f32[64,512,8]{1,2,0:T(8,128)S(1)} fusion(pred[3,8,1,1]{1,0,3,2:T(4,128)(4,1)S(1)} %fusion.90, f32[3,4,64,512]{3,2,1,0:T(8,128)S(1)} %fusion.70), kind=kOutput, calls=%fused_computation.4 | convolution fusion | flops 40632320 | bytes 2621464 | tf_op jit(solution)/shard_map/kd,kjnv->jdnv/dot_general | solution.py:58
  167.6 2.2 %fusion.20 = bf16[3,1,128,512]{3,2,1,0:T(8,128)(2,1)} fusion(bf16[3,4,64,512]{3,2,1,0:T(8,128)(2,1)} %gather_fusion, pred[3]{0:T(512)(128)(4,1)S(1)} %get-tuple-element.37, f32[3]{0:T(128)S(1)} %get-tuple-element.36, f32[3,4,128]{2,1,0:T(4,128)S(1)} %broadcast_multiply_fusion.1, bf16[3,1,64,128]{3,2,1,0:T(8,128)(2,1)S(1)} %fusion.79, ...), kind=kOutput, calls=%fused_computation.23 | convolution fusion | flops 102236160 | bytes 1382415 | tf_op jit(solution)/shard_map/ktnq,ktnu->kqu/dot_general | solution.py:69
  (124 shorter events, 31.8 us)
Async XLA Ops:
  7.2 45.6 %all-gather.3.cloned.1.call-start = ((), (), s32[]{:S(2)}) async-start(), calls=%async_computation | async-start | bytes 1310720 | tf_op jit(solution)/shard_map/all_gather | solution.py:38
  7.9 69.7 %all-gather.5.cloned.1.call-start = ((), (), s32[]{:S(2)}) async-start(), calls=%async_computation.1 | async-start | bytes 1966080 | tf_op jit(solution)/shard_map/all_gather | solution.py:37
  9.9 37.0 %collective-permute-start = (s32[]{:T(128)}, s32[]{:T(128)}, u32[]{:S(2)}, u32[]{:S(2)}) collective-permute-start(s32[]{:T(128)} %bitcast.1), channel_id=1, source_target_pairs={{0,508},{4,0},{8,4},{12,8},{16,12},{20,16},{24,20},{28,24},{32,28}... | collective-permute-start | bytes 20 | tf_op jit(solution)/shard_map/ppermute | solution.py:35
  23.2 25.1 %collective-permute-start.2 = (s32[]{:T(128)}, s32[]{:T(128)}, u32[]{:S(2)}, u32[]{:S(2)}) collective-permute-start(s32[]{:T(128)} %bitcast.3), channel_id=1, source_target_pairs={{0,4},{4,8},{8,12},{12,16},{16,20},{20,24},{24,28},{28,32},{32,36}... | collective-permute-start | bytes 20 | tf_op jit(solution)/shard_map/ppermute | solution.py:35
  25.1 24.5 %collective-permute-start.4 = (s32[]{:T(128)}, s32[]{:T(128)}, u32[]{:S(2)}, u32[]{:S(2)}) collective-permute-start(s32[]{:T(128)} %bitcast.5), channel_id=1, source_target_pairs={{0,256},{4,260},{8,264},{12,268},{16,272},{20,276},{24,280},{28,28... | collective-permute-start | bytes 20 | tf_op jit(solution)/shard_map/ppermute | solution.py:35
  52.8 17.5 %copy-start = (f32[8,4,64,128]{3,2,1,0:T(8,128)S(1)}, f32[8,4,64,128]{3,2,1,0:T(8,128)}, u32[]{:S(2)}) copy-start(f32[8,4,64,128]{3,2,1,0:T(8,128)} %all-gather.3.cloned.1.call-done) | copy-start | bytes 3145732
  54.3 18.1 %collective-permute-start.1 = (bf16[64,512]{1,0:T(8,128)(2,1)S(1)}, bf16[64,512]{1,0:T(8,128)(2,1)S(1)}, u32[]{:S(2)}, u32[]{:S(2)}) collective-permute-start(bf16[64,512]{1,0:T(8,128)(2,1)S(1)} %get-tuple-element.28), channel_id=1, source_target_pairs={{0,4},{4,8},{8,12},{12,16},{16,20},{20,24},{24,28},{28,32},{32,36}... | collective-permute-start | bytes 196616 | tf_op jit(solution)/shard_map/ppermute | solution.py:48
  56.2 16.2 %collective-permute-start.3 = (bf16[64,512]{1,0:T(8,128)(2,1)S(1)}, bf16[64,512]{1,0:T(8,128)(2,1)S(1)}, u32[]{:S(2)}, u32[]{:S(2)}) collective-permute-start(bf16[64,512]{1,0:T(8,128)(2,1)S(1)} %get-tuple-element.30), channel_id=1, source_target_pairs={{0,508},{4,0},{8,4},{12,8},{16,12},{20,16},{24,20},{28,24},{32,28}... | collective-permute-start | bytes 196616 | tf_op jit(solution)/shard_map/ppermute | solution.py:48
  63.2 10.1 %collective-permute-start.5 = (bf16[64,512]{1,0:T(8,128)(2,1)S(1)}, bf16[64,512]{1,0:T(8,128)(2,1)S(1)}, u32[]{:S(2)}, u32[]{:S(2)}) collective-permute-start(bf16[64,512]{1,0:T(8,128)(2,1)S(1)} %get-tuple-element.29), channel_id=1, source_target_pairs={{0,256},{4,260},{8,264},{12,268},{16,272},{20,276},{24,280},{28,28... | collective-permute-start | bytes 196616 | tf_op jit(solution)/shard_map/ppermute | solution.py:48
  83.7 17.7 %collective-permute-start.6 = (bf16[64,512]{1,0:T(8,128)(2,1)S(1)}, bf16[64,512]{1,0:T(8,128)(2,1)S(1)}, u32[]{:S(2)}, u32[]{:S(2)}) collective-permute-start(bf16[64,512]{1,0:T(8,128)(2,1)S(1)} %get-tuple-element.25), channel_id=1, source_target_pairs={{0,4},{4,8},{8,12},{12,16},{16,20},{20,24},{24,28},{28,32},{32,36}... | collective-permute-start | bytes 196616 | tf_op jit(solution)/shard_map/ppermute | solution.py:48
  85.6 16.4 %collective-permute-start.7 = (bf16[64,512]{1,0:T(8,128)(2,1)}, bf16[64,512]{1,0:T(8,128)(2,1)S(1)}, u32[]{:S(2)}, u32[]{:S(2)}) collective-permute-start(bf16[64,512]{1,0:T(8,128)(2,1)} %get-tuple-element.27), channel_id=1, source_target_pairs={{0,508},{4,0},{8,4},{12,8},{16,12},{20,16},{24,20},{28,24},{32,28}... | collective-permute-start | bytes 196616 | tf_op jit(solution)/shard_map/ppermute | solution.py:48
  92.6 10.7 %collective-permute-start.8 = (bf16[64,512]{1,0:T(8,128)(2,1)}, bf16[64,512]{1,0:T(8,128)(2,1)S(1)}, u32[]{:S(2)}, u32[]{:S(2)}) collective-permute-start(bf16[64,512]{1,0:T(8,128)(2,1)} %get-tuple-element.26), channel_id=1, source_target_pairs={{0,256},{4,260},{8,264},{12,268},{16,272},{20,276},{24,280},{28,28... | collective-permute-start | bytes 196616 | tf_op jit(solution)/shard_map/ppermute | solution.py:48
  107.9 19.0 %copy-start.2 = (f32[64,512,8]{1,2,0:T(8,128)}, f32[64,512,8]{1,2,0:T(8,128)S(1)}, u32[]{:S(2)}) copy-start(f32[64,512,8]{1,2,0:T(8,128)S(1)} %convert_reduce_fusion.3) | copy-start | bytes 3145732
  107.9 19.0 %copy-start.4 = (f32[1,8,64,512]{3,2,1,0:T(8,128)S(1)}, f32[1,8,64,512]{3,2,1,0:T(8,128)}, u32[]{:S(2)}) copy-start(f32[1,8,64,512]{3,2,1,0:T(8,128)} %reshape.232) | copy-start | bytes 3145732
  107.9 19.0 %copy-start.11 = (f32[1,8,64,512]{3,2,1,0:T(8,128)S(1)}, f32[1,8,64,512]{3,2,1,0:T(8,128)}, u32[]{:S(2)}) copy-start(f32[1,8,64,512]{3,2,1,0:T(8,128)} %reshape.230) | copy-start | bytes 3145732
  110.0 20.5 %collective-permute-start.9 = (bf16[64,512]{1,0:T(8,128)(2,1)S(1)}, bf16[64,512]{1,0:T(8,128)(2,1)S(1)}, u32[]{:S(2)}, u32[]{:S(2)}) collective-permute-start(bf16[64,512]{1,0:T(8,128)(2,1)S(1)} %get-tuple-element.22), channel_id=1, source_target_pairs={{0,4},{4,8},{8,12},{12,16},{16,20},{20,24},{24,28},{28,32},{32,36}... | collective-permute-start | bytes 196616 | tf_op jit(solution)/shard_map/ppermute | solution.py:48
  111.9 18.7 %collective-permute-start.10 = (bf16[64,512]{1,0:T(8,128)(2,1)}, bf16[64,512]{1,0:T(8,128)(2,1)S(1)}, u32[]{:S(2)}, u32[]{:S(2)}) collective-permute-start(bf16[64,512]{1,0:T(8,128)(2,1)} %get-tuple-element.24), channel_id=1, source_target_pairs={{0,508},{4,0},{8,4},{12,8},{16,12},{20,16},{24,20},{28,24},{32,28}... | collective-permute-start | bytes 196616 | tf_op jit(solution)/shard_map/ppermute | solution.py:48
  118.9 11.7 %collective-permute-start.11 = (bf16[64,512]{1,0:T(8,128)(2,1)}, bf16[64,512]{1,0:T(8,128)(2,1)S(1)}, u32[]{:S(2)}, u32[]{:S(2)}) collective-permute-start(bf16[64,512]{1,0:T(8,128)(2,1)} %get-tuple-element.23), channel_id=1, source_target_pairs={{0,256},{4,260},{8,264},{12,268},{16,272},{20,276},{24,280},{28,28... | collective-permute-start | bytes 196616 | tf_op jit(solution)/shard_map/ppermute | solution.py:48
  135.4 22.2 %copy-start.18 = (bf16[3,1,64,128]{3,2,1,0:T(8,128)(2,1)S(1)}, bf16[3,1,64,128]{3,2,1,0:T(8,128)(2,1)}, u32[]{:S(2)}) copy-start(bf16[3,1,64,128]{3,2,1,0:T(8,128)(2,1)} %fusion.88) | copy-start | bytes 147460
  135.4 22.2 %copy-start.19 = (bf16[3,1,64,128]{3,2,1,0:T(8,128)(2,1)S(1)}, bf16[3,1,64,128]{3,2,1,0:T(8,128)(2,1)}, u32[]{:S(2)}) copy-start(bf16[3,1,64,128]{3,2,1,0:T(8,128)(2,1)} %fusion.85) | copy-start | bytes 147460
  138.4 19.4 %copy-start.1 = (bf16[3,4,128,512]{3,2,1,0:T(8,128)(2,1)S(1)}, bf16[3,4,128,512]{3,2,1,0:T(8,128)(2,1)}, u32[]{:S(2)}) copy-start(bf16[3,4,128,512]{3,2,1,0:T(8,128)(2,1)} %all-gather.5.cloned.1.call-done) | copy-start | bytes 4718596
  138.5 15.6 %collective-permute-start.12 = (bf16[64,512]{1,0:T(8,128)(2,1)S(1)}, bf16[64,512]{1,0:T(8,128)(2,1)S(1)}, u32[]{:S(2)}, u32[]{:S(2)}) collective-permute-start(bf16[64,512]{1,0:T(8,128)(2,1)S(1)} %get-tuple-element.19), channel_id=1, source_target_pairs={{0,4},{4,8},{8,12},{12,16},{16,20},{20,24},{24,28},{28,32},{32,36}... | collective-permute-start | bytes 196616 | tf_op jit(solution)/shard_map/ppermute | solution.py:48
  140.5 13.6 %collective-permute-start.13 = (bf16[64,512]{1,0:T(8,128)(2,1)S(1)}, bf16[64,512]{1,0:T(8,128)(2,1)S(1)}, u32[]{:S(2)}, u32[]{:S(2)}) collective-permute-start(bf16[64,512]{1,0:T(8,128)(2,1)S(1)} %get-tuple-element.21), channel_id=1, source_target_pairs={{0,508},{4,0},{8,4},{12,8},{16,12},{20,16},{24,20},{28,24},{32,28}... | collective-permute-start | bytes 196616 | tf_op jit(solution)/shard_map/ppermute | solution.py:48
  147.5 10.1 %collective-permute-start.14 = (bf16[64,512]{1,0:T(8,128)(2,1)S(1)}, bf16[64,512]{1,0:T(8,128)(2,1)S(1)}, u32[]{:S(2)}, u32[]{:S(2)}) collective-permute-start(bf16[64,512]{1,0:T(8,128)(2,1)S(1)} %get-tuple-element.20), channel_id=1, source_target_pairs={{0,256},{4,260},{8,264},{12,268},{16,272},{20,276},{24,280},{28,28... | collective-permute-start | bytes 196616 | tf_op jit(solution)/shard_map/ppermute | solution.py:48
  (15 other events, 69.1 us)
Sparse Core Ops, SparseCore 0:
  10.1 35.4 all-gather.2
  47.7 29.8 all-gather.4

commit v3 on v2

--- a/solution.py
+++ b/solution.py
@@ -26,7 +26,12 @@
     offsets = (-1, 1, n_areas // 2)
 
     occupied = jnp.arange(slot_cap) < slot_count[0]
-    select = ((slot_dst[:, None] == jnp.arange(sub_dev)[None, :]) & occupied[:, None]).astype(jnp.float32)
+    same = ((slot_dst[:, None] == slot_dst[None, :]) & occupied[None, :]).astype(jnp.float32)
+    earlier = (slot_dst[:, None] == slot_dst[None, :]) & occupied[None, :] & (
+        jnp.arange(slot_cap)[None, :] < jnp.arange(slot_cap)[:, None]
+    )
+    lead = occupied & ~jnp.any(earlier, axis=1)
+    first = ((slot_dst[:, None] == jnp.arange(sub_dev)[None, :]) & lead[:, None]).astype(jnp.float32)
 
     wanted = jnp.clip(slot_src % sub_dev, 0, sub_dev - 1).astype(jnp.int32)
     provide = []
@@ -35,10 +40,11 @@
         provide.append(lax.ppermute(wanted[k], "area", perm))
 
     w_full = lax.all_gather(weights[:, 0], "blk", axis=1, tiled=False)
-    act_full = lax.all_gather(activity[:, 0], "blk", axis=1, tiled=False)
-    ext_full = lax.all_gather(ext_input[:, 0], "blk", axis=1, tiled=False)
-    current = act_full.transpose(0, 2, 1, 3).reshape(sub_dev, trials, sub_width)
-    drive_in = ext_full.transpose(0, 2, 1, 3).reshape(sub_dev, trials, sub_width).astype(jnp.float32)
+    state = jnp.stack([activity[:, 0], ext_input[:, 0].astype(jnp.float32)], axis=1)
+    state_full = lax.all_gather(state, "blk", axis=2, tiled=False)
+    state_full = state_full.transpose(1, 0, 3, 2, 4).reshape(2, sub_dev, trials, sub_width)
+    current = state_full[0]
+    drive_in = state_full[1]
 
     def exchange(rate_full):
         got = []
@@ -55,8 +61,11 @@
         presyn = exchange(rate_full)
         presyn_parts = presyn.reshape(slot_cap, trials, n_parts, quarter)
         contrib = jnp.einsum("knjq,kjqv->kjnv", presyn_parts, w_full, preferred_element_type=jnp.float32)
-        partial_value = jnp.einsum("kd,kjnv->jdnv", select, contrib, precision=lax.Precision.HIGHEST)
-        summed = jnp.sum(partial_value.astype(jnp.bfloat16).astype(jnp.float32), axis=0)
+        per_slot = []
+        for k in range(slot_cap):
+            grouped = sum(same[k, l] * contrib[l] for l in range(slot_cap))
+            per_slot.append(jnp.sum(grouped.astype(jnp.bfloat16).astype(jnp.float32), axis=0))
+        summed = sum(first[k][:, None, None] * per_slot[k][None] for k in range(slot_cap))
         current = current + euler_step * (summed - current + drive_in)
         rate_full = jnp.tanh(current).astype(jnp.bfloat16)
         pre_list.append(lax.dynamic_slice_in_dim(presyn, my_blk * quarter, quarter, 2))

time: 178 us -> 190 us (1.067)
  other arithmetic: 16.3 us -> 42.7 us
  waiting for transfers between devices: 11.1 us -> 27.9 us
  blocking collectives: 15.6 us -> 0 us
  matrix products: 19.3 us -> 3.95 us
  starting transfers between devices: 82.6 us -> 77.5 us
  local copies, waits for them, and re-layouts: 10.5 us -> 15.4 us
    reduce_sum x0 -> x4, other arithmetic: none -> 24 us  [body(): jnp.sum(grouped.astype(jnp.bfloat16).astype(jnp.float32), axis=0)]
    all_gather x1 -> x0, blocking collectives: 15.6 us -> none  [body(): ext_full = lax.all_gather(ext_input[:, 0], 'blk', axis=1, tiled=False)]
    dot_general x4 -> x0, matrix products: 11.4 us -> none  [body(): jnp.einsum('kd,kjnv->jdnv', select, contrib, precision=lax.Precision.HIGH...]
    all_gather x1, waiting for transfers between devices: 0.02 us -> 10.3 us  [body(): state_full = lax.all_gather(state, 'blk', axis=2, tiled=False)]
    all_gather x1, waiting for transfers between devices: 4.31 us -> 11.8 us  [body(): w_full = lax.all_gather(weights[:, 0], 'blk', axis=1, tiled=False)]
    ppermute x12, starting transfers between devices: 65.4 us -> 60.3 us  [exchange(): got.append(lax.ppermute(payload, 'area', perm))]
    convert_element_type x6, other arithmetic: 11.2 us -> 6.63 us  [body(): rate_full = jnp.tanh(current).astype(jnp.bfloat16)]
    convert_element_type x3 -> x0, local copies, waits for them, and re-layouts: 3.21 us -> none  [body(): ext_full.transpose(0, 2, 1, 3).reshape(sub_dev, trials, sub_width)]
  transfers between devices with their start and end apart: 17 -> 17, of which waited for: 4 -> 5; matrix products, arithmetic and copies ran while one was open for 7% -> 6% of each run, Pallas kernels for 0% -> 0%
where the time goes in v3:
time: 190 us; the launch traced here: 189 us
  starting transfers between devices  77.5 us (41%)
  other arithmetic  42.7 us (22%)
  waiting for transfers between devices  27.9 us (15%)
  between operations  21.3 us (11%)
  local copies, waits for them, and re-layouts  15.4 us (8%)
  matrix products  3.95 us (2%)
    ppermute x12, starting transfers between devices, exchange(): got.append(lax.ppermute(payload, 'area', perm))  60.3 us
    reduce_sum x4, other arithmetic, body(): jnp.sum(grouped.astype(jnp.bfloat16).astype(jnp.float32), axis=0)  24 us
    ppermute x3, starting transfers between devices, body(): provide.append(lax.ppermute(wanted[k], 'area', perm))  17.1 us
    all_gather x1, waiting for transfers between devices, body(): w_full = lax.all_gather(weights[:, 0], 'blk', axis=1, tiled=False)  11.8 us
    all_gather x1, waiting for transfers between devices, body(): state_full = lax.all_gather(state, 'blk', axis=2, tiled=False)  10.3 us
    convert_element_type x6, other arithmetic, body(): rate_full = jnp.tanh(current).astype(jnp.bfloat16)  6.63 us
  transfers between devices with their start and end apart: 17, of which 5 were waited for; matrix products, arithmetic and copies ran while one was open for 6% of the time, Pallas kernels for 0%

profile of v3, /device:TPU:6, one launch (start us, length us, event | category | flops | bytes accessed | tf_op | source)
XLA Modules:
  0.0 188.8 jit_solution(7103056636673753418)
XLA Ops:
  11.4 13.3 %collective-permute-start = (s32[]{:T(128)}, s32[]{:T(128)}, u32[]{:S(2)}, u32[]{:S(2)}) collective-permute-start(s32[]{:T(128)} %bitcast.5), channel_id=1, source_target_pairs={{0,508},{4,0},{8,4},{12,8},{16,12},{20,16},{24,20},{28,24},{32,28}... | collective-permute-start | bytes 20 | tf_op jit(solution)/shard_map/ppermute | solution.py:40
  24.7 1.9 %collective-permute-start.4 = (s32[]{:T(128)}, s32[]{:T(128)}, u32[]{:S(2)}, u32[]{:S(2)}) collective-permute-start(s32[]{:T(128)} %bitcast.9), channel_id=1, source_target_pairs={{0,256},{4,260},{8,264},{12,268},{16,272},{20,276},{24,280},{28,28... | collective-permute-start | bytes 20 | tf_op jit(solution)/shard_map/ppermute | solution.py:40
  26.6 1.9 %collective-permute-start.2 = (s32[]{:T(128)}, s32[]{:T(128)}, u32[]{:S(2)}, u32[]{:S(2)}) collective-permute-start(s32[]{:T(128)} %bitcast.7), channel_id=1, source_target_pairs={{0,4},{4,8},{8,12},{12,16},{16,20},{20,24},{24,28},{28,32},{32,36}... | collective-permute-start | bytes 20 | tf_op jit(solution)/shard_map/ppermute | solution.py:40
  31.9 2.3 %collective-permute-done.4 = s32[]{:T(128)} collective-permute-done((s32[]{:T(128)}, s32[]{:T(128)}, u32[]{:S(2)}, u32[]{:S(2)}) %collective-permute-start.4) | collective-permute-done | bytes 36 | tf_op jit(solution)/shard_map/ppermute | solution.py:40
  38.7 10.3 %all-gather.6.cloned.1.call-done = f32[8,2,256,128]{3,2,1,0:T(8,128)} async-done(((f32[8,2,64,128]{3,2,1,0:T(8,128)}), f32[8,2,256,128]{3,2,1,0:T(8,128)}) %all-gather.6.cloned.1.call-update) | async-done | bytes 2097168 | tf_op jit(solution)/shard_map/all_gather | solution.py:44
  49.0 2.9 %copy.87 = f32[8,2,4,64,128]{4,2,1,3,0:T(4,128)S(1)} copy(f32[8,2,4,64,128]{4,3,2,1,0:T(8,128)} %bitcast.101) | data formatting | bytes 4194304 | tf_op jit(solution)/shard_map/all_gather | solution.py:44
  53.5 1.9 %collective-permute-start.1 = (bf16[64,512]{1,0:T(8,128)(2,1)S(1)}, bf16[64,512]{1,0:T(8,128)(2,1)S(1)}, u32[]{:S(2)}, u32[]{:S(2)}) collective-permute-start(bf16[64,512]{1,0:T(8,128)(2,1)S(1)} %get-tuple-element.41), channel_id=1, source_target_pairs={{0,4},{4,8},{8,12},{12,16},{16,20},{20,24},{24,28},{28,32},{32,36}... | collective-permute-start | bytes 196616 | tf_op jit(solution)/shard_map/ppermute | solution.py:54
  55.4 8.0 %collective-permute-start.5 = (bf16[64,512]{1,0:T(8,128)(2,1)S(1)}, bf16[64,512]{1,0:T(8,128)(2,1)S(1)}, u32[]{:S(2)}, u32[]{:S(2)}) collective-permute-start(bf16[64,512]{1,0:T(8,128)(2,1)S(1)} %get-tuple-element.42), channel_id=1, source_target_pairs={{0,256},{4,260},{8,264},{12,268},{16,272},{20,276},{24,280},{28,28... | collective-permute-start | bytes 196616 | tf_op jit(solution)/shard_map/ppermute | solution.py:54
  63.4 6.7 %collective-permute-start.3 = (bf16[64,512]{1,0:T(8,128)(2,1)S(1)}, bf16[64,512]{1,0:T(8,128)(2,1)S(1)}, u32[]{:S(2)}, u32[]{:S(2)}) collective-permute-start(bf16[64,512]{1,0:T(8,128)(2,1)S(1)} %get-tuple-element.43), channel_id=1, source_target_pairs={{0,508},{4,0},{8,4},{12,8},{16,12},{20,16},{24,20},{28,24},{32,28}... | collective-permute-start | bytes 196616 | tf_op jit(solution)/shard_map/ppermute | solution.py:54
  72.0 11.8 %all-gather.4.cloned.1.call-done = bf16[3,4,128,512]{3,2,1,0:T(8,128)(2,1)} async-done(((bf16[3,1,128,512]{3,2,1,0:T(8,128)(2,1)}), bf16[3,4,128,512]{3,2,1,0:T(8,128)(2,1)}) %all-gather.4.cloned.1.call-update) | async-done | bytes 1572880 | tf_op jit(solution)/shard_map/all_gather | solution.py:42
  85.7 6.0 %convert_reduce_fusion.12 = (f32[64,512]{1,0:T(8,128)S(1)}, f32[64,512]{1,0:T(8,128)S(1)}, f32[64,512]{1,0:T(8,128)S(1)}) fusion(f32[3,4,64,512]{3,2,1,0:T(8,128)S(1)} %fusion.15, f32[]{:T(128)} %bitcast.12, f32[]{:T(128)} %bitcast.11, f32[]{:T(128)} %bitcast.4, f32[]{:T(128)} %bitcast.16, f32[]{:T(128)} %bitcast.15, f32[]{:T(128)} %bitcast.14, f32[]{:T(128)} %bitcast.20, ...), kind=kLoop, calls=%fused_computation.39 | loop fusion | flops 3047424 | bytes 1966116 | tf_op jit(solution)/shard_map/reduce_sum | solution.py:67
  94.8 8.0 %collective-permute-start.8 = (bf16[64,512]{1,0:T(8,128)(2,1)}, bf16[64,512]{1,0:T(8,128)(2,1)S(1)}, u32[]{:S(2)}, u32[]{:S(2)}) collective-permute-start(bf16[64,512]{1,0:T(8,128)(2,1)} %get-tuple-element.39), channel_id=1, source_target_pairs={{0,256},{4,260},{8,264},{12,268},{16,272},{20,276},{24,280},{28,28... | collective-permute-start | bytes 196616 | tf_op jit(solution)/shard_map/ppermute | solution.py:54
  102.8 6.7 %collective-permute-start.7 = (bf16[64,512]{1,0:T(8,128)(2,1)}, bf16[64,512]{1,0:T(8,128)(2,1)S(1)}, u32[]{:S(2)}, u32[]{:S(2)}) collective-permute-start(bf16[64,512]{1,0:T(8,128)(2,1)} %get-tuple-element.40), channel_id=1, source_target_pairs={{0,508},{4,0},{8,4},{12,8},{16,12},{20,16},{24,20},{28,24},{32,28}... | collective-permute-start | bytes 196616 | tf_op jit(solution)/shard_map/ppermute | solution.py:54
  112.7 6.0 %convert_reduce_fusion.9 = (f32[64,512]{1,0:T(8,128)S(1)}, f32[64,512]{1,0:T(8,128)S(1)}, f32[64,512]{1,0:T(8,128)S(1)}) fusion(f32[3,4,64,512]{3,2,1,0:T(8,128)S(1)} %fusion.21, f32[]{:T(128)} %bitcast.12, f32[]{:T(128)} %bitcast.11, f32[]{:T(128)} %bitcast.4, f32[]{:T(128)} %bitcast.16, f32[]{:T(128)} %bitcast.15, f32[]{:T(128)} %bitcast.14, f32[]{:T(128)} %bitcast.20, ...), kind=kLoop, calls=%fused_computation.36 | loop fusion | flops 3047424 | bytes 1966116 | tf_op jit(solution)/shard_map/reduce_sum | solution.py:67
  120.6 1.9 %collective-permute-start.9 = (bf16[64,512]{1,0:T(8,128)(2,1)S(1)}, bf16[64,512]{1,0:T(8,128)(2,1)S(1)}, u32[]{:S(2)}, u32[]{:S(2)}) collective-permute-start(bf16[64,512]{1,0:T(8,128)(2,1)S(1)} %get-tuple-element.35), channel_id=1, source_target_pairs={{0,4},{4,8},{8,12},{12,16},{16,20},{20,24},{24,28},{28,32},{32,36}... | collective-permute-start | bytes 196616 | tf_op jit(solution)/shard_map/ppermute | solution.py:54
  122.5 3.1 %collective-permute-start.11 = (bf16[64,512]{1,0:T(8,128)(2,1)S(1)}, bf16[64,512]{1,0:T(8,128)(2,1)S(1)}, u32[]{:S(2)}, u32[]{:S(2)}) collective-permute-start(bf16[64,512]{1,0:T(8,128)(2,1)S(1)} %get-tuple-element.36), channel_id=1, source_target_pairs={{0,256},{4,260},{8,264},{12,268},{16,272},{20,276},{24,280},{28,28... | collective-permute-start | bytes 196616 | tf_op jit(solution)/shard_map/ppermute | solution.py:54
  125.6 6.0 %collective-permute-start.10 = (bf16[64,512]{1,0:T(8,128)(2,1)S(1)}, bf16[64,512]{1,0:T(8,128)(2,1)S(1)}, u32[]{:S(2)}, u32[]{:S(2)}) collective-permute-start(bf16[64,512]{1,0:T(8,128)(2,1)S(1)} %get-tuple-element.37), channel_id=1, source_target_pairs={{0,508},{4,0},{8,4},{12,8},{16,12},{20,16},{24,20},{28,24},{32,28}... | collective-permute-start | bytes 196616 | tf_op jit(solution)/shard_map/ppermute | solution.py:54
  134.2 6.0 %convert_reduce_fusion.6 = (f32[64,512]{1,0:T(8,128)S(1)}, f32[64,512]{1,0:T(8,128)S(1)}, f32[64,512]{1,0:T(8,128)S(1)}) fusion(f32[3,4,64,512]{3,2,1,0:T(8,128)S(1)} %fusion.27, f32[]{:T(128)} %bitcast.12, f32[]{:T(128)} %bitcast.11, f32[]{:T(128)} %bitcast.4, f32[]{:T(128)} %bitcast.16, f32[]{:T(128)} %bitcast.15, f32[]{:T(128)} %bitcast.14, f32[]{:T(128)} %bitcast.20, ...), kind=kLoop, calls=%fused_computation.33 | loop fusion | flops 3047424 | bytes 1966116 | tf_op jit(solution)/shard_map/reduce_sum | solution.py:67
  142.5 1.9 %collective-permute-start.12 = (bf16[64,512]{1,0:T(8,128)(2,1)S(1)}, bf16[64,512]{1,0:T(8,128)(2,1)}, u32[]{:S(2)}, u32[]{:S(2)}) collective-permute-start(bf16[64,512]{1,0:T(8,128)(2,1)S(1)} %get-tuple-element.32), channel_id=1, source_target_pairs={{0,4},{4,8},{8,12},{12,16},{16,20},{20,24},{24,28},{28,32},{32,36}... | collective-permute-start | bytes 196616 | tf_op jit(solution)/shard_map/ppermute | solution.py:54
  144.4 7.3 %collective-permute-start.14 = (bf16[64,512]{1,0:T(8,128)(2,1)}, bf16[64,512]{1,0:T(8,128)(2,1)}, u32[]{:S(2)}, u32[]{:S(2)}) collective-permute-start(bf16[64,512]{1,0:T(8,128)(2,1)} %get-tuple-element.33), channel_id=1, source_target_pairs={{0,256},{4,260},{8,264},{12,268},{16,272},{20,276},{24,280},{28,28... | collective-permute-start | bytes 196616 | tf_op jit(solution)/shard_map/ppermute | solution.py:54
  151.7 6.9 %collective-permute-start.13 = (bf16[64,512]{1,0:T(8,128)(2,1)}, bf16[64,512]{1,0:T(8,128)(2,1)}, u32[]{:S(2)}, u32[]{:S(2)}) collective-permute-start(bf16[64,512]{1,0:T(8,128)(2,1)} %get-tuple-element.34), channel_id=1, source_target_pairs={{0,508},{4,0},{8,4},{12,8},{16,12},{20,16},{24,20},{28,24},{32,28}... | collective-permute-start | bytes 196616 | tf_op jit(solution)/shard_map/ppermute | solution.py:54
  158.6 2.4 %tanh_convert_fusion.1 = (bf16[1,8,64,512]{3,2,1,0:T(8,128)(2,1)S(1)}, f32[1,8,64,512]{3,2,1,0:T(8,128)}, bf16[1,8,64,512]{3,2,1,0:T(8,128)(2,1)}, bf16[1,8,64,512]{3,2,1,0:T(8,128)(2,1)}) fusion(f32[64,512]{1,0:T(8,128)S(1)} %get-tuple-element.15, f32[64,512]{1,0:T(8,128)S(1)} %get-tuple-element.14, f32[64,512]{1,0:T(8,128)S(1)} %get-tuple-element.13, ...), kind=kLoop, calls=%fused_computation.12 | loop fusion | flops 7864320 | bytes 5898336 | tf_op jit(solution)/shard_map/convert_element_type | solution.py:70
  165.7 5.9 %convert_reduce_fusion.1 = (f32[64,512]{1,0:T(8,128)S(1)}, f32[64,512]{1,0:T(8,128)S(1)}, f32[64,512]{1,0:T(8,128)S(1)}) fusion(f32[3,4,64,512]{3,2,1,0:T(8,128)S(1)} %fusion.33, f32[]{:T(128)} %bitcast.20, f32[]{:T(128)} %bitcast.19, f32[]{:T(128)} %bitcast.18, f32[]{:T(128)} %bitcast.12, f32[]{:T(128)} %bitcast.11, f32[]{:T(128)} %bitcast.4, f32[]{:T(128)} %bitcast.16, ...), kind=kLoop, calls=%fused_computation.28 | loop fusion | flops 3047424 | bytes 1966116 | tf_op jit(solution)/shard_map/reduce_sum | solution.py:67
  176.7 2.2 %gather_fusion = bf16[3,4,64,512]{3,2,1,0:T(8,128)(2,1)S(1)} fusion(bf16[4,8,64,512]{3,2,1,0:T(8,128)(2,1)} %fusion, s32[1024]{0:T(1024)S(1)} %pad_clamp_fusion), kind=kCustom, calls=%fused_computation | custom fusion | bytes 1572876 | tf_op jit(solution)/shard_map/jit(_take)/gather | solution.py:77
  (165 shorter events, 35.9 us)
Async XLA Ops:
  7.2 22.9 %copy-start.36 = (s32[3]{0:T(128)S(1)}, s32[3]{0:T(128)}, u32[]{:S(2)}) copy-start(s32[3]{0:T(128)} %param.13) | copy-start | bytes 40
  7.2 41.8 %all-gather.6.cloned.1.call-start = ((), (), s32[]{:S(2)}) async-start(), calls=%async_computation.1 | async-start | bytes 2621440 | tf_op jit(solution)/shard_map/all_gather | solution.py:44
  10.0 73.9 %all-gather.4.cloned.1.call-start = ((), (), s32[]{:S(2)}) async-start(), calls=%async_computation | async-start | bytes 1966080 | tf_op jit(solution)/shard_map/all_gather | solution.py:42
  11.4 19.3 %collective-permute-start = (s32[]{:T(128)}, s32[]{:T(128)}, u32[]{:S(2)}, u32[]{:S(2)}) collective-permute-start(s32[]{:T(128)} %bitcast.5), channel_id=1, source_target_pairs={{0,508},{4,0},{8,4},{12,8},{16,12},{20,16},{24,20},{28,24},{32,28}... | collective-permute-start | bytes 20 | tf_op jit(solution)/shard_map/ppermute | solution.py:40
  24.7 9.6 %collective-permute-start.4 = (s32[]{:T(128)}, s32[]{:T(128)}, u32[]{:S(2)}, u32[]{:S(2)}) collective-permute-start(s32[]{:T(128)} %bitcast.9), channel_id=1, source_target_pairs={{0,256},{4,260},{8,264},{12,268},{16,272},{20,276},{24,280},{28,28... | collective-permute-start | bytes 20 | tf_op jit(solution)/shard_map/ppermute | solution.py:40
  26.6 8.9 %collective-permute-start.2 = (s32[]{:T(128)}, s32[]{:T(128)}, u32[]{:S(2)}, u32[]{:S(2)}) collective-permute-start(s32[]{:T(128)} %bitcast.7), channel_id=1, source_target_pairs={{0,4},{4,8},{8,12},{12,16},{16,20},{20,24},{24,28},{28,32},{32,36}... | collective-permute-start | bytes 20 | tf_op jit(solution)/shard_map/ppermute | solution.py:40
  53.5 17.1 %collective-permute-start.1 = (bf16[64,512]{1,0:T(8,128)(2,1)S(1)}, bf16[64,512]{1,0:T(8,128)(2,1)S(1)}, u32[]{:S(2)}, u32[]{:S(2)}) collective-permute-start(bf16[64,512]{1,0:T(8,128)(2,1)S(1)} %get-tuple-element.41), channel_id=1, source_target_pairs={{0,4},{4,8},{8,12},{12,16},{16,20},{20,24},{24,28},{28,32},{32,36}... | collective-permute-start | bytes 196616 | tf_op jit(solution)/shard_map/ppermute | solution.py:54
  55.4 15.2 %collective-permute-start.5 = (bf16[64,512]{1,0:T(8,128)(2,1)S(1)}, bf16[64,512]{1,0:T(8,128)(2,1)S(1)}, u32[]{:S(2)}, u32[]{:S(2)}) collective-permute-start(bf16[64,512]{1,0:T(8,128)(2,1)S(1)} %get-tuple-element.42), channel_id=1, source_target_pairs={{0,256},{4,260},{8,264},{12,268},{16,272},{20,276},{24,280},{28,28... | collective-permute-start | bytes 196616 | tf_op jit(solution)/shard_map/ppermute | solution.py:54
  63.4 8.6 %collective-permute-start.3 = (bf16[64,512]{1,0:T(8,128)(2,1)S(1)}, bf16[64,512]{1,0:T(8,128)(2,1)S(1)}, u32[]{:S(2)}, u32[]{:S(2)}) collective-permute-start(bf16[64,512]{1,0:T(8,128)(2,1)S(1)} %get-tuple-element.43), channel_id=1, source_target_pairs={{0,508},{4,0},{8,4},{12,8},{16,12},{20,16},{24,20},{28,24},{32,28}... | collective-permute-start | bytes 196616 | tf_op jit(solution)/shard_map/ppermute | solution.py:54
  91.7 20.6 %copy-start = (bf16[3,4,128,512]{3,2,1,0:T(8,128)(2,1)S(1)}, bf16[3,4,128,512]{3,2,1,0:T(8,128)(2,1)}, u32[]{:S(2)}) copy-start(bf16[3,4,128,512]{3,2,1,0:T(8,128)(2,1)} %all-gather.4.cloned.1.call-done) | copy-start | bytes 4718596
  92.9 17.3 %collective-permute-start.6 = (bf16[64,512]{1,0:T(8,128)(2,1)S(1)}, bf16[64,512]{1,0:T(8,128)(2,1)S(1)}, u32[]{:S(2)}, u32[]{:S(2)}) collective-permute-start(bf16[64,512]{1,0:T(8,128)(2,1)S(1)} %get-tuple-element.38), channel_id=1, source_target_pairs={{0,4},{4,8},{8,12},{12,16},{16,20},{20,24},{24,28},{28,32},{32,36}... | collective-permute-start | bytes 196616 | tf_op jit(solution)/shard_map/ppermute | solution.py:54
  94.8 15.4 %collective-permute-start.8 = (bf16[64,512]{1,0:T(8,128)(2,1)}, bf16[64,512]{1,0:T(8,128)(2,1)S(1)}, u32[]{:S(2)}, u32[]{:S(2)}) collective-permute-start(bf16[64,512]{1,0:T(8,128)(2,1)} %get-tuple-element.39), channel_id=1, source_target_pairs={{0,256},{4,260},{8,264},{12,268},{16,272},{20,276},{24,280},{28,28... | collective-permute-start | bytes 196616 | tf_op jit(solution)/shard_map/ppermute | solution.py:54
  102.8 8.9 %collective-permute-start.7 = (bf16[64,512]{1,0:T(8,128)(2,1)}, bf16[64,512]{1,0:T(8,128)(2,1)S(1)}, u32[]{:S(2)}, u32[]{:S(2)}) collective-permute-start(bf16[64,512]{1,0:T(8,128)(2,1)} %get-tuple-element.40), channel_id=1, source_target_pairs={{0,508},{4,0},{8,4},{12,8},{16,12},{20,16},{24,20},{28,24},{32,28}... | collective-permute-start | bytes 196616 | tf_op jit(solution)/shard_map/ppermute | solution.py:54
  120.6 11.8 %collective-permute-start.9 = (bf16[64,512]{1,0:T(8,128)(2,1)S(1)}, bf16[64,512]{1,0:T(8,128)(2,1)S(1)}, u32[]{:S(2)}, u32[]{:S(2)}) collective-permute-start(bf16[64,512]{1,0:T(8,128)(2,1)S(1)} %get-tuple-element.35), channel_id=1, source_target_pairs={{0,4},{4,8},{8,12},{12,16},{16,20},{20,24},{24,28},{28,32},{32,36}... | collective-permute-start | bytes 196616 | tf_op jit(solution)/shard_map/ppermute | solution.py:54
  122.5 10.5 %collective-permute-start.11 = (bf16[64,512]{1,0:T(8,128)(2,1)S(1)}, bf16[64,512]{1,0:T(8,128)(2,1)S(1)}, u32[]{:S(2)}, u32[]{:S(2)}) collective-permute-start(bf16[64,512]{1,0:T(8,128)(2,1)S(1)} %get-tuple-element.36), channel_id=1, source_target_pairs={{0,256},{4,260},{8,264},{12,268},{16,272},{20,276},{24,280},{28,28... | collective-permute-start | bytes 196616 | tf_op jit(solution)/shard_map/ppermute | solution.py:54
  125.6 8.0 %collective-permute-start.10 = (bf16[64,512]{1,0:T(8,128)(2,1)S(1)}, bf16[64,512]{1,0:T(8,128)(2,1)S(1)}, u32[]{:S(2)}, u32[]{:S(2)}) collective-permute-start(bf16[64,512]{1,0:T(8,128)(2,1)S(1)} %get-tuple-element.37), channel_id=1, source_target_pairs={{0,508},{4,0},{8,4},{12,8},{16,12},{20,16},{24,20},{28,24},{32,28}... | collective-permute-start | bytes 196616 | tf_op jit(solution)/shard_map/ppermute | solution.py:54
  140.3 18.3 %copy-start.2 = (f32[1,8,64,4,128]{4,3,0,2,1:T(4,128)S(1)}, f32[1,8,64,4,128]{4,3,0,2,1:T(4,128)}, u32[]{:S(2)}) copy-start(f32[1,8,64,4,128]{4,3,0,2,1:T(4,128)} %copy-done.1) | copy-start | bytes 3145732
  140.3 18.3 %copy-start.8 = (f32[1,8,64,4,128]{4,3,0,2,1:T(4,128)S(1)}, f32[1,8,64,4,128]{4,3,0,2,1:T(4,128)}, u32[]{:S(2)}) copy-start(f32[1,8,64,4,128]{4,3,0,2,1:T(4,128)} %copy-done.7) | copy-start | bytes 3145732
  140.3 18.3 %copy-start.14 = (f32[64,512]{1,0:T(8,128)S(1)}, f32[64,512]{1,0:T(8,128)}, u32[]{:S(2)}) copy-start(f32[64,512]{1,0:T(8,128)} %copy-done.13) | copy-start | bytes 393220
  140.3 18.3 %copy-start.16 = (f32[64,512]{1,0:T(8,128)S(1)}, f32[64,512]{1,0:T(8,128)}, u32[]{:S(2)}) copy-start(f32[64,512]{1,0:T(8,128)} %copy-done.15) | copy-start | bytes 393220
  140.3 18.3 %copy-start.18 = (f32[64,512]{1,0:T(8,128)S(1)}, f32[64,512]{1,0:T(8,128)}, u32[]{:S(2)}) copy-start(f32[64,512]{1,0:T(8,128)} %copy-done.17) | copy-start | bytes 393220
  142.5 18.6 %collective-permute-start.12 = (bf16[64,512]{1,0:T(8,128)(2,1)S(1)}, bf16[64,512]{1,0:T(8,128)(2,1)}, u32[]{:S(2)}, u32[]{:S(2)}) collective-permute-start(bf16[64,512]{1,0:T(8,128)(2,1)S(1)} %get-tuple-element.32), channel_id=1, source_target_pairs={{0,4},{4,8},{8,12},{12,16},{16,20},{20,24},{24,28},{28,32},{32,36}... | collective-permute-start | bytes 196616 | tf_op jit(solution)/shard_map/ppermute | solution.py:54
  144.4 17.6 %collective-permute-start.14 = (bf16[64,512]{1,0:T(8,128)(2,1)}, bf16[64,512]{1,0:T(8,128)(2,1)}, u32[]{:S(2)}, u32[]{:S(2)}) collective-permute-start(bf16[64,512]{1,0:T(8,128)(2,1)} %get-tuple-element.33), channel_id=1, source_target_pairs={{0,256},{4,260},{8,264},{12,268},{16,272},{20,276},{24,280},{28,28... | collective-permute-start | bytes 196616 | tf_op jit(solution)/shard_map/ppermute | solution.py:54
  151.7 11.2 %collective-permute-start.13 = (bf16[64,512]{1,0:T(8,128)(2,1)}, bf16[64,512]{1,0:T(8,128)(2,1)}, u32[]{:S(2)}, u32[]{:S(2)}) collective-permute-start(bf16[64,512]{1,0:T(8,128)(2,1)} %get-tuple-element.34), channel_id=1, source_target_pairs={{0,508},{4,0},{8,4},{12,8},{16,12},{20,16},{24,20},{28,24},{32,28}... | collective-permute-start | bytes 196616 | tf_op jit(solution)/shard_map/ppermute | solution.py:54
  (33 other events, 200.8 us)
Sparse Core Ops, SparseCore 0:
  10.1 38.8 all-gather.5
  51.1 32.7 all-gather.3

commit v4 on v2

--- a/solution.py
+++ b/solution.py
@@ -16,6 +16,7 @@
 
 def body(activity, ext_input, weights, slot_dst, slot_src, slot_count, hebb_mask):
     n_areas = lax.axis_size("area")
+    n_blk = lax.axis_size("blk")
     my_blk = lax.axis_index("blk")
     sub_dev = activity.shape[0]
     trials = activity.shape[2]
@@ -26,7 +27,12 @@
     offsets = (-1, 1, n_areas // 2)
 
     occupied = jnp.arange(slot_cap) < slot_count[0]
-    select = ((slot_dst[:, None] == jnp.arange(sub_dev)[None, :]) & occupied[:, None]).astype(jnp.float32)
+    same = ((slot_dst[:, None] == slot_dst[None, :]) & occupied[None, :]).astype(jnp.float32)
+    earlier = (slot_dst[:, None] == slot_dst[None, :]) & occupied[None, :] & (
+        jnp.arange(slot_cap)[None, :] < jnp.arange(slot_cap)[:, None]
+    )
+    lead = occupied & ~jnp.any(earlier, axis=1)
+    first = ((slot_dst[:, None] == jnp.arange(sub_dev)[None, :]) & lead[:, None]).astype(jnp.float32)
 
     wanted = jnp.clip(slot_src % sub_dev, 0, sub_dev - 1).astype(jnp.int32)
     provide = []
@@ -35,10 +41,16 @@
         provide.append(lax.ppermute(wanted[k], "area", perm))
 
     w_full = lax.all_gather(weights[:, 0], "blk", axis=1, tiled=False)
-    act_full = lax.all_gather(activity[:, 0], "blk", axis=1, tiled=False)
     ext_full = lax.all_gather(ext_input[:, 0], "blk", axis=1, tiled=False)
+    drive_in = ext_full.transpose(0, 2, 1, 3).reshape(sub_dev, trials, sub_width).astype(jnp.float32)
+    own_act = activity[:, 0]
+    by_shift = [own_act] + [
+        lax.ppermute(own_act, "blk", [(b, (b + s) % n_blk) for b in range(n_blk)]) for s in range(1, n_blk)
+    ]
+    by_shift = jnp.stack(by_shift, axis=1)
+    part_to_shift = (my_blk - jnp.arange(n_blk)) % n_blk
+    act_full = jnp.take(by_shift, part_to_shift, axis=1)
     current = act_full.transpose(0, 2, 1, 3).reshape(sub_dev, trials, sub_width)
-    drive_in = ext_full.transpose(0, 2, 1, 3).reshape(sub_dev, trials, sub_width).astype(jnp.float32)
 
     def exchange(rate_full):
         got = []
@@ -48,15 +60,22 @@
             got.append(lax.ppermute(payload, "area", perm))
         return jnp.stack(got)
 
+    same_b = same.astype(jnp.bfloat16)
+    w_rhs = w_full.transpose(1, 0, 2, 3).reshape(n_parts, slot_cap * quarter, sub_width)
     rate_full = jnp.tanh(current).astype(jnp.bfloat16)
     pre_list = []
     post_list = []
     for step_idx in range(STEPS):
         presyn = exchange(rate_full)
         presyn_parts = presyn.reshape(slot_cap, trials, n_parts, quarter)
-        contrib = jnp.einsum("knjq,kjqv->kjnv", presyn_parts, w_full, preferred_element_type=jnp.float32)
-        partial_value = jnp.einsum("kd,kjnv->jdnv", select, contrib, precision=lax.Precision.HIGHEST)
-        summed = jnp.sum(partial_value.astype(jnp.bfloat16).astype(jnp.float32), axis=0)
+        lhs = same_b[None, :, None, :, None] * presyn_parts.transpose(2, 1, 0, 3)[:, None]
+        lhs = lhs.reshape(n_parts, slot_cap * trials, slot_cap * quarter)
+        grouped = lax.dot_general(
+            lhs, w_rhs, (((2,), (1,)), ((0,), (0,))), preferred_element_type=jnp.float32
+        )
+        per_slot = jnp.sum(grouped.astype(jnp.bfloat16).astype(jnp.float32), axis=0)
+        per_slot = per_slot.reshape(slot_cap, trials, sub_width)
+        summed = jnp.einsum("kd,knv->dnv", first, per_slot, precision=lax.Precision.HIGHEST)
         current = current + euler_step * (summed - current + drive_in)
         rate_full = jnp.tanh(current).astype(jnp.bfloat16)
         pre_list.append(lax.dynamic_slice_in_dim(presyn, my_blk * quarter, quarter, 2))

time: 178 us -> 170 us (0.955)
  starting transfers between devices: 82.6 us -> 63.2 us
  waiting for transfers between devices: 11.1 us -> 29.1 us
  other arithmetic: 16.3 us -> 7.61 us
  local copies, waits for them, and re-layouts: 10.5 us -> 14.5 us
    ppermute x12, starting transfers between devices: 65.4 us -> 37 us  [exchange(): got.append(lax.ppermute(payload, 'area', perm))]
    ppermute x12, waiting for transfers between devices: 5.43 us -> 24.9 us  [exchange(): got.append(lax.ppermute(payload, 'area', perm))]
    ppermute x0 -> x3, starting transfers between devices: none -> 13.2 us  [body(): lax.ppermute(own_act, 'blk', [(b, (b + s) % n_blk) for b in range(n_blk)])]
    convert_element_type x6 -> x1, other arithmetic: 11.2 us -> 0.57 us  [body(): rate_full = jnp.tanh(current).astype(jnp.bfloat16)]
    mul x0 -> x9, local copies, waits for them, and re-layouts: none -> 4.75 us  [body(): same_b[None, :, None, :, None] * presyn_parts.transpose(2, 1, 0, 3)[:, None]]
    all_gather x1, waiting for transfers between devices: 4.31 us -> 0.02 us  [body(): w_full = lax.all_gather(weights[:, 0], 'blk', axis=1, tiled=False)]
    ppermute x3, starting transfers between devices: 17.1 us -> 13 us  [body(): provide.append(lax.ppermute(wanted[k], 'area', perm))]
    ppermute x3, waiting for transfers between devices: 0.01 us -> 4.07 us  [body(): provide.append(lax.ppermute(wanted[k], 'area', perm))]
  transfers between devices with their start and end apart: 17 -> 19, of which waited for: 4 -> 8; matrix products, arithmetic and copies ran while one was open for 7% -> 6% of each run, Pallas kernels for 0% -> 0%
where the time goes in v4:
time: 170 us; the launch traced here: 169 us
  starting transfers between devices  63.2 us (37%)
  waiting for transfers between devices  29.1 us (17%)
  between operations  21.2 us (12%)
  matrix products  18.1 us (11%)
  blocking collectives  15.6 us (9%)
  local copies, waits for them, and re-layouts  14.5 us (9%)
  other arithmetic  7.61 us (4%)
    ppermute x12, starting transfers between devices, exchange(): got.append(lax.ppermute(payload, 'area', perm))  37 us
    ppermute x12, waiting for transfers between devices, exchange(): got.append(lax.ppermute(payload, 'area', perm))  24.9 us
    all_gather x1, blocking collectives, body(): ext_full = lax.all_gather(ext_input[:, 0], 'blk', axis=1, tiled=False)  15.6 us
    ppermute x3, starting transfers between devices, body(): lax.ppermute(own_act, 'blk', [(b, (b + s) % n_blk) for b in range(n_blk)])  13.2 us
    ppermute x3, starting transfers between devices, body(): provide.append(lax.ppermute(wanted[k], 'area', perm))  13 us
    dot_general x4, matrix products, body(): jnp.einsum('kd,knv->dnv', first, per_slot, precision=lax.Precision.HIGHEST)  9.56 us
    dot_general x4, matrix products, body(): lax.dot_general(lhs, w_rhs, (((2,), (1,)), ((0,), (0,))), preferred_eleme...  7.43 us
    mul x9, local copies, waits for them, and re-layouts, body(): same_b[None, :, None, :, None] * presyn_parts.transpose(2, 1, 0, 3)[:, None]  4.75 us
  transfers between devices with their start and end apart: 19, of which 8 were waited for; matrix products, arithmetic and copies ran while one was open for 6% of the time, Pallas kernels for 0%

profile of v4, /device:TPU:6, one launch (start us, length us, event | category | flops | bytes accessed | tf_op | source)
XLA Modules:
  0.0 169.3 jit_solution(10723410463534128339)
XLA Ops:
  7.2 2.9 %collective-permute-start.2 = (f32[8,64,128]{2,1,0:T(8,128)}, f32[8,64,128]{2,1,0:T(8,128)S(1)}, u32[]{:S(2)}, u32[]{:S(2)}) collective-permute-start(f32[8,64,128]{2,1,0:T(8,128)} %bitcast.166), channel_id=1, source_target_pairs={{0,3},{1,0},{2,1},{3,2},{4,7},{5,4},{6,5},{7,6},{8,11},{9,8},{10,9... | collective-permute-start | bytes 786440 | tf_op jit(solution)/shard_map/ppermute | solution.py:48
  10.1 8.4 %collective-permute-start.1 = (f32[8,64,128]{2,1,0:T(8,128)}, f32[8,64,128]{2,1,0:T(8,128)S(1)}, u32[]{:S(2)}, u32[]{:S(2)}) collective-permute-start(f32[8,64,128]{2,1,0:T(8,128)} %bitcast.167), channel_id=1, source_target_pairs={{0,2},{1,3},{2,0},{3,1},{4,6},{5,7},{6,4},{7,5},{8,10},{9,11},{10,... | collective-permute-start | bytes 786440 | tf_op jit(solution)/shard_map/ppermute | solution.py:48
  21.7 9.2 %collective-permute-start.3 = (s32[]{:T(128)}, s32[]{:T(128)}, u32[]{:S(2)}, u32[]{:S(2)}) collective-permute-start(s32[]{:T(128)} %bitcast.11), channel_id=1, source_target_pairs={{0,508},{4,0},{8,4},{12,8},{16,12},{20,16},{24,20},{28,24},{32,28}... | collective-permute-start | bytes 20 | tf_op jit(solution)/shard_map/ppermute | solution.py:41
  30.9 1.9 %collective-permute-start.7 = (s32[]{:T(128)}, s32[]{:T(128)}, u32[]{:S(2)}, u32[]{:S(2)}) collective-permute-start(s32[]{:T(128)} %bitcast.13), channel_id=1, source_target_pairs={{0,256},{4,260},{8,264},{12,268},{16,272},{20,276},{24,280},{28,28... | collective-permute-start | bytes 20 | tf_op jit(solution)/shard_map/ppermute | solution.py:41
  35.3 15.6 %all_gather.7 = bf16[8,4,64,128]{3,2,1,0:T(8,128)(2,1)S(1)} all-gather(bf16[8,1,64,128]{3,2,1,0:T(8,128)(2,1)} %param.8), channel_id=1, replica_groups=mesh['area'=128,'blk'=4] {'blk'}, dimensions={1}, use_global_device_ids=true | all-gather | bytes 655360 | tf_op jit(solution)/shard_map/all_gather | solution.py:44
  56.8 4.1 %collective-permute-done.5 = s32[]{:T(128)} collective-permute-done((s32[]{:T(128)}, s32[]{:T(128)}, u32[]{:S(2)}, u32[]{:S(2)}) %collective-permute-start.5) | collective-permute-done | bytes 36 | tf_op jit(solution)/shard_map/ppermute | solution.py:41
  66.1 2.9 %collective-permute-start.6 = (bf16[64,512]{1,0:T(8,128)(2,1)S(1)}, bf16[64,512]{1,0:T(8,128)(2,1)S(1)}, u32[]{:S(2)}, u32[]{:S(2)}) collective-permute-start(bf16[64,512]{1,0:T(8,128)(2,1)S(1)} %bitcast.187), channel_id=1, source_target_pairs={{0,508},{4,0},{8,4},{12,8},{16,12},{20,16},{24,20},{28,24},{32,28}... | collective-permute-start | bytes 196616 | tf_op jit(solution)/shard_map/ppermute | solution.py:60
  69.0 7.7 %collective-permute-start.8 = (bf16[64,512]{1,0:T(8,128)(2,1)S(1)}, bf16[64,512]{1,0:T(8,128)(2,1)S(1)}, u32[]{:S(2)}, u32[]{:S(2)}) collective-permute-start(bf16[64,512]{1,0:T(8,128)(2,1)S(1)} %bitcast.183), channel_id=1, source_target_pairs={{0,256},{4,260},{8,264},{12,268},{16,272},{20,276},{24,280},{28,28... | collective-permute-start | bytes 196616 | tf_op jit(solution)/shard_map/ppermute | solution.py:60
  79.3 6.3 %collective-permute-done.4 = bf16[64,512]{1,0:T(8,128)(2,1)S(1)} collective-permute-done((bf16[64,512]{1,0:T(8,128)(2,1)S(1)}, bf16[64,512]{1,0:T(8,128)(2,1)S(1)}, u32[]{:S(2)}, u32[]{:S(2)}) %collective-permute-start.4) | collective-permute-done | bytes 65568 | tf_op jit(solution)/shard_map/ppermute | solution.py:60
  89.5 3.0 %tanh_convert_fusion.3 = (bf16[8,64,512]{2,0,1:T(8,128)(2,1)S(1)}, f32[8,64,512]{2,0,1:T(8,128)}) fusion(f32[8,64,4,128]{3,1,2,0:T(8,128)S(1)} %convert_bitcast_fusion, pred[3,8,1]{1,0,2:T(4,128)(4,1)S(1)} %fusion.50, f32[3,64,512]{2,1,0:T(8,128)S(1)} %bitcast.152, f32[8,64,4,128]{3,1,0,2:T(8,128)S(1)} %select_bitcast_fusion), kind=kOutput, calls=%fused_computation.43 | convolution fusion | flops 10747904 | bytes 4063256 | tf_op jit(solution)/shard_map/kd,knv->dnv/dot_general | solution.py:78
  94.9 2.5 %collective-permute-start.11 = (bf16[64,512]{1,0:T(8,128)(2,1)S(1)}, bf16[64,512]{1,0:T(8,128)(2,1)S(1)}, u32[]{:S(2)}, u32[]{:S(2)}) collective-permute-start(bf16[64,512]{1,0:T(8,128)(2,1)S(1)} %bitcast.180), channel_id=1, source_target_pairs={{0,256},{4,260},{8,264},{12,268},{16,272},{20,276},{24,280},{28,28... | collective-permute-start | bytes 196616 | tf_op jit(solution)/shard_map/ppermute | solution.py:60
  97.4 2.1 %collective-permute-start.9 = (bf16[64,512]{1,0:T(8,128)(2,1)S(1)}, bf16[64,512]{1,0:T(8,128)(2,1)S(1)}, u32[]{:S(2)}, u32[]{:S(2)}) collective-permute-start(bf16[64,512]{1,0:T(8,128)(2,1)S(1)} %bitcast.176), channel_id=1, source_target_pairs={{0,4},{4,8},{8,12},{12,16},{16,20},{20,24},{24,28},{28,32},{32,36}... | collective-permute-start | bytes 196616 | tf_op jit(solution)/shard_map/ppermute | solution.py:60
  100.2 5.2 %collective-permute-done.11 = bf16[64,512]{1,0:T(8,128)(2,1)S(1)} collective-permute-done((bf16[64,512]{1,0:T(8,128)(2,1)S(1)}, bf16[64,512]{1,0:T(8,128)(2,1)S(1)}, u32[]{:S(2)}, u32[]{:S(2)}) %collective-permute-start.11) | collective-permute-done | bytes 65568 | tf_op jit(solution)/shard_map/ppermute | solution.py:60
  107.5 2.2 %convert_reduce_fusion.3 = f32[192,512]{1,0:T(8,128)S(1)} fusion(bf16[4,384,512]{2,1,0:T(8,128)(2,1)} %bitcast.145, bf16[4,192,384]{2,1,0:T(8,128)(2,1)S(1)} %mul.103, bf16[192,384]{1,0:T(8,128)(2,1)} %bitcast.172), kind=kOutput, calls=%fused_computation.8 | convolution fusion | flops 303366144 | bytes 2703360 | tf_op jit(solution)/shard_map/dot_general | solution.py:73
  109.7 2.5 %tanh_convert_fusion.2 = (bf16[8,64,512]{2,0,1:T(8,128)(2,1)S(1)}, f32[8,64,512]{2,0,1:T(8,128)}) fusion(f32[8,64,512]{2,0,1:T(8,128)S(1)} %copy-done, f32[8,64,4,128]{3,1,2,0:T(8,128)S(1)} %convert_bitcast_fusion, pred[3,8,1]{1,0,2:T(4,128)(4,1)S(1)} %fusion.50, f32[3,64,512]{2,1,0:T(8,128)S(1)} %bitcast.150), kind=kOutput, calls=%fused_computation.42 | convolution fusion | flops 10747904 | bytes 4063256 | tf_op jit(solution)/shard_map/kd,knv->dnv/dot_general | solution.py:78
  114.6 7.3 %collective-permute-start.14 = (bf16[64,512]{1,0:T(8,128)(2,1)S(1)}, bf16[64,512]{1,0:T(8,128)(2,1)S(1)}, u32[]{:S(2)}, u32[]{:S(2)}) collective-permute-start(bf16[64,512]{1,0:T(8,128)(2,1)S(1)} %bitcast.181), channel_id=1, source_target_pairs={{0,256},{4,260},{8,264},{12,268},{16,272},{20,276},{24,280},{28,28... | collective-permute-start | bytes 196616 | tf_op jit(solution)/shard_map/ppermute | solution.py:60
  121.9 2.3 %collective-permute-start.12 = (bf16[64,512]{1,0:T(8,128)(2,1)S(1)}, bf16[64,512]{1,0:T(8,128)(2,1)S(1)}, u32[]{:S(2)}, u32[]{:S(2)}) collective-permute-start(bf16[64,512]{1,0:T(8,128)(2,1)S(1)} %bitcast.177), channel_id=1, source_target_pairs={{0,4},{4,8},{8,12},{12,16},{16,20},{20,24},{24,28},{28,32},{32,36}... | collective-permute-start | bytes 196616 | tf_op jit(solution)/shard_map/ppermute | solution.py:60
  124.9 5.9 %collective-permute-done.12 = bf16[64,512]{1,0:T(8,128)(2,1)S(1)} collective-permute-done((bf16[64,512]{1,0:T(8,128)(2,1)S(1)}, bf16[64,512]{1,0:T(8,128)(2,1)S(1)}, u32[]{:S(2)}, u32[]{:S(2)}) %collective-permute-start.12) | collective-permute-done | bytes 65568 | tf_op jit(solution)/shard_map/ppermute | solution.py:60
  133.1 2.3 %convert_reduce_fusion.2 = f32[192,512]{1,0:T(8,128)S(1)} fusion(bf16[4,384,512]{2,1,0:T(8,128)(2,1)} %bitcast.146, bf16[4,192,384]{2,1,0:T(8,128)(2,1)} %mul.107, bf16[192,384]{1,0:T(8,128)(2,1)} %bitcast.173), kind=kOutput, calls=%fused_computation.7 | convolution fusion | flops 303366144 | bytes 2703360 | tf_op jit(solution)/shard_map/dot_general | solution.py:73
  135.5 2.5 %tanh_convert_fusion.1 = (bf16[8,64,512]{2,0,1:T(8,128)(2,1)S(1)}, f32[8,64,512]{2,0,1:T(8,128)}) fusion(f32[8,64,512]{2,0,1:T(8,128)S(1)} %copy-done.1, f32[8,64,4,128]{3,1,2,0:T(8,128)S(1)} %convert_bitcast_fusion, pred[3,8,1]{1,0,2:T(4,128)(4,1)S(1)} %fusion.50, f32[3,64,512]{2,1,0:T(8,128)S(1)} %bitcast.151), kind=kOutput, calls=%fused_computation.41 | convolution fusion | flops 10747904 | bytes 4063256 | tf_op jit(solution)/shard_map/kd,knv->dnv/dot_general | solution.py:78
  140.4 2.5 %collective-permute-start.17 = (bf16[64,512]{1,0:T(8,128)(2,1)S(1)}, bf16[64,512]{1,0:T(8,128)(2,1)S(1)}, u32[]{:S(2)}, u32[]{:S(2)}) collective-permute-start(bf16[64,512]{1,0:T(8,128)(2,1)S(1)} %bitcast.182), channel_id=1, source_target_pairs={{0,256},{4,260},{8,264},{12,268},{16,272},{20,276},{24,280},{28,28... | collective-permute-start | bytes 196616 | tf_op jit(solution)/shard_map/ppermute | solution.py:60
  142.9 2.1 %collective-permute-start.15 = (bf16[64,512]{1,0:T(8,128)(2,1)S(1)}, bf16[64,512]{1,0:T(8,128)(2,1)S(1)}, u32[]{:S(2)}, u32[]{:S(2)}) collective-permute-start(bf16[64,512]{1,0:T(8,128)(2,1)S(1)} %bitcast.178), channel_id=1, source_target_pairs={{0,4},{4,8},{8,12},{12,16},{16,20},{20,24},{24,28},{28,32},{32,36}... | collective-permute-start | bytes 196616 | tf_op jit(solution)/shard_map/ppermute | solution.py:60
  145.7 5.0 %collective-permute-done.17 = bf16[64,512]{1,0:T(8,128)(2,1)S(1)} collective-permute-done((bf16[64,512]{1,0:T(8,128)(2,1)S(1)}, bf16[64,512]{1,0:T(8,128)(2,1)S(1)}, u32[]{:S(2)}, u32[]{:S(2)}) %collective-permute-start.17) | collective-permute-done | bytes 65568 | tf_op jit(solution)/shard_map/ppermute | solution.py:60
  154.1 2.3 %convert_reduce_fusion.1 = f32[192,512]{1,0:T(8,128)S(1)} fusion(bf16[4,384,512]{2,1,0:T(8,128)(2,1)} %bitcast.147, bf16[4,192,384]{2,1,0:T(8,128)(2,1)} %mul.111, bf16[192,384]{1,0:T(8,128)(2,1)} %bitcast.174), kind=kOutput, calls=%fused_computation.6 | convolution fusion | flops 303366144 | bytes 2703360 | tf_op jit(solution)/shard_map/dot_general | solution.py:73
  (148 shorter events, 39.4 us)
Async XLA Ops:
  7.2 56.9 %copy-start.18 = (f32[8,1,64,128]{3,2,1,0:T(8,128)S(1)}, f32[8,1,64,128]{3,2,1,0:T(8,128)}, u32[]{:S(2)}) copy-start(f32[8,1,64,128]{3,2,1,0:T(8,128)} %param.7) | copy-start | bytes 786436
  7.2 80.1 %all-gather.2.cloned.1.call-start = ((), (), s32[]{:S(2)}) async-start(), calls=%async_computation | async-start | bytes 1966080 | tf_op jit(solution)/shard_map/all_gather | solution.py:43
  7.2 56.8 %collective-permute-start.2 = (f32[8,64,128]{2,1,0:T(8,128)}, f32[8,64,128]{2,1,0:T(8,128)S(1)}, u32[]{:S(2)}, u32[]{:S(2)}) collective-permute-start(f32[8,64,128]{2,1,0:T(8,128)} %bitcast.166), channel_id=1, source_target_pairs={{0,3},{1,0},{2,1},{3,2},{4,7},{5,4},{6,5},{7,6},{8,11},{9,8},{10,9... | collective-permute-start | bytes 786440 | tf_op jit(solution)/shard_map/ppermute | solution.py:48
  10.1 54.0 %collective-permute-start.1 = (f32[8,64,128]{2,1,0:T(8,128)}, f32[8,64,128]{2,1,0:T(8,128)S(1)}, u32[]{:S(2)}, u32[]{:S(2)}) collective-permute-start(f32[8,64,128]{2,1,0:T(8,128)} %bitcast.167), channel_id=1, source_target_pairs={{0,2},{1,3},{2,0},{3,1},{4,6},{5,7},{6,4},{7,5},{8,10},{9,11},{10,... | collective-permute-start | bytes 786440 | tf_op jit(solution)/shard_map/ppermute | solution.py:48
  18.5 45.6 %collective-permute-start = (f32[8,64,128]{2,1,0:T(8,128)}, f32[8,64,128]{2,1,0:T(8,128)S(1)}, u32[]{:S(2)}, u32[]{:S(2)}) collective-permute-start(f32[8,64,128]{2,1,0:T(8,128)} %bitcast.168), channel_id=1, source_target_pairs={{0,1},{1,2},{2,3},{3,0},{4,5},{5,6},{6,7},{7,4},{8,9},{9,10},{10,1... | collective-permute-start | bytes 786440 | tf_op jit(solution)/shard_map/ppermute | solution.py:48
  21.7 30.7 %collective-permute-start.3 = (s32[]{:T(128)}, s32[]{:T(128)}, u32[]{:S(2)}, u32[]{:S(2)}) collective-permute-start(s32[]{:T(128)} %bitcast.11), channel_id=1, source_target_pairs={{0,508},{4,0},{8,4},{12,8},{16,12},{20,16},{24,20},{28,24},{32,28}... | collective-permute-start | bytes 20 | tf_op jit(solution)/shard_map/ppermute | solution.py:41
  30.9 24.7 %collective-permute-start.7 = (s32[]{:T(128)}, s32[]{:T(128)}, u32[]{:S(2)}, u32[]{:S(2)}) collective-permute-start(s32[]{:T(128)} %bitcast.13), channel_id=1, source_target_pairs={{0,256},{4,260},{8,264},{12,268},{16,272},{20,276},{24,280},{28,28... | collective-permute-start | bytes 20 | tf_op jit(solution)/shard_map/ppermute | solution.py:41
  52.5 8.4 %collective-permute-start.5 = (s32[]{:T(128)}, s32[]{:T(128)}, u32[]{:S(2)}, u32[]{:S(2)}) collective-permute-start(s32[]{:T(128)} %bitcast.12), channel_id=1, source_target_pairs={{0,4},{4,8},{8,12},{12,16},{16,20},{20,24},{24,28},{28,32},{32,36}... | collective-permute-start | bytes 20 | tf_op jit(solution)/shard_map/ppermute | solution.py:41
  66.1 12.5 %collective-permute-start.6 = (bf16[64,512]{1,0:T(8,128)(2,1)S(1)}, bf16[64,512]{1,0:T(8,128)(2,1)S(1)}, u32[]{:S(2)}, u32[]{:S(2)}) collective-permute-start(bf16[64,512]{1,0:T(8,128)(2,1)S(1)} %bitcast.187), channel_id=1, source_target_pairs={{0,508},{4,0},{8,4},{12,8},{16,12},{20,16},{24,20},{28,24},{32,28}... | collective-permute-start | bytes 196616 | tf_op jit(solution)/shard_map/ppermute | solution.py:60
  69.0 10.2 %collective-permute-start.8 = (bf16[64,512]{1,0:T(8,128)(2,1)S(1)}, bf16[64,512]{1,0:T(8,128)(2,1)S(1)}, u32[]{:S(2)}, u32[]{:S(2)}) collective-permute-start(bf16[64,512]{1,0:T(8,128)(2,1)S(1)} %bitcast.183), channel_id=1, source_target_pairs={{0,256},{4,260},{8,264},{12,268},{16,272},{20,276},{24,280},{28,28... | collective-permute-start | bytes 196616 | tf_op jit(solution)/shard_map/ppermute | solution.py:60
  76.7 8.9 %collective-permute-start.4 = (bf16[64,512]{1,0:T(8,128)(2,1)S(1)}, bf16[64,512]{1,0:T(8,128)(2,1)S(1)}, u32[]{:S(2)}, u32[]{:S(2)}) collective-permute-start(bf16[64,512]{1,0:T(8,128)(2,1)S(1)} %bitcast.179), channel_id=1, source_target_pairs={{0,4},{4,8},{8,12},{12,16},{16,20},{20,24},{24,28},{28,32},{32,36}... | collective-permute-start | bytes 196616 | tf_op jit(solution)/shard_map/ppermute | solution.py:60
  89.4 10.1 %copy-start.5 = (bf16[64,512]{1,0:T(8,128)(2,1)S(1)}, bf16[64,512]{1,0:T(8,128)(2,1)}, u32[]{:S(2)}) copy-start(bf16[64,512]{1,0:T(8,128)(2,1)} %copy-done.4) | copy-start | bytes 196612
  89.4 10.1 %copy-start.7 = (bf16[64,512]{1,0:T(8,128)(2,1)S(1)}, bf16[64,512]{1,0:T(8,128)(2,1)}, u32[]{:S(2)}) copy-start(bf16[64,512]{1,0:T(8,128)(2,1)} %copy-done.6) | copy-start | bytes 196612
  93.0 7.2 %collective-permute-start.10 = (bf16[64,512]{1,0:T(8,128)(2,1)S(1)}, bf16[64,512]{1,0:T(8,128)(2,1)S(1)}, u32[]{:S(2)}, u32[]{:S(2)}) collective-permute-start(bf16[64,512]{1,0:T(8,128)(2,1)S(1)} %bitcast.184), channel_id=1, source_target_pairs={{0,508},{4,0},{8,4},{12,8},{16,12},{20,16},{24,20},{28,24},{32,28}... | collective-permute-start | bytes 196616 | tf_op jit(solution)/shard_map/ppermute | solution.py:60
  94.9 10.5 %collective-permute-start.11 = (bf16[64,512]{1,0:T(8,128)(2,1)S(1)}, bf16[64,512]{1,0:T(8,128)(2,1)S(1)}, u32[]{:S(2)}, u32[]{:S(2)}) collective-permute-start(bf16[64,512]{1,0:T(8,128)(2,1)S(1)} %bitcast.180), channel_id=1, source_target_pairs={{0,256},{4,260},{8,264},{12,268},{16,272},{20,276},{24,280},{28,28... | collective-permute-start | bytes 196616 | tf_op jit(solution)/shard_map/ppermute | solution.py:60
  97.4 8.9 %collective-permute-start.9 = (bf16[64,512]{1,0:T(8,128)(2,1)S(1)}, bf16[64,512]{1,0:T(8,128)(2,1)S(1)}, u32[]{:S(2)}, u32[]{:S(2)}) collective-permute-start(bf16[64,512]{1,0:T(8,128)(2,1)S(1)} %bitcast.176), channel_id=1, source_target_pairs={{0,4},{4,8},{8,12},{12,16},{16,20},{20,24},{24,28},{28,32},{32,36}... | collective-permute-start | bytes 196616 | tf_op jit(solution)/shard_map/ppermute | solution.py:60
  109.7 14.5 %copy-start.11 = (bf16[64,512]{1,0:T(8,128)(2,1)S(1)}, bf16[64,512]{1,0:T(8,128)(2,1)}, u32[]{:S(2)}) copy-start(bf16[64,512]{1,0:T(8,128)(2,1)} %copy-done.10) | copy-start | bytes 196612
  112.7 12.2 %collective-permute-start.13 = (bf16[64,512]{1,0:T(8,128)(2,1)S(1)}, bf16[64,512]{1,0:T(8,128)(2,1)S(1)}, u32[]{:S(2)}, u32[]{:S(2)}) collective-permute-start(bf16[64,512]{1,0:T(8,128)(2,1)S(1)} %bitcast.185), channel_id=1, source_target_pairs={{0,508},{4,0},{8,4},{12,8},{16,12},{20,16},{24,20},{28,24},{32,28}... | collective-permute-start | bytes 196616 | tf_op jit(solution)/shard_map/ppermute | solution.py:60
  114.6 10.3 %collective-permute-start.14 = (bf16[64,512]{1,0:T(8,128)(2,1)S(1)}, bf16[64,512]{1,0:T(8,128)(2,1)S(1)}, u32[]{:S(2)}, u32[]{:S(2)}) collective-permute-start(bf16[64,512]{1,0:T(8,128)(2,1)S(1)} %bitcast.181), channel_id=1, source_target_pairs={{0,256},{4,260},{8,264},{12,268},{16,272},{20,276},{24,280},{28,28... | collective-permute-start | bytes 196616 | tf_op jit(solution)/shard_map/ppermute | solution.py:60
  121.9 8.9 %collective-permute-start.12 = (bf16[64,512]{1,0:T(8,128)(2,1)S(1)}, bf16[64,512]{1,0:T(8,128)(2,1)S(1)}, u32[]{:S(2)}, u32[]{:S(2)}) collective-permute-start(bf16[64,512]{1,0:T(8,128)(2,1)S(1)} %bitcast.177), channel_id=1, source_target_pairs={{0,4},{4,8},{8,12},{12,16},{16,20},{20,24},{24,28},{28,32},{32,36}... | collective-permute-start | bytes 196616 | tf_op jit(solution)/shard_map/ppermute | solution.py:60
  135.5 9.5 %copy-start.9 = (bf16[64,512]{1,0:T(8,128)(2,1)S(1)}, bf16[64,512]{1,0:T(8,128)(2,1)}, u32[]{:S(2)}) copy-start(bf16[64,512]{1,0:T(8,128)(2,1)} %copy-done.8) | copy-start | bytes 196612
  138.5 7.2 %collective-permute-start.16 = (bf16[64,512]{1,0:T(8,128)(2,1)S(1)}, bf16[64,512]{1,0:T(8,128)(2,1)S(1)}, u32[]{:S(2)}, u32[]{:S(2)}) collective-permute-start(bf16[64,512]{1,0:T(8,128)(2,1)S(1)} %bitcast.186), channel_id=1, source_target_pairs={{0,508},{4,0},{8,4},{12,8},{16,12},{20,16},{24,20},{28,24},{32,28}... | collective-permute-start | bytes 196616 | tf_op jit(solution)/shard_map/ppermute | solution.py:60
  140.4 10.3 %collective-permute-start.17 = (bf16[64,512]{1,0:T(8,128)(2,1)S(1)}, bf16[64,512]{1,0:T(8,128)(2,1)S(1)}, u32[]{:S(2)}, u32[]{:S(2)}) collective-permute-start(bf16[64,512]{1,0:T(8,128)(2,1)S(1)} %bitcast.182), channel_id=1, source_target_pairs={{0,256},{4,260},{8,264},{12,268},{16,272},{20,276},{24,280},{28,28... | collective-permute-start | bytes 196616 | tf_op jit(solution)/shard_map/ppermute | solution.py:60
  142.9 8.9 %collective-permute-start.15 = (bf16[64,512]{1,0:T(8,128)(2,1)S(1)}, bf16[64,512]{1,0:T(8,128)(2,1)S(1)}, u32[]{:S(2)}, u32[]{:S(2)}) collective-permute-start(bf16[64,512]{1,0:T(8,128)(2,1)S(1)} %bitcast.178), channel_id=1, source_target_pairs={{0,4},{4,8},{8,12},{12,16},{16,20},{20,24},{24,28},{28,32},{32,36}... | collective-permute-start | bytes 196616 | tf_op jit(solution)/shard_map/ppermute | solution.py:60
  (18 other events, 42.3 us)
Sparse Core Ops, SparseCore 0:
  20.5 35.3 all-gather.1

commit v5 on v4

--- a/solution.py
+++ b/solution.py
@@ -41,16 +41,16 @@
         provide.append(lax.ppermute(wanted[k], "area", perm))
 
     w_full = lax.all_gather(weights[:, 0], "blk", axis=1, tiled=False)
-    ext_full = lax.all_gather(ext_input[:, 0], "blk", axis=1, tiled=False)
-    drive_in = ext_full.transpose(0, 2, 1, 3).reshape(sub_dev, trials, sub_width).astype(jnp.float32)
-    own_act = activity[:, 0]
-    by_shift = [own_act] + [
-        lax.ppermute(own_act, "blk", [(b, (b + s) % n_blk) for b in range(n_blk)]) for s in range(1, n_blk)
+    own_state = jnp.stack([activity[:, 0], ext_input[:, 0].astype(jnp.float32)])
+    by_shift = [own_state] + [
+        lax.ppermute(own_state, "blk", [(b, (b + s) % n_blk) for b in range(n_blk)]) for s in range(1, n_blk)
     ]
-    by_shift = jnp.stack(by_shift, axis=1)
+    by_shift = jnp.stack(by_shift, axis=2)
     part_to_shift = (my_blk - jnp.arange(n_blk)) % n_blk
-    act_full = jnp.take(by_shift, part_to_shift, axis=1)
-    current = act_full.transpose(0, 2, 1, 3).reshape(sub_dev, trials, sub_width)
+    state_full = jnp.take(by_shift, part_to_shift, axis=2)
+    state_full = state_full.transpose(0, 1, 3, 2, 4).reshape(2, sub_dev, trials, sub_width)
+    current = state_full[0]
+    drive_in = state_full[1]
 
     def exchange(rate_full):
         got = []

time: 170 us -> 162 us (0.953)
  blocking collectives: 15.6 us -> 0 us
  starting transfers between devices: 63.2 us -> 65.7 us
  other arithmetic: 7.61 us -> 9.85 us
  local copies, waits for them, and re-layouts: 14.5 us -> 16.6 us
    all_gather x1 -> x0, blocking collectives: 15.6 us -> none  [body(): ext_full = lax.all_gather(ext_input[:, 0], 'blk', axis=1, tiled=False)]
    ppermute x12, starting transfers between devices: 37 us -> 39.9 us  [exchange(): got.append(lax.ppermute(payload, 'area', perm))]
    another operation x1 -> x2, other arithmetic: 0.1 us -> 2.58 us  [body(): by_shift = jnp.stack(by_shift, axis=2)]
    unnamed x60 -> x64, local copies, waits for them, and re-layouts: 2.97 us -> 3.46 us
  transfers between devices with their start and end apart: 19 -> 19, of which waited for: 8 -> 10; matrix products, arithmetic and copies ran while one was open for 6% -> 8% of each run, Pallas kernels for 0% -> 0%
where the time goes in v5:
time: 162 us; the launch traced here: 160 us
  starting transfers between devices  65.7 us (41%)
  waiting for transfers between devices  28.9 us (18%)
  between operations  21.4 us (13%)
  matrix products  17.8 us (11%)
  local copies, waits for them, and re-layouts  16.6 us (10%)
  other arithmetic  9.85 us (6%)
    ppermute x12, starting transfers between devices, exchange(): got.append(lax.ppermute(payload, 'area', perm))  39.9 us
    ppermute x12, waiting for transfers between devices, exchange(): got.append(lax.ppermute(payload, 'area', perm))  25 us
    ppermute x3, starting transfers between devices, body(): provide.append(lax.ppermute(wanted[k], 'area', perm))  13.4 us
    ppermute x3, starting transfers between devices, body(): lax.ppermute(own_state, 'blk', [(b, (b + s) % n_blk) for b in range(n_blk)])  12.4 us
    dot_general x4, matrix products, body(): jnp.einsum('kd,knv->dnv', first, per_slot, precision=lax.Precision.HIGHEST)  9.47 us
    dot_general x4, matrix products, body(): lax.dot_general(lhs, w_rhs, (((2,), (1,)), ((0,), (0,))), preferred_eleme...  7.26 us
    mul x9, local copies, waits for them, and re-layouts, body(): same_b[None, :, None, :, None] * presyn_parts.transpose(2, 1, 0, 3)[:, None]  4.76 us
    ppermute x3, waiting for transfers between devices, body(): provide.append(lax.ppermute(wanted[k], 'area', perm))  3.93 us
  transfers between devices with their start and end apart: 19, of which 10 were waited for; matrix products, arithmetic and copies ran while one was open for 8% of the time, Pallas kernels for 0%

profile of v5, /device:TPU:6, one launch (start us, length us, event | category | flops | bytes accessed | tf_op | source)
XLA Modules:
  0.0 160.3 jit_solution(2359236830974731230)
XLA Ops:
  9.2 3.3 %collective-permute-start.1 = (f32[2,8,64,128]{3,2,1,0:T(8,128)S(1)}, f32[2,8,64,128]{3,2,1,0:T(8,128)S(1)}, u32[]{:S(2)}, u32[]{:S(2)}) collective-permute-start(f32[2,8,64,128]{3,2,1,0:T(8,128)S(1)} %get-tuple-element.21), channel_id=1, source_target_pairs={{0,2},{1,3},{2,0},{3,1},{4,6},{5,7},{6,4},{7,5},{8,10},{9,11},{10,... | collective-permute-start | bytes 1572872 | tf_op jit(solution)/shard_map/ppermute | solution.py:46
  12.6 6.3 %collective-permute-start = (f32[2,8,64,128]{3,2,1,0:T(8,128)S(1)}, f32[2,8,64,128]{3,2,1,0:T(8,128)S(1)}, u32[]{:S(2)}, u32[]{:S(2)}) collective-permute-start(f32[2,8,64,128]{3,2,1,0:T(8,128)S(1)} %get-tuple-element.21), channel_id=1, source_target_pairs={{0,1},{1,2},{2,3},{3,0},{4,5},{5,6},{6,7},{7,4},{8,9},{9,10},{10,1... | collective-permute-start | bytes 1572872 | tf_op jit(solution)/shard_map/ppermute | solution.py:46
  18.9 2.8 %collective-permute-start.2 = (f32[2,8,64,128]{3,2,1,0:T(8,128)S(1)}, f32[2,8,64,128]{3,2,1,0:T(8,128)S(1)}, u32[]{:S(2)}, u32[]{:S(2)}) collective-permute-start(f32[2,8,64,128]{3,2,1,0:T(8,128)S(1)} %get-tuple-element.21), channel_id=1, source_target_pairs={{0,3},{1,0},{2,1},{3,2},{4,7},{5,4},{6,5},{7,6},{8,11},{9,8},{10,9... | collective-permute-start | bytes 1572872 | tf_op jit(solution)/shard_map/ppermute | solution.py:46
  22.4 9.5 %collective-permute-start.3 = (s32[]{:T(128)}, s32[]{:T(128)}, u32[]{:S(2)}, u32[]{:S(2)}) collective-permute-start(s32[]{:T(128)} %bitcast.11), channel_id=1, source_target_pairs={{0,508},{4,0},{8,4},{12,8},{16,12},{20,16},{24,20},{28,24},{32,28}... | collective-permute-start | bytes 20 | tf_op jit(solution)/shard_map/ppermute | solution.py:41
  38.9 2.4 %collective-permute-done.7 = s32[]{:T(128)} collective-permute-done((s32[]{:T(128)}, s32[]{:T(128)}, u32[]{:S(2)}, u32[]{:S(2)}) %collective-permute-start.7) | collective-permute-done | bytes 36 | tf_op jit(solution)/shard_map/ppermute | solution.py:41
  55.2 6.1 %collective-permute-start.6 = (bf16[64,512]{1,0:T(8,128)(2,1)S(1)}, bf16[64,512]{1,0:T(8,128)(2,1)S(1)}, u32[]{:S(2)}, u32[]{:S(2)}) collective-permute-start(bf16[64,512]{1,0:T(8,128)(2,1)S(1)} %bitcast.184), channel_id=1, source_target_pairs={{0,508},{4,0},{8,4},{12,8},{16,12},{20,16},{24,20},{28,24},{32,28}... | collective-permute-start | bytes 196616 | tf_op jit(solution)/shard_map/ppermute | solution.py:60
  61.3 4.7 %collective-permute-start.8 = (bf16[64,512]{1,0:T(8,128)(2,1)S(1)}, bf16[64,512]{1,0:T(8,128)(2,1)S(1)}, u32[]{:S(2)}, u32[]{:S(2)}) collective-permute-start(bf16[64,512]{1,0:T(8,128)(2,1)S(1)} %bitcast.180), channel_id=1, source_target_pairs={{0,256},{4,260},{8,264},{12,268},{16,272},{20,276},{24,280},{28,28... | collective-permute-start | bytes 196616 | tf_op jit(solution)/shard_map/ppermute | solution.py:60
  68.0 3.3 %collective-permute-done.8 = bf16[64,512]{1,0:T(8,128)(2,1)S(1)} collective-permute-done((bf16[64,512]{1,0:T(8,128)(2,1)S(1)}, bf16[64,512]{1,0:T(8,128)(2,1)S(1)}, u32[]{:S(2)}, u32[]{:S(2)}) %collective-permute-start.8) | collective-permute-done | bytes 65568 | tf_op jit(solution)/shard_map/ppermute | solution.py:60
  71.4 3.6 %collective-permute-done.4 = bf16[64,512]{1,0:T(8,128)(2,1)S(1)} collective-permute-done((bf16[64,512]{1,0:T(8,128)(2,1)S(1)}, bf16[64,512]{1,0:T(8,128)(2,1)S(1)}, u32[]{:S(2)}, u32[]{:S(2)}) %collective-permute-start.4) | collective-permute-done | bytes 65568 | tf_op jit(solution)/shard_map/ppermute | solution.py:60
  79.1 3.0 %tanh_convert_fusion.3 = (bf16[8,64,512]{2,0,1:T(8,128)(2,1)S(1)}, f32[8,64,512]{2,0,1:T(8,128)}) fusion(f32[1,8,64,4,128]{4,2,1,0,3:T(8,128)S(1)} %get-tuple-element.6, pred[3,8,1]{1,0,2:T(4,128)(4,1)S(1)} %fusion.50, f32[3,64,512]{2,1,0:T(8,128)S(1)} %bitcast.149, f32[1,8,64,4,128]{4,2,1,0,3:T(8,128)S(1)} %get-tuple-element.7), kind=kOutput, calls=%fused_computation.42 | convolution fusion | flops 10747904 | bytes 4063256 | tf_op jit(solution)/shard_map/kd,knv->dnv/dot_general | solution.py:78
  84.5 5.0 %collective-permute-start.11 = (bf16[64,512]{1,0:T(8,128)(2,1)S(1)}, bf16[64,512]{1,0:T(8,128)(2,1)S(1)}, u32[]{:S(2)}, u32[]{:S(2)}) collective-permute-start(bf16[64,512]{1,0:T(8,128)(2,1)S(1)} %bitcast.177), channel_id=1, source_target_pairs={{0,256},{4,260},{8,264},{12,268},{16,272},{20,276},{24,280},{28,28... | collective-permute-start | bytes 196616 | tf_op jit(solution)/shard_map/ppermute | solution.py:60
  92.3 4.0 %collective-permute-done.11 = bf16[64,512]{1,0:T(8,128)(2,1)S(1)} collective-permute-done((bf16[64,512]{1,0:T(8,128)(2,1)S(1)}, bf16[64,512]{1,0:T(8,128)(2,1)S(1)}, u32[]{:S(2)}, u32[]{:S(2)}) %collective-permute-start.11) | collective-permute-done | bytes 65568 | tf_op jit(solution)/shard_map/ppermute | solution.py:60
  99.6 2.2 %convert_reduce_fusion.3 = f32[192,512]{1,0:T(8,128)S(1)} fusion(bf16[4,384,512]{2,1,0:T(8,128)(2,1)} %bitcast.144, bf16[4,192,384]{2,1,0:T(8,128)(2,1)S(1)} %mul.103, bf16[192,384]{1,0:T(8,128)(2,1)} %bitcast.169), kind=kOutput, calls=%fused_computation.10 | convolution fusion | flops 303366144 | bytes 2703360 | tf_op jit(solution)/shard_map/dot_general | solution.py:73
  101.8 2.5 %tanh_convert_fusion.2 = (bf16[8,64,512]{2,0,1:T(8,128)(2,1)S(1)}, f32[8,64,512]{2,0,1:T(8,128)}) fusion(f32[8,64,512]{2,0,1:T(8,128)S(1)} %copy-done, f32[1,8,64,4,128]{4,2,1,0,3:T(8,128)S(1)} %get-tuple-element.6, pred[3,8,1]{1,0,2:T(4,128)(4,1)S(1)} %fusion.50, f32[3,64,512]{2,1,0:T(8,128)S(1)} %bitcast.150), kind=kOutput, calls=%fused_computation.41 | convolution fusion | flops 10747904 | bytes 4063256 | tf_op jit(solution)/shard_map/kd,knv->dnv/dot_general | solution.py:78
  106.7 4.7 %collective-permute-start.14 = (bf16[64,512]{1,0:T(8,128)(2,1)S(1)}, bf16[64,512]{1,0:T(8,128)(2,1)S(1)}, u32[]{:S(2)}, u32[]{:S(2)}) collective-permute-start(bf16[64,512]{1,0:T(8,128)(2,1)S(1)} %bitcast.178), channel_id=1, source_target_pairs={{0,256},{4,260},{8,264},{12,268},{16,272},{20,276},{24,280},{28,28... | collective-permute-start | bytes 196616 | tf_op jit(solution)/shard_map/ppermute | solution.py:60
  111.5 2.3 %collective-permute-start.12 = (bf16[64,512]{1,0:T(8,128)(2,1)S(1)}, bf16[64,512]{1,0:T(8,128)(2,1)S(1)}, u32[]{:S(2)}, u32[]{:S(2)}) collective-permute-start(bf16[64,512]{1,0:T(8,128)(2,1)S(1)} %bitcast.174), channel_id=1, source_target_pairs={{0,4},{4,8},{8,12},{12,16},{16,20},{20,24},{24,28},{28,32},{32,36}... | collective-permute-start | bytes 196616 | tf_op jit(solution)/shard_map/ppermute | solution.py:60
  114.4 2.6 %collective-permute-done.14 = bf16[64,512]{1,0:T(8,128)(2,1)S(1)} collective-permute-done((bf16[64,512]{1,0:T(8,128)(2,1)S(1)}, bf16[64,512]{1,0:T(8,128)(2,1)S(1)}, u32[]{:S(2)}, u32[]{:S(2)}) %collective-permute-start.14) | collective-permute-done | bytes 65568 | tf_op jit(solution)/shard_map/ppermute | solution.py:60
  117.0 3.3 %collective-permute-done.12 = bf16[64,512]{1,0:T(8,128)(2,1)S(1)} collective-permute-done((bf16[64,512]{1,0:T(8,128)(2,1)S(1)}, bf16[64,512]{1,0:T(8,128)(2,1)S(1)}, u32[]{:S(2)}, u32[]{:S(2)}) %collective-permute-start.12) | collective-permute-done | bytes 65568 | tf_op jit(solution)/shard_map/ppermute | solution.py:60
  121.8 2.2 %convert_reduce_fusion.2 = f32[192,512]{1,0:T(8,128)S(1)} fusion(bf16[4,384,512]{2,1,0:T(8,128)(2,1)} %bitcast.145, bf16[4,192,384]{2,1,0:T(8,128)(2,1)S(1)} %mul.107, bf16[192,384]{1,0:T(8,128)(2,1)} %bitcast.170), kind=kOutput, calls=%fused_computation.9 | convolution fusion | flops 303366144 | bytes 2703360 | tf_op jit(solution)/shard_map/dot_general | solution.py:73
  124.0 2.5 %tanh_convert_fusion.1 = (bf16[8,64,512]{2,0,1:T(8,128)(2,1)S(1)}, f32[8,64,512]{2,0,1:T(8,128)}) fusion(f32[8,64,512]{2,0,1:T(8,128)S(1)} %copy-done.1, f32[1,8,64,4,128]{4,2,1,0,3:T(8,128)S(1)} %get-tuple-element.6, pred[3,8,1]{1,0,2:T(4,128)(4,1)S(1)} %fusion.50, f32[3,64,512]{2,1,0:T(8,128)S(1)} %bitcast.151), kind=kOutput, calls=%fused_computation.40 | convolution fusion | flops 10747904 | bytes 4063256 | tf_op jit(solution)/shard_map/kd,knv->dnv/dot_general | solution.py:78
  128.9 5.0 %collective-permute-start.17 = (bf16[64,512]{1,0:T(8,128)(2,1)S(1)}, bf16[64,512]{1,0:T(8,128)(2,1)S(1)}, u32[]{:S(2)}, u32[]{:S(2)}) collective-permute-start(bf16[64,512]{1,0:T(8,128)(2,1)S(1)} %bitcast.179), channel_id=1, source_target_pairs={{0,256},{4,260},{8,264},{12,268},{16,272},{20,276},{24,280},{28,28... | collective-permute-start | bytes 196616 | tf_op jit(solution)/shard_map/ppermute | solution.py:60
  136.7 3.2 %collective-permute-done.17 = bf16[64,512]{1,0:T(8,128)(2,1)S(1)} collective-permute-done((bf16[64,512]{1,0:T(8,128)(2,1)S(1)}, bf16[64,512]{1,0:T(8,128)(2,1)S(1)}, u32[]{:S(2)}, u32[]{:S(2)}) %collective-permute-start.17) | collective-permute-done | bytes 65568 | tf_op jit(solution)/shard_map/ppermute | solution.py:60
  139.9 2.9 %collective-permute-done.15 = bf16[64,512]{1,0:T(8,128)(2,1)S(1)} collective-permute-done((bf16[64,512]{1,0:T(8,128)(2,1)S(1)}, bf16[64,512]{1,0:T(8,128)(2,1)S(1)}, u32[]{:S(2)}, u32[]{:S(2)}) %collective-permute-start.15) | collective-permute-done | bytes 65568 | tf_op jit(solution)/shard_map/ppermute | solution.py:60
  145.2 2.3 %convert_reduce_fusion.1 = f32[192,512]{1,0:T(8,128)S(1)} fusion(bf16[4,384,512]{2,1,0:T(8,128)(2,1)} %bitcast.146, bf16[4,192,384]{2,1,0:T(8,128)(2,1)} %mul.111, bf16[192,384]{1,0:T(8,128)(2,1)} %bitcast.171), kind=kOutput, calls=%fused_computation.8 | convolution fusion | flops 303366144 | bytes 2703360 | tf_op jit(solution)/shard_map/dot_general | solution.py:73
  (153 shorter events, 49.1 us)
Async XLA Ops:
  7.2 14.5 %copy-start.22 = (s32[3]{0:T(128)S(1)}, s32[3]{0:T(128)}, u32[]{:S(2)}) copy-start(s32[3]{0:T(128)} %param.10) | copy-start | bytes 40
  7.2 14.5 %copy-start.24 = (s32[3]{0:T(128)S(1)}, s32[3]{0:T(128)}, u32[]{:S(2)}) copy-start(s32[3]{0:T(128)} %param.11) | copy-start | bytes 40
  7.2 28.5 %copy-start.23 = (s32[3]{0:T(128)S(1)}, s32[3]{0:T(128)}, u32[]{:S(2)}) copy-start(s32[3]{0:T(128)} %param.13) | copy-start | bytes 40
  7.2 69.7 %all-gather.2.cloned.1.call-start = ((), (), s32[]{:S(2)}) async-start(), calls=%async_computation | async-start | bytes 1966080 | tf_op jit(solution)/shard_map/all_gather | solution.py:43
  9.2 38.1 %collective-permute-start.1 = (f32[2,8,64,128]{3,2,1,0:T(8,128)S(1)}, f32[2,8,64,128]{3,2,1,0:T(8,128)S(1)}, u32[]{:S(2)}, u32[]{:S(2)}) collective-permute-start(f32[2,8,64,128]{3,2,1,0:T(8,128)S(1)} %get-tuple-element.21), channel_id=1, source_target_pairs={{0,2},{1,3},{2,0},{3,1},{4,6},{5,7},{6,4},{7,5},{8,10},{9,11},{10,... | collective-permute-start | bytes 1572872 | tf_op jit(solution)/shard_map/ppermute | solution.py:46
  12.6 34.8 %collective-permute-start = (f32[2,8,64,128]{3,2,1,0:T(8,128)S(1)}, f32[2,8,64,128]{3,2,1,0:T(8,128)S(1)}, u32[]{:S(2)}, u32[]{:S(2)}) collective-permute-start(f32[2,8,64,128]{3,2,1,0:T(8,128)S(1)} %get-tuple-element.21), channel_id=1, source_target_pairs={{0,1},{1,2},{2,3},{3,0},{4,5},{5,6},{6,7},{7,4},{8,9},{9,10},{10,1... | collective-permute-start | bytes 1572872 | tf_op jit(solution)/shard_map/ppermute | solution.py:46
  18.9 28.5 %collective-permute-start.2 = (f32[2,8,64,128]{3,2,1,0:T(8,128)S(1)}, f32[2,8,64,128]{3,2,1,0:T(8,128)S(1)}, u32[]{:S(2)}, u32[]{:S(2)}) collective-permute-start(f32[2,8,64,128]{3,2,1,0:T(8,128)S(1)} %get-tuple-element.21), channel_id=1, source_target_pairs={{0,3},{1,0},{2,1},{3,2},{4,7},{5,4},{6,5},{7,6},{8,11},{9,8},{10,9... | collective-permute-start | bytes 1572872 | tf_op jit(solution)/shard_map/ppermute | solution.py:46
  22.4 13.3 %collective-permute-start.3 = (s32[]{:T(128)}, s32[]{:T(128)}, u32[]{:S(2)}, u32[]{:S(2)}) collective-permute-start(s32[]{:T(128)} %bitcast.11), channel_id=1, source_target_pairs={{0,508},{4,0},{8,4},{12,8},{16,12},{20,16},{24,20},{28,24},{32,28}... | collective-permute-start | bytes 20 | tf_op jit(solution)/shard_map/ppermute | solution.py:41
  32.0 9.4 %collective-permute-start.7 = (s32[]{:T(128)}, s32[]{:T(128)}, u32[]{:S(2)}, u32[]{:S(2)}) collective-permute-start(s32[]{:T(128)} %bitcast.13), channel_id=1, source_target_pairs={{0,256},{4,260},{8,264},{12,268},{16,272},{20,276},{24,280},{28,28... | collective-permute-start | bytes 20 | tf_op jit(solution)/shard_map/ppermute | solution.py:41
  35.7 8.4 %collective-permute-start.5 = (s32[]{:T(128)}, s32[]{:T(128)}, u32[]{:S(2)}, u32[]{:S(2)}) collective-permute-start(s32[]{:T(128)} %bitcast.12), channel_id=1, source_target_pairs={{0,4},{4,8},{8,12},{12,16},{16,20},{20,24},{24,28},{28,32},{32,36}... | collective-permute-start | bytes 20 | tf_op jit(solution)/shard_map/ppermute | solution.py:41
  55.2 12.8 %collective-permute-start.6 = (bf16[64,512]{1,0:T(8,128)(2,1)S(1)}, bf16[64,512]{1,0:T(8,128)(2,1)S(1)}, u32[]{:S(2)}, u32[]{:S(2)}) collective-permute-start(bf16[64,512]{1,0:T(8,128)(2,1)S(1)} %bitcast.184), channel_id=1, source_target_pairs={{0,508},{4,0},{8,4},{12,8},{16,12},{20,16},{24,20},{28,24},{32,28}... | collective-permute-start | bytes 196616 | tf_op jit(solution)/shard_map/ppermute | solution.py:60
  61.3 10.1 %collective-permute-start.8 = (bf16[64,512]{1,0:T(8,128)(2,1)S(1)}, bf16[64,512]{1,0:T(8,128)(2,1)S(1)}, u32[]{:S(2)}, u32[]{:S(2)}) collective-permute-start(bf16[64,512]{1,0:T(8,128)(2,1)S(1)} %bitcast.180), channel_id=1, source_target_pairs={{0,256},{4,260},{8,264},{12,268},{16,272},{20,276},{24,280},{28,28... | collective-permute-start | bytes 196616 | tf_op jit(solution)/shard_map/ppermute | solution.py:60
  66.1 8.9 %collective-permute-start.4 = (bf16[64,512]{1,0:T(8,128)(2,1)S(1)}, bf16[64,512]{1,0:T(8,128)(2,1)S(1)}, u32[]{:S(2)}, u32[]{:S(2)}) collective-permute-start(bf16[64,512]{1,0:T(8,128)(2,1)S(1)} %bitcast.176), channel_id=1, source_target_pairs={{0,4},{4,8},{8,12},{12,16},{16,20},{20,24},{24,28},{28,32},{32,36}... | collective-permute-start | bytes 196616 | tf_op jit(solution)/shard_map/ppermute | solution.py:60
  79.1 12.6 %copy-start.11 = (bf16[64,512]{1,0:T(8,128)(2,1)S(1)}, bf16[64,512]{1,0:T(8,128)(2,1)}, u32[]{:S(2)}) copy-start(bf16[64,512]{1,0:T(8,128)(2,1)} %copy-done.10) | copy-start | bytes 196612
  82.6 9.7 %collective-permute-start.10 = (bf16[64,512]{1,0:T(8,128)(2,1)S(1)}, bf16[64,512]{1,0:T(8,128)(2,1)S(1)}, u32[]{:S(2)}, u32[]{:S(2)}) collective-permute-start(bf16[64,512]{1,0:T(8,128)(2,1)S(1)} %bitcast.181), channel_id=1, source_target_pairs={{0,508},{4,0},{8,4},{12,8},{16,12},{20,16},{24,20},{28,24},{32,28}... | collective-permute-start | bytes 196616 | tf_op jit(solution)/shard_map/ppermute | solution.py:60
  84.5 11.8 %collective-permute-start.11 = (bf16[64,512]{1,0:T(8,128)(2,1)S(1)}, bf16[64,512]{1,0:T(8,128)(2,1)S(1)}, u32[]{:S(2)}, u32[]{:S(2)}) collective-permute-start(bf16[64,512]{1,0:T(8,128)(2,1)S(1)} %bitcast.177), channel_id=1, source_target_pairs={{0,256},{4,260},{8,264},{12,268},{16,272},{20,276},{24,280},{28,28... | collective-permute-start | bytes 196616 | tf_op jit(solution)/shard_map/ppermute | solution.py:60
  89.5 8.9 %collective-permute-start.9 = (bf16[64,512]{1,0:T(8,128)(2,1)S(1)}, bf16[64,512]{1,0:T(8,128)(2,1)S(1)}, u32[]{:S(2)}, u32[]{:S(2)}) collective-permute-start(bf16[64,512]{1,0:T(8,128)(2,1)S(1)} %bitcast.173), channel_id=1, source_target_pairs={{0,4},{4,8},{8,12},{12,16},{16,20},{20,24},{24,28},{28,32},{32,36}... | collective-permute-start | bytes 196616 | tf_op jit(solution)/shard_map/ppermute | solution.py:60
  104.8 9.6 %collective-permute-start.13 = (bf16[64,512]{1,0:T(8,128)(2,1)S(1)}, bf16[64,512]{1,0:T(8,128)(2,1)S(1)}, u32[]{:S(2)}, u32[]{:S(2)}) collective-permute-start(bf16[64,512]{1,0:T(8,128)(2,1)S(1)} %bitcast.182), channel_id=1, source_target_pairs={{0,508},{4,0},{8,4},{12,8},{16,12},{20,16},{24,20},{28,24},{32,28}... | collective-permute-start | bytes 196616 | tf_op jit(solution)/shard_map/ppermute | solution.py:60
  106.7 10.3 %collective-permute-start.14 = (bf16[64,512]{1,0:T(8,128)(2,1)S(1)}, bf16[64,512]{1,0:T(8,128)(2,1)S(1)}, u32[]{:S(2)}, u32[]{:S(2)}) collective-permute-start(bf16[64,512]{1,0:T(8,128)(2,1)S(1)} %bitcast.178), channel_id=1, source_target_pairs={{0,256},{4,260},{8,264},{12,268},{16,272},{20,276},{24,280},{28,28... | collective-permute-start | bytes 196616 | tf_op jit(solution)/shard_map/ppermute | solution.py:60
  111.5 8.9 %collective-permute-start.12 = (bf16[64,512]{1,0:T(8,128)(2,1)S(1)}, bf16[64,512]{1,0:T(8,128)(2,1)S(1)}, u32[]{:S(2)}, u32[]{:S(2)}) collective-permute-start(bf16[64,512]{1,0:T(8,128)(2,1)S(1)} %bitcast.174), channel_id=1, source_target_pairs={{0,4},{4,8},{8,12},{12,16},{16,20},{20,24},{24,28},{28,32},{32,36}... | collective-permute-start | bytes 196616 | tf_op jit(solution)/shard_map/ppermute | solution.py:60
  124.0 12.1 %copy-start.9 = (bf16[64,512]{1,0:T(8,128)(2,1)S(1)}, bf16[64,512]{1,0:T(8,128)(2,1)}, u32[]{:S(2)}) copy-start(bf16[64,512]{1,0:T(8,128)(2,1)} %copy-done.8) | copy-start | bytes 196612
  127.0 9.7 %collective-permute-start.16 = (bf16[64,512]{1,0:T(8,128)(2,1)S(1)}, bf16[64,512]{1,0:T(8,128)(2,1)S(1)}, u32[]{:S(2)}, u32[]{:S(2)}) collective-permute-start(bf16[64,512]{1,0:T(8,128)(2,1)S(1)} %bitcast.183), channel_id=1, source_target_pairs={{0,508},{4,0},{8,4},{12,8},{16,12},{20,16},{24,20},{28,24},{32,28}... | collective-permute-start | bytes 196616 | tf_op jit(solution)/shard_map/ppermute | solution.py:60
  128.9 11.0 %collective-permute-start.17 = (bf16[64,512]{1,0:T(8,128)(2,1)S(1)}, bf16[64,512]{1,0:T(8,128)(2,1)S(1)}, u32[]{:S(2)}, u32[]{:S(2)}) collective-permute-start(bf16[64,512]{1,0:T(8,128)(2,1)S(1)} %bitcast.179), channel_id=1, source_target_pairs={{0,256},{4,260},{8,264},{12,268},{16,272},{20,276},{24,280},{28,28... | collective-permute-start | bytes 196616 | tf_op jit(solution)/shard_map/ppermute | solution.py:60
  133.9 8.9 %collective-permute-start.15 = (bf16[64,512]{1,0:T(8,128)(2,1)S(1)}, bf16[64,512]{1,0:T(8,128)(2,1)S(1)}, u32[]{:S(2)}, u32[]{:S(2)}) collective-permute-start(bf16[64,512]{1,0:T(8,128)(2,1)S(1)} %bitcast.175), channel_id=1, source_target_pairs={{0,4},{4,8},{8,12},{12,16},{16,20},{20,24},{24,28},{28,32},{32,36}... | collective-permute-start | bytes 196616 | tf_op jit(solution)/shard_map/ppermute | solution.py:60
  (20 other events, 50.3 us)
Sparse Core Ops, SparseCore 0:
  21.8 32.4 all-gather.1

commit v6 on v5

v6 whole, which is shorter than its diff:
```python
import jax
import jax.numpy as jnp
from jax import lax
from jax.sharding import PartitionSpec as P

STEPS = 4


euler_step = 0.5


def centre(x):
    xf = x.astype(jnp.float32)
    return (xf - jnp.mean(xf, axis=-2, keepdims=True)).astype(jnp.bfloat16)


def body(activity, ext_input, weights, slot_dst, slot_src, slot_count, hebb_mask):
    n_areas = lax.axis_size("area")
    n_blk = lax.axis_size("blk")
    my_blk = lax.axis_index("blk")
    sub_dev = activity.shape[0]
    trials = activity.shape[2]
    quarter = activity.shape[3]
    slot_cap = slot_src.shape[0]
    sub_width = weights.shape[3]
    offsets = (-1, 1, n_areas // 2)

    occupied = jnp.arange(slot_cap) < slot_count[0]
    select = ((slot_dst[:, None] == jnp.arange(sub_dev)[None, :]) & occupied[:, None]).astype(jnp.float32)

    wanted = jnp.clip(slot_src % sub_dev, 0, sub_dev - 1).astype(jnp.int32)
    provide = []
    for k in range(slot_cap):
        perm = [(i, (i + offsets[k]) % n_areas) for i in range(n_areas)]
        provide.append(lax.ppermute(wanted[k], "area", perm))
    provide = jnp.stack(provide)
    select_provided = jnp.take(select, provide, axis=1)

    w_full = lax.all_gather(weights[:, 0], "blk", axis=1, tiled=False)
    w_full = w_full.reshape(slot_cap, sub_width, sub_width)
    own_state = jnp.stack([activity[:, 0], ext_input[:, 0].astype(jnp.float32)])
    by_shift = [own_state] + [
        lax.ppermute(own_state, "blk", [(b, (b + s) % n_blk) for b in range(n_blk)]) for s in range(1, n_blk)
    ]
    by_shift = jnp.stack(by_shift, axis=2)
    part_to_shift = (my_blk - jnp.arange(n_blk)) % n_blk
    state_full = jnp.take(by_shift, part_to_shift, axis=2)
    state_full = state_full.transpose(0, 1, 3, 2, 4).reshape(2, sub_dev, trials, sub_width)
    current = state_full[0]
    drive_in = state_full[1]
    drive_provided = jnp.take(drive_in, provide, axis=0)

    def advance(cur, contrib, sel, drive):
        summed = sum(sel[k][:, None, None] * contrib[k][None] for k in range(slot_cap))
        return cur + euler_step * (summed - cur + drive)

    def exchange(payload):
        got = []
        for k in range(slot_cap):
            perm = [(i, (i - offsets[k]) % n_areas) for i in range(n_areas)]
            got.append(lax.ppermute(payload[k], "area", perm))
        return jnp.stack(got)

    payload = jnp.tanh(jnp.take(current, provide, axis=0)).astype(jnp.bfloat16)
    pre_list = []
    post_list = []
    for step_idx in range(STEPS):
        presyn = exchange(payload)
        contrib = jnp.einsum("knu,kuv->knv", presyn, w_full, preferred_element_type=jnp.float32)
        if step_idx + 1 < STEPS:
            provided_now = advance(jnp.take(current, provide, axis=0), contrib, select_provided, drive_provided)
            payload = jnp.tanh(provided_now).astype(jnp.bfloat16)
        current = advance(current, contrib, select, drive_in)
        pre_list.append(lax.dynamic_slice_in_dim(presyn, my_blk * quarter, quarter, 2))
        post_list.append(jnp.tanh(jnp.take(current, slot_dst, axis=0)).astype(jnp.bfloat16))
    final_state = lax.dynamic_slice_in_dim(current, my_blk * quarter, quarter, 2)[:, None]

    pre_centered = centre(jnp.stack(pre_list, axis=1))
    post_centered = centre(jnp.stack(post_list, axis=1))
    change = jnp.einsum("ktnq,ktnu->kqu", pre_centered, post_centered, preferred_element_type=jnp.float32)
    gate_on = (occupied & (hebb_mask == 1)).astype(jnp.float32)
    norm_scale = (STEPS * trials) ** (-0.5)
    plasticity = (change * gate_on[:, None, None] * norm_scale).astype(jnp.bfloat16)[:, None]
    return (final_state, plasticity)


def solution(mesh):
    in_specs = (
        P("area", "blk", None, None),
        P("area", "blk", None, None),
        P("area", "blk", None, None),
        P("area"),
        P("area"),
        P("area"),
        P("area"),
    )
    out_specs = (P("area", "blk", None, None), P("area", "blk", None, None))
    return jax.shard_map(body, mesh=mesh, in_specs=in_specs, out_specs=out_specs, check_vma=False)
```

time: 162 us -> 160 us (0.988)
  the two profiles are of different devices: /device:TPU:6 before, /device:TPU:249 now
where the time goes in v6:
time: 160 us; the launch traced here: 158 us
  starting transfers between devices  70.4 us (44%)
  local copies, waits for them, and re-layouts  26.2 us (16%)
  waiting for transfers between devices  21.2 us (13%)
  other arithmetic  20.1 us (13%)
  between operations  15.5 us (10%)
  matrix products  5.05 us (3%)
    ppermute x12, starting transfers between devices, exchange(): got.append(lax.ppermute(payload[k], 'area', perm))  42.1 us
    ppermute x12, waiting for transfers between devices, exchange(): got.append(lax.ppermute(payload[k], 'area', perm))  20.2 us
    ppermute x3, starting transfers between devices, body(): provide.append(lax.ppermute(wanted[k], 'area', perm))  17.1 us
    ppermute x3, starting transfers between devices, body(): lax.ppermute(own_state, 'blk', [(b, (b + s) % n_blk) for b in range(n_blk)])  11.1 us
    gather x4, local copies, waits for them, and re-layouts, body(): jnp.take(current, slot_dst, axis=0)  5.47 us
    gather x2, local copies, waits for them, and re-layouts, body(): jnp.take(current, provide, axis=0)  5.14 us
    another operation x4, local copies, waits for them, and re-layouts, body(): pre_centered = centre(jnp.stack(pre_list, axis=1))  4.28 us
  transfers between devices with their start and end apart: 19, of which 8 were waited for; matrix products, arithmetic and copies ran while one was open for 14% of the time, Pallas kernels for 0%

profile of v6, /device:TPU:249, one launch (start us, length us, event | category | flops | bytes accessed | tf_op | source)
XLA Modules:
  0.0 158.4 jit_solution(1689792795040362648)
XLA Ops:
  9.2 4.7 %collective-permute-start.1 = (f32[2,8,64,128]{3,2,1,0:T(8,128)S(1)}, f32[2,8,64,128]{3,2,1,0:T(8,128)S(1)}, u32[]{:S(2)}, u32[]{:S(2)}) collective-permute-start(f32[2,8,64,128]{3,2,1,0:T(8,128)S(1)} %get-tuple-element.22), channel_id=1, source_target_pairs={{0,2},{1,3},{2,0},{3,1},{4,6},{5,7},{6,4},{7,5},{8,10},{9,11},{10,... | collective-permute-start | bytes 1572872 | tf_op jit(solution)/shard_map/ppermute | solution.py:43
  13.9 2.2 %collective-permute-start = (f32[2,8,64,128]{3,2,1,0:T(8,128)S(1)}, f32[2,8,64,128]{3,2,1,0:T(8,128)S(1)}, u32[]{:S(2)}, u32[]{:S(2)}) collective-permute-start(f32[2,8,64,128]{3,2,1,0:T(8,128)S(1)} %get-tuple-element.22), channel_id=1, source_target_pairs={{0,1},{1,2},{2,3},{3,0},{4,5},{5,6},{6,7},{7,4},{8,9},{9,10},{10,1... | collective-permute-start | bytes 1572872 | tf_op jit(solution)/shard_map/ppermute | solution.py:43
  16.1 4.3 %collective-permute-start.2 = (f32[2,8,64,128]{3,2,1,0:T(8,128)S(1)}, f32[2,8,64,128]{3,2,1,0:T(8,128)S(1)}, u32[]{:S(2)}, u32[]{:S(2)}) collective-permute-start(f32[2,8,64,128]{3,2,1,0:T(8,128)S(1)} %get-tuple-element.22), channel_id=1, source_target_pairs={{0,3},{1,0},{2,1},{3,2},{4,7},{5,4},{6,5},{7,6},{8,11},{9,8},{10,9... | collective-permute-start | bytes 1572872 | tf_op jit(solution)/shard_map/ppermute | solution.py:43
  21.1 3.4 %collective-permute-start.3 = (s32[]{:T(128)}, s32[]{:T(128)}, u32[]{:S(2)}, u32[]{:S(2)}) collective-permute-start(s32[]{:T(128)} %bitcast.9), channel_id=1, source_target_pairs={{0,508},{4,0},{8,4},{12,8},{16,12},{20,16},{24,20},{28,24},{32,28}... | collective-permute-start | bytes 20 | tf_op jit(solution)/shard_map/ppermute | solution.py:35
  24.6 7.9 %collective-permute-start.5 = (s32[]{:T(128)}, s32[]{:T(128)}, u32[]{:S(2)}, u32[]{:S(2)}) collective-permute-start(s32[]{:T(128)} %bitcast.13), channel_id=1, source_target_pairs={{0,256},{4,260},{8,264},{12,268},{16,272},{20,276},{24,280},{28,28... | collective-permute-start | bytes 20 | tf_op jit(solution)/shard_map/ppermute | solution.py:35
  35.1 5.7 %collective-permute-start.4 = (s32[]{:T(128)}, s32[]{:T(128)}, u32[]{:S(2)}, u32[]{:S(2)}) collective-permute-start(s32[]{:T(128)} %bitcast.11), channel_id=1, source_target_pairs={{0,4},{4,8},{8,12},{12,16},{16,20},{20,24},{24,28},{28,32},{32,36}... | collective-permute-start | bytes 20 | tf_op jit(solution)/shard_map/ppermute | solution.py:35
  48.6 2.0 %gather_fusion = f32[4,2,8,64,128]{4,3,2,1,0:T(8,128)} fusion(f32[2,8,4,64,128]{4,3,1,0,2:T(8,128)S(1)} %pad_maximum_fusion, s32[1024]{0:T(1024)S(1)} %pad_clamp_fusion.3), kind=kCustom, calls=%fused_computation.8 | custom fusion | bytes 4194320 | tf_op jit(solution)/shard_map/jit(_take)/gather | solution.py:47
  55.3 7.6 %collective-permute-start.6 = (bf16[64,512]{1,0:T(8,128)(2,1)}, bf16[64,512]{1,0:T(8,128)(2,1)}, u32[]{:S(2)}, u32[]{:S(2)}) collective-permute-start(bf16[64,512]{1,0:T(8,128)(2,1)} %get-tuple-element.44), channel_id=1, source_target_pairs={{0,4},{4,8},{8,12},{12,16},{16,20},{20,24},{24,28},{28,32},{32,36}... | collective-permute-start | bytes 196616 | tf_op jit(solution)/shard_map/ppermute | solution.py:61
  69.3 3.0 %collective-permute-done.8 = bf16[64,512]{1,0:T(8,128)(2,1)} collective-permute-done((bf16[64,512]{1,0:T(8,128)(2,1)}, bf16[64,512]{1,0:T(8,128)(2,1)}, u32[]{:S(2)}, u32[]{:S(2)}) %collective-permute-start.8) | collective-permute-done | bytes 65568 | tf_op jit(solution)/shard_map/ppermute | solution.py:61
  78.7 2.3 %collective-permute-start.9 = (bf16[64,512]{1,0:T(8,128)(2,1)S(1)}, bf16[64,512]{1,0:T(8,128)(2,1)S(1)}, u32[]{:S(2)}, u32[]{:S(2)}) collective-permute-start(bf16[64,512]{1,0:T(8,128)(2,1)S(1)} %get-tuple-element.41), channel_id=1, source_target_pairs={{0,4},{4,8},{8,12},{12,16},{16,20},{20,24},{24,28},{28,32},{32,36}... | collective-permute-start | bytes 196616 | tf_op jit(solution)/shard_map/ppermute | solution.py:61
  81.0 7.3 %collective-permute-start.11 = (bf16[64,512]{1,0:T(8,128)(2,1)S(1)}, bf16[64,512]{1,0:T(8,128)(2,1)S(1)}, u32[]{:S(2)}, u32[]{:S(2)}) collective-permute-start(bf16[64,512]{1,0:T(8,128)(2,1)S(1)} %get-tuple-element.42), channel_id=1, source_target_pairs={{0,256},{4,260},{8,264},{12,268},{16,272},{20,276},{24,280},{28,28... | collective-permute-start | bytes 196616 | tf_op jit(solution)/shard_map/ppermute | solution.py:61
  88.3 2.4 %collective-permute-start.10 = (bf16[64,512]{1,0:T(8,128)(2,1)S(1)}, bf16[64,512]{1,0:T(8,128)(2,1)S(1)}, u32[]{:S(2)}, u32[]{:S(2)}) collective-permute-start(bf16[64,512]{1,0:T(8,128)(2,1)S(1)} %get-tuple-element.43), channel_id=1, source_target_pairs={{0,508},{4,0},{8,4},{12,8},{16,12},{20,16},{24,20},{28,24},{32,28}... | collective-permute-start | bytes 196616 | tf_op jit(solution)/shard_map/ppermute | solution.py:61
  92.6 4.6 %collective-permute-done.10 = bf16[64,512]{1,0:T(8,128)(2,1)S(1)} collective-permute-done((bf16[64,512]{1,0:T(8,128)(2,1)S(1)}, bf16[64,512]{1,0:T(8,128)(2,1)S(1)}, u32[]{:S(2)}, u32[]{:S(2)}) %collective-permute-start.10) | collective-permute-done | bytes 65568 | tf_op jit(solution)/shard_map/ppermute | solution.py:61
  100.4 2.6 %gather_fusion.4 = f32[3,64,512]{2,1,0:T(8,128)} fusion(f32[8,64,512]{2,1,0:T(8,128)} %get-tuple-element.16, s32[1024]{0:T(1024)S(1)} %pad_clamp_fusion.2), kind=kCustom, calls=%fused_computation.2.clone | custom fusion | bytes 786444 | tf_op jit(solution)/shard_map/jit(_take)/gather | solution.py:71
  104.8 2.5 %gather_fusion.5 = f32[3,64,512]{2,1,0:T(8,128)} fusion(f32[8,64,512]{2,1,0:T(8,128)} %get-tuple-element.15, s32[1024]{0:T(1024)S(1)} %pad_clamp_fusion.2), kind=kCustom, calls=%fused_computation.3.clone | custom fusion | bytes 786444 | tf_op jit(solution)/shard_map/jit(_take)/gather | solution.py:71
  107.4 2.5 %gather_fusion.7 = f32[3,64,512]{2,1,0:T(8,128)} fusion(f32[8,64,512]{2,1,0:T(8,128)} %get-tuple-element.15, s32[1024]{0:T(1024)S(1)} %pad_clamp_fusion), kind=kCustom, calls=%fused_computation.5.clone | custom fusion | bytes 786444 | tf_op jit(solution)/shard_map/jit(_take)/gather | solution.py:75
  111.3 2.1 %collective-permute-start.12 = (bf16[64,512]{1,0:T(8,128)(2,1)S(1)}, bf16[64,512]{1,0:T(8,128)(2,1)S(1)}, u32[]{:S(2)}, u32[]{:S(2)}) collective-permute-start(bf16[64,512]{1,0:T(8,128)(2,1)S(1)} %get-tuple-element.38), channel_id=1, source_target_pairs={{0,4},{4,8},{8,12},{12,16},{16,20},{20,24},{24,28},{28,32},{32,36}... | collective-permute-start | bytes 196616 | tf_op jit(solution)/shard_map/ppermute | solution.py:61
  113.4 2.1 %collective-permute-start.14 = (bf16[64,512]{1,0:T(8,128)(2,1)S(1)}, bf16[64,512]{1,0:T(8,128)(2,1)S(1)}, u32[]{:S(2)}, u32[]{:S(2)}) collective-permute-start(bf16[64,512]{1,0:T(8,128)(2,1)S(1)} %get-tuple-element.39), channel_id=1, source_target_pairs={{0,256},{4,260},{8,264},{12,268},{16,272},{20,276},{24,280},{28,28... | collective-permute-start | bytes 196616 | tf_op jit(solution)/shard_map/ppermute | solution.py:61
  115.5 2.7 %collective-permute-start.13 = (bf16[64,512]{1,0:T(8,128)(2,1)S(1)}, bf16[64,512]{1,0:T(8,128)(2,1)S(1)}, u32[]{:S(2)}, u32[]{:S(2)}) collective-permute-start(bf16[64,512]{1,0:T(8,128)(2,1)S(1)} %get-tuple-element.40), channel_id=1, source_target_pairs={{0,508},{4,0},{8,4},{12,8},{16,12},{20,16},{24,20},{28,24},{32,28}... | collective-permute-start | bytes 196616 | tf_op jit(solution)/shard_map/ppermute | solution.py:61
  119.6 4.1 %collective-permute-done.14 = bf16[64,512]{1,0:T(8,128)(2,1)S(1)} collective-permute-done((bf16[64,512]{1,0:T(8,128)(2,1)S(1)}, bf16[64,512]{1,0:T(8,128)(2,1)S(1)}, u32[]{:S(2)}, u32[]{:S(2)}) %collective-permute-start.14) | collective-permute-done | bytes 65568 | tf_op jit(solution)/shard_map/ppermute | solution.py:61
  125.2 2.1 %collective-permute-start.15 = (bf16[64,512]{1,0:T(8,128)(2,1)S(1)}, bf16[64,512]{1,0:T(8,128)(2,1)S(1)}, u32[]{:S(2)}, u32[]{:S(2)}) collective-permute-start(bf16[64,512]{1,0:T(8,128)(2,1)S(1)} %get-tuple-element.35), channel_id=1, source_target_pairs={{0,4},{4,8},{8,12},{12,16},{16,20},{20,24},{24,28},{28,32},{32,36}... | collective-permute-start | bytes 196616 | tf_op jit(solution)/shard_map/ppermute | solution.py:61
  127.2 7.1 %collective-permute-start.17 = (bf16[64,512]{1,0:T(8,128)(2,1)S(1)}, bf16[64,512]{1,0:T(8,128)(2,1)S(1)}, u32[]{:S(2)}, u32[]{:S(2)}) collective-permute-start(bf16[64,512]{1,0:T(8,128)(2,1)S(1)} %get-tuple-element.36), channel_id=1, source_target_pairs={{0,256},{4,260},{8,264},{12,268},{16,272},{20,276},{24,280},{28,28... | collective-permute-start | bytes 196616 | tf_op jit(solution)/shard_map/ppermute | solution.py:61
  134.3 2.7 %collective-permute-start.16 = (bf16[64,512]{1,0:T(8,128)(2,1)S(1)}, bf16[64,512]{1,0:T(8,128)(2,1)S(1)}, u32[]{:S(2)}, u32[]{:S(2)}) collective-permute-start(bf16[64,512]{1,0:T(8,128)(2,1)S(1)} %get-tuple-element.37), channel_id=1, source_target_pairs={{0,508},{4,0},{8,4},{12,8},{16,12},{20,16},{24,20},{28,24},{32,28}... | collective-permute-start | bytes 196616 | tf_op jit(solution)/shard_map/ppermute | solution.py:61
  137.7 5.6 %collective-permute-done.16 = bf16[64,512]{1,0:T(8,128)(2,1)S(1)} collective-permute-done((bf16[64,512]{1,0:T(8,128)(2,1)S(1)}, bf16[64,512]{1,0:T(8,128)(2,1)S(1)}, u32[]{:S(2)}, u32[]{:S(2)}) %collective-permute-start.16) | collective-permute-done | bytes 65568 | tf_op jit(solution)/shard_map/ppermute | solution.py:61
  (142 shorter events, 49.5 us)
Async XLA Ops:
  7.2 27.3 %copy-start.28 = (s32[3]{0:T(128)S(1)}, s32[3]{0:T(128)}, u32[]{:S(2)}) copy-start(s32[3]{0:T(128)} %param.15) | copy-start | bytes 40
  7.2 68.5 %all-gather.2.cloned.1.call-start = ((), (), s32[]{:S(2)}) async-start(), calls=%async_computation | async-start | bytes 1966080 | tf_op jit(solution)/shard_map/all_gather | solution.py:39
  9.2 37.0 %collective-permute-start.1 = (f32[2,8,64,128]{3,2,1,0:T(8,128)S(1)}, f32[2,8,64,128]{3,2,1,0:T(8,128)S(1)}, u32[]{:S(2)}, u32[]{:S(2)}) collective-permute-start(f32[2,8,64,128]{3,2,1,0:T(8,128)S(1)} %get-tuple-element.22), channel_id=1, source_target_pairs={{0,2},{1,3},{2,0},{3,1},{4,6},{5,7},{6,4},{7,5},{8,10},{9,11},{10,... | collective-permute-start | bytes 1572872 | tf_op jit(solution)/shard_map/ppermute | solution.py:43
  13.9 32.3 %collective-permute-start = (f32[2,8,64,128]{3,2,1,0:T(8,128)S(1)}, f32[2,8,64,128]{3,2,1,0:T(8,128)S(1)}, u32[]{:S(2)}, u32[]{:S(2)}) collective-permute-start(f32[2,8,64,128]{3,2,1,0:T(8,128)S(1)} %get-tuple-element.22), channel_id=1, source_target_pairs={{0,1},{1,2},{2,3},{3,0},{4,5},{5,6},{6,7},{7,4},{8,9},{9,10},{10,1... | collective-permute-start | bytes 1572872 | tf_op jit(solution)/shard_map/ppermute | solution.py:43
  16.1 30.1 %collective-permute-start.2 = (f32[2,8,64,128]{3,2,1,0:T(8,128)S(1)}, f32[2,8,64,128]{3,2,1,0:T(8,128)S(1)}, u32[]{:S(2)}, u32[]{:S(2)}) collective-permute-start(f32[2,8,64,128]{3,2,1,0:T(8,128)S(1)} %get-tuple-element.22), channel_id=1, source_target_pairs={{0,3},{1,0},{2,1},{3,2},{4,7},{5,4},{6,5},{7,6},{8,11},{9,8},{10,9... | collective-permute-start | bytes 1572872 | tf_op jit(solution)/shard_map/ppermute | solution.py:43
  21.1 14.0 %collective-permute-start.3 = (s32[]{:T(128)}, s32[]{:T(128)}, u32[]{:S(2)}, u32[]{:S(2)}) collective-permute-start(s32[]{:T(128)} %bitcast.9), channel_id=1, source_target_pairs={{0,508},{4,0},{8,4},{12,8},{16,12},{20,16},{24,20},{28,24},{32,28}... | collective-permute-start | bytes 20 | tf_op jit(solution)/shard_map/ppermute | solution.py:35
  24.6 16.3 %collective-permute-start.5 = (s32[]{:T(128)}, s32[]{:T(128)}, u32[]{:S(2)}, u32[]{:S(2)}) collective-permute-start(s32[]{:T(128)} %bitcast.13), channel_id=1, source_target_pairs={{0,256},{4,260},{8,264},{12,268},{16,272},{20,276},{24,280},{28,28... | collective-permute-start | bytes 20 | tf_op jit(solution)/shard_map/ppermute | solution.py:35
  35.1 6.6 %collective-permute-start.4 = (s32[]{:T(128)}, s32[]{:T(128)}, u32[]{:S(2)}, u32[]{:S(2)}) collective-permute-start(s32[]{:T(128)} %bitcast.11), channel_id=1, source_target_pairs={{0,4},{4,8},{8,12},{12,16},{16,20},{20,24},{24,28},{28,32},{32,36}... | collective-permute-start | bytes 20 | tf_op jit(solution)/shard_map/ppermute | solution.py:35
  55.3 13.9 %collective-permute-start.6 = (bf16[64,512]{1,0:T(8,128)(2,1)}, bf16[64,512]{1,0:T(8,128)(2,1)}, u32[]{:S(2)}, u32[]{:S(2)}) collective-permute-start(bf16[64,512]{1,0:T(8,128)(2,1)} %get-tuple-element.44), channel_id=1, source_target_pairs={{0,4},{4,8},{8,12},{12,16},{16,20},{20,24},{24,28},{28,32},{32,36}... | collective-permute-start | bytes 196616 | tf_op jit(solution)/shard_map/ppermute | solution.py:61
  62.9 9.3 %collective-permute-start.8 = (bf16[64,512]{1,0:T(8,128)(2,1)}, bf16[64,512]{1,0:T(8,128)(2,1)}, u32[]{:S(2)}, u32[]{:S(2)}) collective-permute-start(bf16[64,512]{1,0:T(8,128)(2,1)} %get-tuple-element.45), channel_id=1, source_target_pairs={{0,256},{4,260},{8,264},{12,268},{16,272},{20,276},{24,280},{28,28... | collective-permute-start | bytes 196616 | tf_op jit(solution)/shard_map/ppermute | solution.py:61
  64.9 9.2 %collective-permute-start.7 = (bf16[64,512]{1,0:T(8,128)(2,1)}, bf16[64,512]{1,0:T(8,128)(2,1)}, u32[]{:S(2)}, u32[]{:S(2)}) collective-permute-start(bf16[64,512]{1,0:T(8,128)(2,1)} %get-tuple-element.46), channel_id=1, source_target_pairs={{0,508},{4,0},{8,4},{12,8},{16,12},{20,16},{24,20},{28,24},{32,28}... | collective-permute-start | bytes 196616 | tf_op jit(solution)/shard_map/ppermute | solution.py:61
  75.7 22.2 %copy-start = (bf16[3,4,128,512]{3,2,1,0:T(8,128)(2,1)S(1)}, bf16[3,4,128,512]{3,2,1,0:T(8,128)(2,1)}, u32[]{:S(2)}) copy-start(bf16[3,4,128,512]{3,2,1,0:T(8,128)(2,1)} %all-gather.2.cloned.1.call-done) | copy-start | bytes 4718596
  78.6 19.7 %copy-start.3 = (f32[8,64,512]{2,1,0:T(8,128)S(1)}, f32[8,64,512]{2,1,0:T(8,128)}, u32[]{:S(2)}) copy-start(f32[8,64,512]{2,1,0:T(8,128)} %copy-done.2) | copy-start | bytes 3145732
  78.7 19.7 %copy-start.19 = (f32[8]{0:T(128)S(1)}, f32[8]{0:T(128)}, u32[]{:S(2)}) copy-start(f32[8]{0:T(128)} %get-tuple-element.7) | copy-start | bytes 100
  78.7 19.7 %copy-start.21 = (f32[8]{0:T(128)S(1)}, f32[8]{0:T(128)}, u32[]{:S(2)}) copy-start(f32[8]{0:T(128)} %get-tuple-element.8) | copy-start | bytes 100
  78.7 13.5 %collective-permute-start.9 = (bf16[64,512]{1,0:T(8,128)(2,1)S(1)}, bf16[64,512]{1,0:T(8,128)(2,1)S(1)}, u32[]{:S(2)}, u32[]{:S(2)}) collective-permute-start(bf16[64,512]{1,0:T(8,128)(2,1)S(1)} %get-tuple-element.41), channel_id=1, source_target_pairs={{0,4},{4,8},{8,12},{12,16},{16,20},{20,24},{24,28},{28,32},{32,36}... | collective-permute-start | bytes 196616 | tf_op jit(solution)/shard_map/ppermute | solution.py:61
  81.0 11.6 %collective-permute-start.11 = (bf16[64,512]{1,0:T(8,128)(2,1)S(1)}, bf16[64,512]{1,0:T(8,128)(2,1)S(1)}, u32[]{:S(2)}, u32[]{:S(2)}) collective-permute-start(bf16[64,512]{1,0:T(8,128)(2,1)S(1)} %get-tuple-element.42), channel_id=1, source_target_pairs={{0,256},{4,260},{8,264},{12,268},{16,272},{20,276},{24,280},{28,28... | collective-permute-start | bytes 196616 | tf_op jit(solution)/shard_map/ppermute | solution.py:61
  88.3 8.9 %collective-permute-start.10 = (bf16[64,512]{1,0:T(8,128)(2,1)S(1)}, bf16[64,512]{1,0:T(8,128)(2,1)S(1)}, u32[]{:S(2)}, u32[]{:S(2)}) collective-permute-start(bf16[64,512]{1,0:T(8,128)(2,1)S(1)} %get-tuple-element.43), channel_id=1, source_target_pairs={{0,508},{4,0},{8,4},{12,8},{16,12},{20,16},{24,20},{28,24},{32,28}... | collective-permute-start | bytes 196616 | tf_op jit(solution)/shard_map/ppermute | solution.py:61
  111.3 8.3 %collective-permute-start.12 = (bf16[64,512]{1,0:T(8,128)(2,1)S(1)}, bf16[64,512]{1,0:T(8,128)(2,1)S(1)}, u32[]{:S(2)}, u32[]{:S(2)}) collective-permute-start(bf16[64,512]{1,0:T(8,128)(2,1)S(1)} %get-tuple-element.38), channel_id=1, source_target_pairs={{0,4},{4,8},{8,12},{12,16},{16,20},{20,24},{24,28},{28,32},{32,36}... | collective-permute-start | bytes 196616 | tf_op jit(solution)/shard_map/ppermute | solution.py:61
  113.4 10.4 %collective-permute-start.14 = (bf16[64,512]{1,0:T(8,128)(2,1)S(1)}, bf16[64,512]{1,0:T(8,128)(2,1)S(1)}, u32[]{:S(2)}, u32[]{:S(2)}) collective-permute-start(bf16[64,512]{1,0:T(8,128)(2,1)S(1)} %get-tuple-element.39), channel_id=1, source_target_pairs={{0,256},{4,260},{8,264},{12,268},{16,272},{20,276},{24,280},{28,28... | collective-permute-start | bytes 196616 | tf_op jit(solution)/shard_map/ppermute | solution.py:61
  115.5 8.9 %collective-permute-start.13 = (bf16[64,512]{1,0:T(8,128)(2,1)S(1)}, bf16[64,512]{1,0:T(8,128)(2,1)S(1)}, u32[]{:S(2)}, u32[]{:S(2)}) collective-permute-start(bf16[64,512]{1,0:T(8,128)(2,1)S(1)} %get-tuple-element.40), channel_id=1, source_target_pairs={{0,508},{4,0},{8,4},{12,8},{16,12},{20,16},{24,20},{28,24},{32,28}... | collective-permute-start | bytes 196616 | tf_op jit(solution)/shard_map/ppermute | solution.py:61
  125.2 12.5 %collective-permute-start.15 = (bf16[64,512]{1,0:T(8,128)(2,1)S(1)}, bf16[64,512]{1,0:T(8,128)(2,1)S(1)}, u32[]{:S(2)}, u32[]{:S(2)}) collective-permute-start(bf16[64,512]{1,0:T(8,128)(2,1)S(1)} %get-tuple-element.35), channel_id=1, source_target_pairs={{0,4},{4,8},{8,12},{12,16},{16,20},{20,24},{24,28},{28,32},{32,36}... | collective-permute-start | bytes 196616 | tf_op jit(solution)/shard_map/ppermute | solution.py:61
  127.2 10.4 %collective-permute-start.17 = (bf16[64,512]{1,0:T(8,128)(2,1)S(1)}, bf16[64,512]{1,0:T(8,128)(2,1)S(1)}, u32[]{:S(2)}, u32[]{:S(2)}) collective-permute-start(bf16[64,512]{1,0:T(8,128)(2,1)S(1)} %get-tuple-element.36), channel_id=1, source_target_pairs={{0,256},{4,260},{8,264},{12,268},{16,272},{20,276},{24,280},{28,28... | collective-permute-start | bytes 196616 | tf_op jit(solution)/shard_map/ppermute | solution.py:61
  134.3 8.9 %collective-permute-start.16 = (bf16[64,512]{1,0:T(8,128)(2,1)S(1)}, bf16[64,512]{1,0:T(8,128)(2,1)S(1)}, u32[]{:S(2)}, u32[]{:S(2)}) collective-permute-start(bf16[64,512]{1,0:T(8,128)(2,1)S(1)} %get-tuple-element.37), channel_id=1, source_target_pairs={{0,508},{4,0},{8,4},{12,8},{16,12},{20,16},{24,20},{28,24},{32,28}... | collective-permute-start | bytes 196616 | tf_op jit(solution)/shard_map/ppermute | solution.py:61
  (24 other events, 217.5 us)
Sparse Core Ops, SparseCore 0:
  20.6 31.8 all-gather.1

commit v7 on v6

--- a/solution.py
+++ b/solution.py
@@ -40,15 +40,18 @@
     w_full = w_full.reshape(slot_cap, sub_width, sub_width)
     own_state = jnp.stack([activity[:, 0], ext_input[:, 0].astype(jnp.float32)])
     by_shift = [own_state] + [
-        lax.ppermute(own_state, "blk", [(b, (b + s) % n_blk) for b in range(n_blk)]) for s in range(1, n_blk)
+        lax.ppermute(own_state, "blk", [((b + s) % n_blk, b) for b in range(n_blk)]) for s in range(1, n_blk)
     ]
-    by_shift = jnp.stack(by_shift, axis=2)
-    part_to_shift = (my_blk - jnp.arange(n_blk)) % n_blk
-    state_full = jnp.take(by_shift, part_to_shift, axis=2)
+    twice = jnp.stack(by_shift + by_shift, axis=2)
+    state_full = lax.dynamic_slice_in_dim(twice, (n_blk - my_blk) % n_blk, n_blk, axis=2)
     state_full = state_full.transpose(0, 1, 3, 2, 4).reshape(2, sub_dev, trials, sub_width)
     current = state_full[0]
     drive_in = state_full[1]
-    drive_provided = jnp.take(drive_in, provide, axis=0)
+
+    def pick(x, idx):
+        return jnp.stack([lax.dynamic_index_in_dim(x, idx[k], 0, keepdims=False) for k in range(slot_cap)])
+
+    drive_provided = pick(drive_in, provide)
 
     def advance(cur, contrib, sel, drive):
         summed = sum(sel[k][:, None, None] * contrib[k][None] for k in range(slot_cap))
@@ -61,18 +64,18 @@
             got.append(lax.ppermute(payload[k], "area", perm))
         return jnp.stack(got)
 
-    payload = jnp.tanh(jnp.take(current, provide, axis=0)).astype(jnp.bfloat16)
+    payload = jnp.tanh(pick(current, provide)).astype(jnp.bfloat16)
     pre_list = []
     post_list = []
     for step_idx in range(STEPS):
         presyn = exchange(payload)
         contrib = jnp.einsum("knu,kuv->knv", presyn, w_full, preferred_element_type=jnp.float32)
         if step_idx + 1 < STEPS:
-            provided_now = advance(jnp.take(current, provide, axis=0), contrib, select_provided, drive_provided)
+            provided_now = advance(pick(current, provide), contrib, select_provided, drive_provided)
             payload = jnp.tanh(provided_now).astype(jnp.bfloat16)
         current = advance(current, contrib, select, drive_in)
         pre_list.append(lax.dynamic_slice_in_dim(presyn, my_blk * quarter, quarter, 2))
-        post_list.append(jnp.tanh(jnp.take(current, slot_dst, axis=0)).astype(jnp.bfloat16))
+        post_list.append(jnp.tanh(pick(current, slot_dst)).astype(jnp.bfloat16))
     final_state = lax.dynamic_slice_in_dim(current, my_blk * quarter, quarter, 2)[:, None]
 
     pre_centered = centre(jnp.stack(pre_list, axis=1))

time: 160 us -> 158 us (0.988)
  the two profiles are of different devices: /device:TPU:249 before, /device:TPU:6 now
where the time goes in v7:
time: 158 us; the launch traced here: 156 us
  starting transfers between devices  62.9 us (40%)
  waiting for transfers between devices  33.4 us (21%)
  between operations  26.1 us (17%)
  local copies, waits for them, and re-layouts  16.1 us (10%)
  other arithmetic  13.7 us (9%)
  matrix products  4.21 us (3%)
    ppermute x12, starting transfers between devices, exchange(): got.append(lax.ppermute(payload[k], 'area', perm))  36.8 us
    ppermute x12, waiting for transfers between devices, exchange(): got.append(lax.ppermute(payload[k], 'area', perm))  26.7 us
    ppermute x3, starting transfers between devices, body(): lax.ppermute(own_state, 'blk', [((b + s) % n_blk, b) for b in range(n_blk)])  13 us
    ppermute x3, starting transfers between devices, body(): provide.append(lax.ppermute(wanted[k], 'area', perm))  13 us
    ppermute x3, waiting for transfers between devices, body(): provide.append(lax.ppermute(wanted[k], 'area', perm))  6.59 us
    unnamed x15, local copies, waits for them, and re-layouts  4.17 us
  transfers between devices with their start and end apart: 19, of which 7 were waited for; matrix products, arithmetic and copies ran while one was open for 16% of the time, Pallas kernels for 0%

profile of v7, /device:TPU:6, one launch (start us, length us, event | category | flops | bytes accessed | tf_op | source)
XLA Modules:
  0.0 156.4 jit_solution(15582272480277081791)
XLA Ops:
  9.2 2.7 %collective-permute-start = (f32[2,8,64,128]{3,2,1,0:T(8,128)S(1)}, f32[2,8,64,128]{3,2,1,0:T(8,128)S(1)}, u32[]{:S(2)}, u32[]{:S(2)}) collective-permute-start(f32[2,8,64,128]{3,2,1,0:T(8,128)S(1)} %pad_maximum_fusion.1), channel_id=1, source_target_pairs={{1,0},{2,1},{3,2},{0,3},{5,4},{6,5},{7,6},{4,7},{9,8},{10,9},{11,1... | collective-permute-start | bytes 1572872 | tf_op jit(solution)/shard_map/ppermute | solution.py:43
  11.9 8.4 %collective-permute-start.1 = (f32[2,8,64,128]{3,2,1,0:T(8,128)S(1)}, f32[2,8,64,128]{3,2,1,0:T(8,128)S(1)}, u32[]{:S(2)}, u32[]{:S(2)}) collective-permute-start(f32[2,8,64,128]{3,2,1,0:T(8,128)S(1)} %pad_maximum_fusion.1), channel_id=1, source_target_pairs={{2,0},{3,1},{0,2},{1,3},{6,4},{7,5},{4,6},{5,7},{10,8},{11,9},{8,1... | collective-permute-start | bytes 1572872 | tf_op jit(solution)/shard_map/ppermute | solution.py:43
  20.3 1.9 %collective-permute-start.2 = (f32[2,8,64,128]{3,2,1,0:T(8,128)S(1)}, f32[2,8,64,128]{3,2,1,0:T(8,128)S(1)}, u32[]{:S(2)}, u32[]{:S(2)}) collective-permute-start(f32[2,8,64,128]{3,2,1,0:T(8,128)S(1)} %pad_maximum_fusion.1), channel_id=1, source_target_pairs={{3,0},{0,1},{1,2},{2,3},{7,4},{4,5},{5,6},{6,7},{11,8},{8,9},{9,10... | collective-permute-start | bytes 1572872 | tf_op jit(solution)/shard_map/ppermute | solution.py:43
  23.6 9.2 %collective-permute-start.3 = (s32[]{:T(128)}, s32[]{:T(128)}, u32[]{:S(2)}, u32[]{:S(2)}) collective-permute-start(s32[]{:T(128)} %bitcast.8), channel_id=1, source_target_pairs={{0,508},{4,0},{8,4},{12,8},{16,12},{20,16},{24,20},{28,24},{32,28}... | collective-permute-start | bytes 20 | tf_op jit(solution)/shard_map/ppermute | solution.py:35
  32.8 1.9 %collective-permute-start.5 = (s32[]{:T(128)}, s32[]{:T(128)}, u32[]{:S(2)}, u32[]{:S(2)}) collective-permute-start(s32[]{:T(128)} %bitcast.10), channel_id=1, source_target_pairs={{0,256},{4,260},{8,264},{12,268},{16,272},{20,276},{24,280},{28,28... | collective-permute-start | bytes 20 | tf_op jit(solution)/shard_map/ppermute | solution.py:35
  48.2 6.6 %collective-permute-done.4 = s32[]{:T(128)} collective-permute-done((s32[]{:T(128)}, s32[]{:T(128)}, u32[]{:S(2)}, u32[]{:S(2)}) %collective-permute-start.4) | collective-permute-done | bytes 36 | tf_op jit(solution)/shard_map/ppermute | solution.py:35
  54.8 2.0 %fusion.18 = s32[3]{0:T(128)S(1)} fusion(s32[1,1]{0,1:T(1,128)} %bitcast.26, s32[1,1]{0,1:T(1,128)} %bitcast.25, s32[1,1]{0,1:T(1,128)} %bitcast.24), kind=kLoop, calls=%fused_computation.126 | loop fusion | flops 15 | bytes 24 | tf_op jit(solution)/shard_map/jit(_take)/jit(_where)/select_n | solution.py:37
  57.4 2.0 %compare_and_fusion = pred[3]{0:T(512)(128)(4,1)S(1)} fusion(s32[1]{0:T(128)} %bitcast.23, s32[1]{0:T(128)} %bitcast.22, s32[1]{0:T(128)} %bitcast.21), kind=kLoop, calls=%fused_computation.122 | loop fusion | flops 24 | bytes 15 | tf_op jit(solution)/shard_map/jit(_take)/and | solution.py:37
  77.6 7.8 %collective-permute-start.8 = (bf16[64,512]{1,0:T(8,128)(2,1)S(1)}, bf16[64,512]{1,0:T(8,128)(2,1)S(1)}, u32[]{:S(2)}, u32[]{:S(2)}) collective-permute-start(bf16[64,512]{1,0:T(8,128)(2,1)S(1)} %get-tuple-element.64), channel_id=1, source_target_pairs={{0,256},{4,260},{8,264},{12,268},{16,272},{20,276},{24,280},{28,28... | collective-permute-start | bytes 196616 | tf_op jit(solution)/shard_map/ppermute | solution.py:64
  85.5 1.9 %collective-permute-start.7 = (bf16[64,512]{1,0:T(8,128)(2,1)S(1)}, bf16[64,512]{1,0:T(8,128)(2,1)S(1)}, u32[]{:S(2)}, u32[]{:S(2)}) collective-permute-start(bf16[64,512]{1,0:T(8,128)(2,1)S(1)} %get-tuple-element.65), channel_id=1, source_target_pairs={{0,508},{4,0},{8,4},{12,8},{16,12},{20,16},{24,20},{28,24},{32,28}... | collective-permute-start | bytes 196616 | tf_op jit(solution)/shard_map/ppermute | solution.py:64
  87.4 2.4 %collective-permute-start.6 = (bf16[64,512]{1,0:T(8,128)(2,1)S(1)}, bf16[64,512]{1,0:T(8,128)(2,1)S(1)}, u32[]{:S(2)}, u32[]{:S(2)}) collective-permute-start(bf16[64,512]{1,0:T(8,128)(2,1)S(1)} %get-tuple-element.63), channel_id=1, source_target_pairs={{0,4},{4,8},{8,12},{12,16},{16,20},{20,24},{24,28},{28,32},{32,36}... | collective-permute-start | bytes 196616 | tf_op jit(solution)/shard_map/ppermute | solution.py:64
  89.9 6.9 %collective-permute-done.6 = bf16[64,512]{1,0:T(8,128)(2,1)S(1)} collective-permute-done((bf16[64,512]{1,0:T(8,128)(2,1)S(1)}, bf16[64,512]{1,0:T(8,128)(2,1)S(1)}, u32[]{:S(2)}, u32[]{:S(2)}) %collective-permute-start.6) | collective-permute-done | bytes 65568 | tf_op jit(solution)/shard_map/ppermute | solution.py:64
  99.0 1.9 %collective-permute-start.11 = (bf16[64,512]{1,0:T(8,128)(2,1)S(1)}, bf16[64,512]{1,0:T(8,128)(2,1)S(1)}, u32[]{:S(2)}, u32[]{:S(2)}) collective-permute-start(bf16[64,512]{1,0:T(8,128)(2,1)S(1)} %get-tuple-element.61), channel_id=1, source_target_pairs={{0,256},{4,260},{8,264},{12,268},{16,272},{20,276},{24,280},{28,28... | collective-permute-start | bytes 196616 | tf_op jit(solution)/shard_map/ppermute | solution.py:64
  101.0 1.9 %collective-permute-start.10 = (bf16[64,512]{1,0:T(8,128)(2,1)S(1)}, bf16[64,512]{1,0:T(8,128)(2,1)S(1)}, u32[]{:S(2)}, u32[]{:S(2)}) collective-permute-start(bf16[64,512]{1,0:T(8,128)(2,1)S(1)} %get-tuple-element.62), channel_id=1, source_target_pairs={{0,508},{4,0},{8,4},{12,8},{16,12},{20,16},{24,20},{28,24},{32,28}... | collective-permute-start | bytes 196616 | tf_op jit(solution)/shard_map/ppermute | solution.py:64
  102.9 2.4 %collective-permute-start.9 = (bf16[64,512]{1,0:T(8,128)(2,1)S(1)}, bf16[64,512]{1,0:T(8,128)(2,1)S(1)}, u32[]{:S(2)}, u32[]{:S(2)}) collective-permute-start(bf16[64,512]{1,0:T(8,128)(2,1)S(1)} %get-tuple-element.60), channel_id=1, source_target_pairs={{0,4},{4,8},{8,12},{12,16},{16,20},{20,24},{24,28},{28,32},{32,36}... | collective-permute-start | bytes 196616 | tf_op jit(solution)/shard_map/ppermute | solution.py:64
  105.3 3.8 %collective-permute-done.11 = bf16[64,512]{1,0:T(8,128)(2,1)S(1)} collective-permute-done((bf16[64,512]{1,0:T(8,128)(2,1)S(1)}, bf16[64,512]{1,0:T(8,128)(2,1)S(1)}, u32[]{:S(2)}, u32[]{:S(2)}) %collective-permute-start.11) | collective-permute-done | bytes 65568 | tf_op jit(solution)/shard_map/ppermute | solution.py:64
  109.1 2.7 %collective-permute-done.9 = bf16[64,512]{1,0:T(8,128)(2,1)S(1)} collective-permute-done((bf16[64,512]{1,0:T(8,128)(2,1)S(1)}, bf16[64,512]{1,0:T(8,128)(2,1)S(1)}, u32[]{:S(2)}, u32[]{:S(2)}) %collective-permute-start.9) | collective-permute-done | bytes 65568 | tf_op jit(solution)/shard_map/ppermute | solution.py:64
  113.4 7.8 %collective-permute-start.14 = (bf16[64,512]{1,0:T(8,128)(2,1)S(1)}, bf16[64,512]{1,0:T(8,128)(2,1)S(1)}, u32[]{:S(2)}, u32[]{:S(2)}) collective-permute-start(bf16[64,512]{1,0:T(8,128)(2,1)S(1)} %get-tuple-element.58), channel_id=1, source_target_pairs={{0,256},{4,260},{8,264},{12,268},{16,272},{20,276},{24,280},{28,28... | collective-permute-start | bytes 196616 | tf_op jit(solution)/shard_map/ppermute | solution.py:64
  121.2 1.9 %collective-permute-start.13 = (bf16[64,512]{1,0:T(8,128)(2,1)S(1)}, bf16[64,512]{1,0:T(8,128)(2,1)S(1)}, u32[]{:S(2)}, u32[]{:S(2)}) collective-permute-start(bf16[64,512]{1,0:T(8,128)(2,1)S(1)} %get-tuple-element.59), channel_id=1, source_target_pairs={{0,508},{4,0},{8,4},{12,8},{16,12},{20,16},{24,20},{28,24},{32,28}... | collective-permute-start | bytes 196616 | tf_op jit(solution)/shard_map/ppermute | solution.py:64
  123.1 2.4 %collective-permute-start.12 = (bf16[64,512]{1,0:T(8,128)(2,1)S(1)}, bf16[64,512]{1,0:T(8,128)(2,1)S(1)}, u32[]{:S(2)}, u32[]{:S(2)}) collective-permute-start(bf16[64,512]{1,0:T(8,128)(2,1)S(1)} %get-tuple-element.57), channel_id=1, source_target_pairs={{0,4},{4,8},{8,12},{12,16},{16,20},{20,24},{24,28},{28,32},{32,36}... | collective-permute-start | bytes 196616 | tf_op jit(solution)/shard_map/ppermute | solution.py:64
  125.7 6.9 %collective-permute-done.12 = bf16[64,512]{1,0:T(8,128)(2,1)S(1)} collective-permute-done((bf16[64,512]{1,0:T(8,128)(2,1)S(1)}, bf16[64,512]{1,0:T(8,128)(2,1)S(1)}, u32[]{:S(2)}, u32[]{:S(2)}) %collective-permute-start.12) | collective-permute-done | bytes 65568 | tf_op jit(solution)/shard_map/ppermute | solution.py:64
  137.1 2.4 %collective-permute-start.15 = (bf16[64,512]{1,0:T(8,128)(2,1)S(1)}, bf16[64,512]{1,0:T(8,128)(2,1)S(1)}, u32[]{:S(2)}, u32[]{:S(2)}) collective-permute-start(bf16[64,512]{1,0:T(8,128)(2,1)S(1)} %get-tuple-element.54), channel_id=1, source_target_pairs={{0,4},{4,8},{8,12},{12,16},{16,20},{20,24},{24,28},{28,32},{32,36}... | collective-permute-start | bytes 196616 | tf_op jit(solution)/shard_map/ppermute | solution.py:64
  139.6 3.8 %collective-permute-done.17 = bf16[64,512]{1,0:T(8,128)(2,1)S(1)} collective-permute-done((bf16[64,512]{1,0:T(8,128)(2,1)S(1)}, bf16[64,512]{1,0:T(8,128)(2,1)S(1)}, u32[]{:S(2)}, u32[]{:S(2)}) %collective-permute-start.17) | collective-permute-done | bytes 65568 | tf_op jit(solution)/shard_map/ppermute | solution.py:64
  143.4 2.7 %collective-permute-done.15 = bf16[64,512]{1,0:T(8,128)(2,1)S(1)} collective-permute-done((bf16[64,512]{1,0:T(8,128)(2,1)S(1)}, bf16[64,512]{1,0:T(8,128)(2,1)S(1)}, u32[]{:S(2)}, u32[]{:S(2)}) %collective-permute-start.15) | collective-permute-done | bytes 65568 | tf_op jit(solution)/shard_map/ppermute | solution.py:64
  (94 shorter events, 35.9 us)
Async XLA Ops:
  7.2 60.7 %copy-start.1 = (f32[8,1,64,128]{3,2,1,0:T(8,128)S(1)}, f32[8,1,64,128]{3,2,1,0:T(8,128)}, u32[]{:S(2)}) copy-start(f32[8,1,64,128]{3,2,1,0:T(8,128)} %param.7) | copy-start | bytes 786436
  7.2 89.7 %all-gather.2.cloned.1.call-start = ((), (), s32[]{:S(2)}) async-start(), calls=%async_computation | async-start | bytes 1966080 | tf_op jit(solution)/shard_map/all_gather | solution.py:39
  9.2 56.2 %collective-permute-start = (f32[2,8,64,128]{3,2,1,0:T(8,128)S(1)}, f32[2,8,64,128]{3,2,1,0:T(8,128)S(1)}, u32[]{:S(2)}, u32[]{:S(2)}) collective-permute-start(f32[2,8,64,128]{3,2,1,0:T(8,128)S(1)} %pad_maximum_fusion.1), channel_id=1, source_target_pairs={{1,0},{2,1},{3,2},{0,3},{5,4},{6,5},{7,6},{4,7},{9,8},{10,9},{11,1... | collective-permute-start | bytes 1572872 | tf_op jit(solution)/shard_map/ppermute | solution.py:43
  11.9 54.2 %collective-permute-start.1 = (f32[2,8,64,128]{3,2,1,0:T(8,128)S(1)}, f32[2,8,64,128]{3,2,1,0:T(8,128)S(1)}, u32[]{:S(2)}, u32[]{:S(2)}) collective-permute-start(f32[2,8,64,128]{3,2,1,0:T(8,128)S(1)} %pad_maximum_fusion.1), channel_id=1, source_target_pairs={{2,0},{3,1},{0,2},{1,3},{6,4},{7,5},{4,6},{5,7},{10,8},{11,9},{8,1... | collective-permute-start | bytes 1572872 | tf_op jit(solution)/shard_map/ppermute | solution.py:43
  20.3 46.7 %collective-permute-start.2 = (f32[2,8,64,128]{3,2,1,0:T(8,128)S(1)}, f32[2,8,64,128]{3,2,1,0:T(8,128)S(1)}, u32[]{:S(2)}, u32[]{:S(2)}) collective-permute-start(f32[2,8,64,128]{3,2,1,0:T(8,128)S(1)} %pad_maximum_fusion.1), channel_id=1, source_target_pairs={{3,0},{0,1},{1,2},{2,3},{7,4},{4,5},{5,6},{6,7},{11,8},{8,9},{9,10... | collective-permute-start | bytes 1572872 | tf_op jit(solution)/shard_map/ppermute | solution.py:43
  23.6 22.8 %collective-permute-start.3 = (s32[]{:T(128)}, s32[]{:T(128)}, u32[]{:S(2)}, u32[]{:S(2)}) collective-permute-start(s32[]{:T(128)} %bitcast.8), channel_id=1, source_target_pairs={{0,508},{4,0},{8,4},{12,8},{16,12},{20,16},{24,20},{28,24},{32,28}... | collective-permute-start | bytes 20 | tf_op jit(solution)/shard_map/ppermute | solution.py:35
  32.8 15.5 %collective-permute-start.5 = (s32[]{:T(128)}, s32[]{:T(128)}, u32[]{:S(2)}, u32[]{:S(2)}) collective-permute-start(s32[]{:T(128)} %bitcast.10), channel_id=1, source_target_pairs={{0,256},{4,260},{8,264},{12,268},{16,272},{20,276},{24,280},{28,28... | collective-permute-start | bytes 20 | tf_op jit(solution)/shard_map/ppermute | solution.py:35
  46.3 8.5 %collective-permute-start.4 = (s32[]{:T(128)}, s32[]{:T(128)}, u32[]{:S(2)}, u32[]{:S(2)}) collective-permute-start(s32[]{:T(128)} %bitcast.9), channel_id=1, source_target_pairs={{0,4},{4,8},{8,12},{12,16},{16,20},{20,24},{24,28},{28,32},{32,36}... | collective-permute-start | bytes 20 | tf_op jit(solution)/shard_map/ppermute | solution.py:35
  77.6 12.2 %collective-permute-start.8 = (bf16[64,512]{1,0:T(8,128)(2,1)S(1)}, bf16[64,512]{1,0:T(8,128)(2,1)S(1)}, u32[]{:S(2)}, u32[]{:S(2)}) collective-permute-start(bf16[64,512]{1,0:T(8,128)(2,1)S(1)} %get-tuple-element.64), channel_id=1, source_target_pairs={{0,256},{4,260},{8,264},{12,268},{16,272},{20,276},{24,280},{28,28... | collective-permute-start | bytes 196616 | tf_op jit(solution)/shard_map/ppermute | solution.py:64
  85.5 4.4 %collective-permute-start.7 = (bf16[64,512]{1,0:T(8,128)(2,1)S(1)}, bf16[64,512]{1,0:T(8,128)(2,1)S(1)}, u32[]{:S(2)}, u32[]{:S(2)}) collective-permute-start(bf16[64,512]{1,0:T(8,128)(2,1)S(1)} %get-tuple-element.65), channel_id=1, source_target_pairs={{0,508},{4,0},{8,4},{12,8},{16,12},{20,16},{24,20},{28,24},{32,28}... | collective-permute-start | bytes 196616 | tf_op jit(solution)/shard_map/ppermute | solution.py:64
  87.4 9.4 %collective-permute-start.6 = (bf16[64,512]{1,0:T(8,128)(2,1)S(1)}, bf16[64,512]{1,0:T(8,128)(2,1)S(1)}, u32[]{:S(2)}, u32[]{:S(2)}) collective-permute-start(bf16[64,512]{1,0:T(8,128)(2,1)S(1)} %get-tuple-element.63), channel_id=1, source_target_pairs={{0,4},{4,8},{8,12},{12,16},{16,20},{20,24},{24,28},{28,32},{32,36}... | collective-permute-start | bytes 196616 | tf_op jit(solution)/shard_map/ppermute | solution.py:64
  96.8 15.0 %copy-start = (bf16[3,4,128,512]{3,2,1,0:T(8,128)(2,1)S(1)}, bf16[3,4,128,512]{3,2,1,0:T(8,128)(2,1)}, u32[]{:S(2)}) copy-start(bf16[3,4,128,512]{3,2,1,0:T(8,128)(2,1)} %all-gather.2.cloned.1.call-done) | copy-start | bytes 4718596
  96.8 15.4 %copy-start.2 = (f32[8]{0:T(128)S(1)}, f32[8]{0:T(128)}, u32[]{:S(2)}) copy-start(f32[8]{0:T(128)} %get-tuple-element.7) | copy-start | bytes 100
  96.8 15.4 %copy-start.3 = (f32[8]{0:T(128)S(1)}, f32[8]{0:T(128)}, u32[]{:S(2)}) copy-start(f32[8]{0:T(128)} %get-tuple-element.8) | copy-start | bytes 100
  99.0 10.1 %collective-permute-start.11 = (bf16[64,512]{1,0:T(8,128)(2,1)S(1)}, bf16[64,512]{1,0:T(8,128)(2,1)S(1)}, u32[]{:S(2)}, u32[]{:S(2)}) collective-permute-start(bf16[64,512]{1,0:T(8,128)(2,1)S(1)} %get-tuple-element.61), channel_id=1, source_target_pairs={{0,256},{4,260},{8,264},{12,268},{16,272},{20,276},{24,280},{28,28... | collective-permute-start | bytes 196616 | tf_op jit(solution)/shard_map/ppermute | solution.py:64
  101.0 8.1 %collective-permute-start.10 = (bf16[64,512]{1,0:T(8,128)(2,1)S(1)}, bf16[64,512]{1,0:T(8,128)(2,1)S(1)}, u32[]{:S(2)}, u32[]{:S(2)}) collective-permute-start(bf16[64,512]{1,0:T(8,128)(2,1)S(1)} %get-tuple-element.62), channel_id=1, source_target_pairs={{0,508},{4,0},{8,4},{12,8},{16,12},{20,16},{24,20},{28,24},{32,28}... | collective-permute-start | bytes 196616 | tf_op jit(solution)/shard_map/ppermute | solution.py:64
  102.9 8.9 %collective-permute-start.9 = (bf16[64,512]{1,0:T(8,128)(2,1)S(1)}, bf16[64,512]{1,0:T(8,128)(2,1)S(1)}, u32[]{:S(2)}, u32[]{:S(2)}) collective-permute-start(bf16[64,512]{1,0:T(8,128)(2,1)S(1)} %get-tuple-element.60), channel_id=1, source_target_pairs={{0,4},{4,8},{8,12},{12,16},{16,20},{20,24},{24,28},{28,32},{32,36}... | collective-permute-start | bytes 196616 | tf_op jit(solution)/shard_map/ppermute | solution.py:64
  113.4 12.4 %collective-permute-start.14 = (bf16[64,512]{1,0:T(8,128)(2,1)S(1)}, bf16[64,512]{1,0:T(8,128)(2,1)S(1)}, u32[]{:S(2)}, u32[]{:S(2)}) collective-permute-start(bf16[64,512]{1,0:T(8,128)(2,1)S(1)} %get-tuple-element.58), channel_id=1, source_target_pairs={{0,256},{4,260},{8,264},{12,268},{16,272},{20,276},{24,280},{28,28... | collective-permute-start | bytes 196616 | tf_op jit(solution)/shard_map/ppermute | solution.py:64
  121.2 4.5 %collective-permute-start.13 = (bf16[64,512]{1,0:T(8,128)(2,1)S(1)}, bf16[64,512]{1,0:T(8,128)(2,1)S(1)}, u32[]{:S(2)}, u32[]{:S(2)}) collective-permute-start(bf16[64,512]{1,0:T(8,128)(2,1)S(1)} %get-tuple-element.59), channel_id=1, source_target_pairs={{0,508},{4,0},{8,4},{12,8},{16,12},{20,16},{24,20},{28,24},{32,28}... | collective-permute-start | bytes 196616 | tf_op jit(solution)/shard_map/ppermute | solution.py:64
  123.1 9.5 %collective-permute-start.12 = (bf16[64,512]{1,0:T(8,128)(2,1)S(1)}, bf16[64,512]{1,0:T(8,128)(2,1)S(1)}, u32[]{:S(2)}, u32[]{:S(2)}) collective-permute-start(bf16[64,512]{1,0:T(8,128)(2,1)S(1)} %get-tuple-element.57), channel_id=1, source_target_pairs={{0,4},{4,8},{8,12},{12,16},{16,20},{20,24},{24,28},{28,32},{32,36}... | collective-permute-start | bytes 196616 | tf_op jit(solution)/shard_map/ppermute | solution.py:64
  133.3 10.1 %collective-permute-start.17 = (bf16[64,512]{1,0:T(8,128)(2,1)S(1)}, bf16[64,512]{1,0:T(8,128)(2,1)S(1)}, u32[]{:S(2)}, u32[]{:S(2)}) collective-permute-start(bf16[64,512]{1,0:T(8,128)(2,1)S(1)} %get-tuple-element.55), channel_id=1, source_target_pairs={{0,256},{4,260},{8,264},{12,268},{16,272},{20,276},{24,280},{28,28... | collective-permute-start | bytes 196616 | tf_op jit(solution)/shard_map/ppermute | solution.py:64
  135.2 8.1 %collective-permute-start.16 = (bf16[64,512]{1,0:T(8,128)(2,1)S(1)}, bf16[64,512]{1,0:T(8,128)(2,1)S(1)}, u32[]{:S(2)}, u32[]{:S(2)}) collective-permute-start(bf16[64,512]{1,0:T(8,128)(2,1)S(1)} %get-tuple-element.56), channel_id=1, source_target_pairs={{0,508},{4,0},{8,4},{12,8},{16,12},{20,16},{24,20},{28,24},{32,28}... | collective-permute-start | bytes 196616 | tf_op jit(solution)/shard_map/ppermute | solution.py:64
  137.1 8.9 %collective-permute-start.15 = (bf16[64,512]{1,0:T(8,128)(2,1)S(1)}, bf16[64,512]{1,0:T(8,128)(2,1)S(1)}, u32[]{:S(2)}, u32[]{:S(2)}) collective-permute-start(bf16[64,512]{1,0:T(8,128)(2,1)S(1)} %get-tuple-element.54), channel_id=1, source_target_pairs={{0,4},{4,8},{8,12},{12,16},{16,20},{20,24},{24,28},{28,32},{32,36}... | collective-permute-start | bytes 196616 | tf_op jit(solution)/shard_map/ppermute | solution.py:64
  146.5 2.0 %copy-start.4 = (f32[3]{0:T(128)S(1)}, f32[3]{0:T(128)}, u32[]{:S(2)}) copy-start(f32[3]{0:T(128)} %and_convert_fusion) | copy-start | bytes 40
Sparse Core Ops, SparseCore 0:
  22.4 31.8 all-gather.1

commit v8 on v7

--- a/solution.py
+++ b/solution.py
@@ -42,16 +42,25 @@
     by_shift = [own_state] + [
         lax.ppermute(own_state, "blk", [((b + s) % n_blk, b) for b in range(n_blk)]) for s in range(1, n_blk)
     ]
-    twice = jnp.stack(by_shift + by_shift, axis=2)
-    state_full = lax.dynamic_slice_in_dim(twice, (n_blk - my_blk) % n_blk, n_blk, axis=2)
-    state_full = state_full.transpose(0, 1, 3, 2, 4).reshape(2, sub_dev, trials, sub_width)
-    current = state_full[0]
-    drive_in = state_full[1]
+
+    def in_part_order(pieces):
+        ordered = []
+        for j in range(n_blk):
+            shift_j = (j - my_blk) % n_blk
+            out = pieces[0]
+            for s in range(1, n_blk):
+                out = jnp.where(shift_j == s, pieces[s], out)
+            ordered.append(out)
+        return jnp.stack(ordered, axis=-2)
 
     def pick(x, idx):
         return jnp.stack([lax.dynamic_index_in_dim(x, idx[k], 0, keepdims=False) for k in range(slot_cap)])
 
+    state_full = in_part_order(by_shift).reshape(2, sub_dev, trials, sub_width)
+    current = state_full[0]
+    drive_in = state_full[1]
     drive_provided = pick(drive_in, provide)
+    first_act = in_part_order([pick(piece[0], provide) for piece in by_shift]).reshape(slot_cap, trials, sub_width)
 
     def advance(cur, contrib, sel, drive):
         summed = sum(sel[k][:, None, None] * contrib[k][None] for k in range(slot_cap))
@@ -64,7 +73,7 @@
             got.append(lax.ppermute(payload[k], "area", perm))
         return jnp.stack(got)
 
-    payload = jnp.tanh(pick(current, provide)).astype(jnp.bfloat16)
+    payload = jnp.tanh(first_act).astype(jnp.bfloat16)
     pre_list = []
     post_list = []
     for step_idx in range(STEPS):

time: 158 us -> 142 us (0.90)
  waiting for transfers between devices: 33.4 us -> 13.3 us
  starting transfers between devices: 62.9 us -> 76.6 us
  local copies, waits for them, and re-layouts: 16.1 us -> 9.24 us
  other arithmetic: 13.7 us -> 11 us
    ppermute x12, waiting for transfers between devices: 26.7 us -> 6.79 us  [exchange(): got.append(lax.ppermute(payload[k], 'area', perm))]
    ppermute x12, starting transfers between devices: 36.8 us -> 50.5 us  [exchange(): got.append(lax.ppermute(payload[k], 'area', perm))]
    unnamed x15 -> x19, local copies, waits for them, and re-layouts: 4.17 us -> 0.47 us
    unnamed x2 -> x0, other arithmetic: 2.61 us -> none
    transpose x1 -> x0, local copies, waits for them, and re-layouts: 1.73 us -> none  [body(): state_full.transpose(0, 1, 3, 2, 4).reshape(2, sub_dev, trials, sub_width)]
  transfers between devices with their start and end apart: 19 -> 19, of which waited for: 7 -> 7; matrix products, arithmetic and copies ran while one was open for 16% -> 10% of each run, Pallas kernels for 0% -> 0%
where the time goes in v8:
time: 142 us; the launch traced here: 140 us
  starting transfers between devices  76.6 us (54%)
  between operations  26.2 us (18%)
  waiting for transfers between devices  13.3 us (9%)
  other arithmetic  11 us (8%)
  local copies, waits for them, and re-layouts  9.24 us (7%)
  matrix products  4.09 us (3%)
    ppermute x12, starting transfers between devices, exchange(): got.append(lax.ppermute(payload[k], 'area', perm))  50.5 us
    ppermute x3, starting transfers between devices, body(): provide.append(lax.ppermute(wanted[k], 'area', perm))  13 us
    ppermute x3, starting transfers between devices, body(): lax.ppermute(own_state, 'blk', [((b + s) % n_blk, b) for b in range(n_blk)])  13 us
    ppermute x12, waiting for transfers between devices, exchange(): got.append(lax.ppermute(payload[k], 'area', perm))  6.79 us
    ppermute x3, waiting for transfers between devices, body(): provide.append(lax.ppermute(wanted[k], 'area', perm))  6.44 us
    dot_general x4, matrix products, body(): jnp.einsum('knu,kuv->knv', presyn, w_full, preferred_element_type=jnp.flo...  2.95 us
  transfers between devices with their start and end apart: 19, of which 7 were waited for; matrix products, arithmetic and copies ran while one was open for 10% of the time, Pallas kernels for 0%

profile of v8, /device:TPU:6, one launch (start us, length us, event | category | flops | bytes accessed | tf_op | source)
XLA Modules:
  0.0 140.3 jit_solution(8142210331351419926)
XLA Ops:
  9.2 2.7 %collective-permute-start.2 = (f32[2,8,64,128]{3,2,1,0:T(8,128)S(1)}, f32[2,8,64,128]{3,2,1,0:T(8,128)S(1)}, u32[]{:S(2)}, u32[]{:S(2)}) collective-permute-start(f32[2,8,64,128]{3,2,1,0:T(8,128)S(1)} %pad_maximum_fusion.2), channel_id=1, source_target_pairs={{1,0},{2,1},{3,2},{0,3},{5,4},{6,5},{7,6},{4,7},{9,8},{10,9},{11,1... | collective-permute-start | bytes 1572872 | tf_op jit(solution)/shard_map/ppermute | solution.py:43
  11.9 8.4 %collective-permute-start.1 = (f32[2,8,64,128]{3,2,1,0:T(8,128)S(1)}, f32[2,8,64,128]{3,2,1,0:T(8,128)S(1)}, u32[]{:S(2)}, u32[]{:S(2)}) collective-permute-start(f32[2,8,64,128]{3,2,1,0:T(8,128)S(1)} %pad_maximum_fusion.2), channel_id=1, source_target_pairs={{2,0},{3,1},{0,2},{1,3},{6,4},{7,5},{4,6},{5,7},{10,8},{11,9},{8,1... | collective-permute-start | bytes 1572872 | tf_op jit(solution)/shard_map/ppermute | solution.py:43
  20.3 1.9 %collective-permute-start = (f32[2,8,64,128]{3,2,1,0:T(8,128)S(1)}, f32[2,8,64,128]{3,2,1,0:T(8,128)S(1)}, u32[]{:S(2)}, u32[]{:S(2)}) collective-permute-start(f32[2,8,64,128]{3,2,1,0:T(8,128)S(1)} %pad_maximum_fusion.2), channel_id=1, source_target_pairs={{3,0},{0,1},{1,2},{2,3},{7,4},{4,5},{5,6},{6,7},{11,8},{8,9},{9,10... | collective-permute-start | bytes 1572872 | tf_op jit(solution)/shard_map/ppermute | solution.py:43
  22.9 9.2 %collective-permute-start.3 = (s32[]{:T(128)}, s32[]{:T(128)}, u32[]{:S(2)}, u32[]{:S(2)}) collective-permute-start(s32[]{:T(128)} %bitcast.7), channel_id=1, source_target_pairs={{0,508},{4,0},{8,4},{12,8},{16,12},{20,16},{24,20},{28,24},{32,28}... | collective-permute-start | bytes 20 | tf_op jit(solution)/shard_map/ppermute | solution.py:35
  32.1 1.9 %collective-permute-start.5 = (s32[]{:T(128)}, s32[]{:T(128)}, u32[]{:S(2)}, u32[]{:S(2)}) collective-permute-start(s32[]{:T(128)} %bitcast.11), channel_id=1, source_target_pairs={{0,256},{4,260},{8,264},{12,268},{16,272},{20,276},{24,280},{28,28... | collective-permute-start | bytes 20 | tf_op jit(solution)/shard_map/ppermute | solution.py:35
  42.2 1.9 %collective-permute-start.4 = (s32[]{:T(128)}, s32[]{:T(128)}, u32[]{:S(2)}, u32[]{:S(2)}) collective-permute-start(s32[]{:T(128)} %bitcast.9), channel_id=1, source_target_pairs={{0,4},{4,8},{8,12},{12,16},{16,20},{20,24},{24,28},{28,32},{32,36}... | collective-permute-start | bytes 20 | tf_op jit(solution)/shard_map/ppermute | solution.py:35
  44.1 6.4 %collective-permute-done.4 = s32[]{:T(128)} collective-permute-done((s32[]{:T(128)}, s32[]{:T(128)}, u32[]{:S(2)}, u32[]{:S(2)}) %collective-permute-start.4) | collective-permute-done | bytes 36 | tf_op jit(solution)/shard_map/ppermute | solution.py:35
  50.5 1.8 %fusion.19 = s32[3]{0:T(128)S(1)} fusion(s32[1,1]{0,1:T(1,128)} %bitcast.34, s32[1,1]{0,1:T(1,128)} %bitcast.33, s32[1,1]{0,1:T(1,128)} %bitcast.32), kind=kLoop, calls=%fused_computation.151 | loop fusion | flops 15 | bytes 24 | tf_op jit(solution)/shard_map/jit(_take)/jit(_where)/select_n | solution.py:37
  58.3 1.8 %compare_and_fusion = pred[3]{0:T(512)(128)(4,1)S(1)} fusion(s32[1]{0:T(128)} %bitcast.31, s32[1]{0:T(128)} %bitcast.30, s32[1]{0:T(128)} %bitcast.29), kind=kLoop, calls=%fused_computation.147 | loop fusion | flops 24 | bytes 15 | tf_op jit(solution)/shard_map/jit(_take)/and | solution.py:37
  62.2 1.9 %collective-permute-start.7 = (bf16[64,512]{1,0:T(8,128)(2,1)S(1)}, bf16[64,512]{1,0:T(8,128)(2,1)S(1)}, u32[]{:S(2)}, u32[]{:S(2)}) collective-permute-start(bf16[64,512]{1,0:T(8,128)(2,1)S(1)} %bitcast.250), channel_id=1, source_target_pairs={{0,508},{4,0},{8,4},{12,8},{16,12},{20,16},{24,20},{28,24},{32,28}... | collective-permute-start | bytes 196616 | tf_op jit(solution)/shard_map/ppermute | solution.py:73
  64.1 7.8 %collective-permute-start.8 = (bf16[64,512]{1,0:T(8,128)(2,1)S(1)}, bf16[64,512]{1,0:T(8,128)(2,1)S(1)}, u32[]{:S(2)}, u32[]{:S(2)}) collective-permute-start(bf16[64,512]{1,0:T(8,128)(2,1)S(1)} %bitcast.249), channel_id=1, source_target_pairs={{0,256},{4,260},{8,264},{12,268},{16,272},{20,276},{24,280},{28,28... | collective-permute-start | bytes 196616 | tf_op jit(solution)/shard_map/ppermute | solution.py:73
  72.0 2.1 %collective-permute-start.6 = (bf16[64,512]{1,0:T(8,128)(2,1)S(1)}, bf16[64,512]{1,0:T(8,128)(2,1)S(1)}, u32[]{:S(2)}, u32[]{:S(2)}) collective-permute-start(bf16[64,512]{1,0:T(8,128)(2,1)S(1)} %bitcast.248), channel_id=1, source_target_pairs={{0,4},{4,8},{8,12},{12,16},{16,20},{20,24},{24,28},{28,32},{32,36}... | collective-permute-start | bytes 196616 | tf_op jit(solution)/shard_map/ppermute | solution.py:73
  77.0 1.9 %copy.13 = f32[1,8,64,4,128]{4,3,2,1,0:T(4,128)S(1)} copy(f32[1,8,64,4,128]{4,2,1,0,3:T(8,128)} %get-tuple-element.17) | data formatting | bytes 2097152 | tf_op jit(solution)/shard_map/slice | solution.py:61
  80.9 1.8 %fusion.24 = f32[3,64,512]{2,1,0:T(8,128)S(1)} fusion(bf16[3,512,512]{2,1,0:T(8,128)(2,1)} %bitcast.166, bf16[1,64,512]{2,1,0:T(8,128)(2,1)S(1)} %bitcast.223, bf16[1,64,512]{2,1,0:T(8,128)(2,1)S(1)} %bitcast.221, bf16[1,64,512]{2,1,0:T(8,128)(2,1)S(1)} %bitcast.225), kind=kOutput, calls=%fused_computation.157 | convolution fusion | flops 100859904 | bytes 2162688 | tf_op jit(solution)/shard_map/knu,kuv->knv/dot_general | solution.py:81
  83.0 2.1 %collective-permute-start.9 = (bf16[64,512]{1,0:T(8,128)(2,1)S(1)}, bf16[64,512]{1,0:T(8,128)(2,1)S(1)}, u32[]{:S(2)}, u32[]{:S(2)}) collective-permute-start(bf16[64,512]{1,0:T(8,128)(2,1)S(1)} %get-tuple-element.75), channel_id=1, source_target_pairs={{0,4},{4,8},{8,12},{12,16},{16,20},{20,24},{24,28},{28,32},{32,36}... | collective-permute-start | bytes 196616 | tf_op jit(solution)/shard_map/ppermute | solution.py:73
  85.0 2.8 %collective-permute-start.11 = (bf16[64,512]{1,0:T(8,128)(2,1)S(1)}, bf16[64,512]{1,0:T(8,128)(2,1)S(1)}, u32[]{:S(2)}, u32[]{:S(2)}) collective-permute-start(bf16[64,512]{1,0:T(8,128)(2,1)S(1)} %get-tuple-element.76), channel_id=1, source_target_pairs={{0,256},{4,260},{8,264},{12,268},{16,272},{20,276},{24,280},{28,28... | collective-permute-start | bytes 196616 | tf_op jit(solution)/shard_map/ppermute | solution.py:73
  87.8 6.7 %collective-permute-start.10 = (bf16[64,512]{1,0:T(8,128)(2,1)S(1)}, bf16[64,512]{1,0:T(8,128)(2,1)S(1)}, u32[]{:S(2)}, u32[]{:S(2)}) collective-permute-start(bf16[64,512]{1,0:T(8,128)(2,1)S(1)} %get-tuple-element.77), channel_id=1, source_target_pairs={{0,508},{4,0},{8,4},{12,8},{16,12},{20,16},{24,20},{28,24},{32,28}... | collective-permute-start | bytes 196616 | tf_op jit(solution)/shard_map/ppermute | solution.py:73
  98.1 1.9 %collective-permute-start.12 = (bf16[64,512]{1,0:T(8,128)(2,1)S(1)}, bf16[64,512]{1,0:T(8,128)(2,1)S(1)}, u32[]{:S(2)}, u32[]{:S(2)}) collective-permute-start(bf16[64,512]{1,0:T(8,128)(2,1)S(1)} %get-tuple-element.72), channel_id=1, source_target_pairs={{0,4},{4,8},{8,12},{12,16},{16,20},{20,24},{24,28},{28,32},{32,36}... | collective-permute-start | bytes 196616 | tf_op jit(solution)/shard_map/ppermute | solution.py:73
  100.1 7.0 %collective-permute-start.14 = (bf16[64,512]{1,0:T(8,128)(2,1)S(1)}, bf16[64,512]{1,0:T(8,128)(2,1)S(1)}, u32[]{:S(2)}, u32[]{:S(2)}) collective-permute-start(bf16[64,512]{1,0:T(8,128)(2,1)S(1)} %get-tuple-element.73), channel_id=1, source_target_pairs={{0,256},{4,260},{8,264},{12,268},{16,272},{20,276},{24,280},{28,28... | collective-permute-start | bytes 196616 | tf_op jit(solution)/shard_map/ppermute | solution.py:73
  107.0 6.7 %collective-permute-start.13 = (bf16[64,512]{1,0:T(8,128)(2,1)S(1)}, bf16[64,512]{1,0:T(8,128)(2,1)S(1)}, u32[]{:S(2)}, u32[]{:S(2)}) collective-permute-start(bf16[64,512]{1,0:T(8,128)(2,1)S(1)} %get-tuple-element.74), channel_id=1, source_target_pairs={{0,508},{4,0},{8,4},{12,8},{16,12},{20,16},{24,20},{28,24},{32,28}... | collective-permute-start | bytes 196616 | tf_op jit(solution)/shard_map/ppermute | solution.py:73
  114.0 1.7 %collective-permute-done.13 = bf16[64,512]{1,0:T(8,128)(2,1)S(1)} collective-permute-done((bf16[64,512]{1,0:T(8,128)(2,1)S(1)}, bf16[64,512]{1,0:T(8,128)(2,1)S(1)}, u32[]{:S(2)}, u32[]{:S(2)}) %collective-permute-start.13) | collective-permute-done | bytes 65568 | tf_op jit(solution)/shard_map/ppermute | solution.py:73
  116.3 1.9 %collective-permute-start.15 = (bf16[64,512]{1,0:T(8,128)(2,1)S(1)}, bf16[64,512]{1,0:T(8,128)(2,1)S(1)}, u32[]{:S(2)}, u32[]{:S(2)}) collective-permute-start(bf16[64,512]{1,0:T(8,128)(2,1)S(1)} %get-tuple-element.69), channel_id=1, source_target_pairs={{0,4},{4,8},{8,12},{12,16},{16,20},{20,24},{24,28},{28,32},{32,36}... | collective-permute-start | bytes 196616 | tf_op jit(solution)/shard_map/ppermute | solution.py:73
  118.3 2.8 %collective-permute-start.17 = (bf16[64,512]{1,0:T(8,128)(2,1)S(1)}, bf16[64,512]{1,0:T(8,128)(2,1)S(1)}, u32[]{:S(2)}, u32[]{:S(2)}) collective-permute-start(bf16[64,512]{1,0:T(8,128)(2,1)S(1)} %get-tuple-element.70), channel_id=1, source_target_pairs={{0,256},{4,260},{8,264},{12,268},{16,272},{20,276},{24,280},{28,28... | collective-permute-start | bytes 196616 | tf_op jit(solution)/shard_map/ppermute | solution.py:73
  121.1 6.7 %collective-permute-start.16 = (bf16[64,512]{1,0:T(8,128)(2,1)S(1)}, bf16[64,512]{1,0:T(8,128)(2,1)S(1)}, u32[]{:S(2)}, u32[]{:S(2)}) collective-permute-start(bf16[64,512]{1,0:T(8,128)(2,1)S(1)} %get-tuple-element.71), channel_id=1, source_target_pairs={{0,508},{4,0},{8,4},{12,8},{16,12},{20,16},{24,20},{28,24},{32,28}... | collective-permute-start | bytes 196616 | tf_op jit(solution)/shard_map/ppermute | solution.py:73
  (108 shorter events, 22.1 us)
Async XLA Ops:
  7.2 53.2 %copy-start.1 = (f32[8,1,64,128]{3,2,1,0:T(8,128)S(1)}, f32[8,1,64,128]{3,2,1,0:T(8,128)}, u32[]{:S(2)}) copy-start(f32[8,1,64,128]{3,2,1,0:T(8,128)} %param.7) | copy-start | bytes 786436
  7.2 15.1 %copy-start.5 = (s32[3]{0:T(128)S(1)}, s32[3]{0:T(128)}, u32[]{:S(2)}) copy-start(s32[3]{0:T(128)} %param.11) | copy-start | bytes 40
  7.2 26.9 %copy-start.2 = (s32[3]{0:T(128)S(1)}, s32[3]{0:T(128)}, u32[]{:S(2)}) copy-start(s32[3]{0:T(128)} %param.10) | copy-start | bytes 40
  7.2 32.6 %copy-start.6 = (s32[3]{0:T(128)S(1)}, s32[3]{0:T(128)}, u32[]{:S(2)}) copy-start(s32[3]{0:T(128)} %param.13) | copy-start | bytes 40
  7.2 73.7 %all-gather.2.cloned.1.call-start = ((), (), s32[]{:S(2)}) async-start(), calls=%async_computation | async-start | bytes 1966080 | tf_op jit(solution)/shard_map/all_gather | solution.py:39
  9.2 51.2 %collective-permute-start.2 = (f32[2,8,64,128]{3,2,1,0:T(8,128)S(1)}, f32[2,8,64,128]{3,2,1,0:T(8,128)S(1)}, u32[]{:S(2)}, u32[]{:S(2)}) collective-permute-start(f32[2,8,64,128]{3,2,1,0:T(8,128)S(1)} %pad_maximum_fusion.2), channel_id=1, source_target_pairs={{1,0},{2,1},{3,2},{0,3},{5,4},{6,5},{7,6},{4,7},{9,8},{10,9},{11,1... | collective-permute-start | bytes 1572872 | tf_op jit(solution)/shard_map/ppermute | solution.py:43
  11.9 48.5 %collective-permute-start.1 = (f32[2,8,64,128]{3,2,1,0:T(8,128)S(1)}, f32[2,8,64,128]{3,2,1,0:T(8,128)S(1)}, u32[]{:S(2)}, u32[]{:S(2)}) collective-permute-start(f32[2,8,64,128]{3,2,1,0:T(8,128)S(1)} %pad_maximum_fusion.2), channel_id=1, source_target_pairs={{2,0},{3,1},{0,2},{1,3},{6,4},{7,5},{4,6},{5,7},{10,8},{11,9},{8,1... | collective-permute-start | bytes 1572872 | tf_op jit(solution)/shard_map/ppermute | solution.py:43
  20.3 40.2 %collective-permute-start = (f32[2,8,64,128]{3,2,1,0:T(8,128)S(1)}, f32[2,8,64,128]{3,2,1,0:T(8,128)S(1)}, u32[]{:S(2)}, u32[]{:S(2)}) collective-permute-start(f32[2,8,64,128]{3,2,1,0:T(8,128)S(1)} %pad_maximum_fusion.2), channel_id=1, source_target_pairs={{3,0},{0,1},{1,2},{2,3},{7,4},{4,5},{5,6},{6,7},{11,8},{8,9},{9,10... | collective-permute-start | bytes 1572872 | tf_op jit(solution)/shard_map/ppermute | solution.py:43
  22.9 19.3 %collective-permute-start.3 = (s32[]{:T(128)}, s32[]{:T(128)}, u32[]{:S(2)}, u32[]{:S(2)}) collective-permute-start(s32[]{:T(128)} %bitcast.7), channel_id=1, source_target_pairs={{0,508},{4,0},{8,4},{12,8},{16,12},{20,16},{24,20},{28,24},{32,28}... | collective-permute-start | bytes 20 | tf_op jit(solution)/shard_map/ppermute | solution.py:35
  32.1 12.0 %collective-permute-start.5 = (s32[]{:T(128)}, s32[]{:T(128)}, u32[]{:S(2)}, u32[]{:S(2)}) collective-permute-start(s32[]{:T(128)} %bitcast.11), channel_id=1, source_target_pairs={{0,256},{4,260},{8,264},{12,268},{16,272},{20,276},{24,280},{28,28... | collective-permute-start | bytes 20 | tf_op jit(solution)/shard_map/ppermute | solution.py:35
  42.2 8.4 %collective-permute-start.4 = (s32[]{:T(128)}, s32[]{:T(128)}, u32[]{:S(2)}, u32[]{:S(2)}) collective-permute-start(s32[]{:T(128)} %bitcast.9), channel_id=1, source_target_pairs={{0,4},{4,8},{8,12},{12,16},{16,20},{20,24},{24,28},{28,32},{32,36}... | collective-permute-start | bytes 20 | tf_op jit(solution)/shard_map/ppermute | solution.py:35
  62.2 17.3 %collective-permute-start.7 = (bf16[64,512]{1,0:T(8,128)(2,1)S(1)}, bf16[64,512]{1,0:T(8,128)(2,1)S(1)}, u32[]{:S(2)}, u32[]{:S(2)}) collective-permute-start(bf16[64,512]{1,0:T(8,128)(2,1)S(1)} %bitcast.250), channel_id=1, source_target_pairs={{0,508},{4,0},{8,4},{12,8},{16,12},{20,16},{24,20},{28,24},{32,28}... | collective-permute-start | bytes 196616 | tf_op jit(solution)/shard_map/ppermute | solution.py:73
  64.1 15.3 %collective-permute-start.8 = (bf16[64,512]{1,0:T(8,128)(2,1)S(1)}, bf16[64,512]{1,0:T(8,128)(2,1)S(1)}, u32[]{:S(2)}, u32[]{:S(2)}) collective-permute-start(bf16[64,512]{1,0:T(8,128)(2,1)S(1)} %bitcast.249), channel_id=1, source_target_pairs={{0,256},{4,260},{8,264},{12,268},{16,272},{20,276},{24,280},{28,28... | collective-permute-start | bytes 196616 | tf_op jit(solution)/shard_map/ppermute | solution.py:73
  72.0 8.9 %collective-permute-start.6 = (bf16[64,512]{1,0:T(8,128)(2,1)S(1)}, bf16[64,512]{1,0:T(8,128)(2,1)S(1)}, u32[]{:S(2)}, u32[]{:S(2)}) collective-permute-start(bf16[64,512]{1,0:T(8,128)(2,1)S(1)} %bitcast.248), channel_id=1, source_target_pairs={{0,4},{4,8},{8,12},{12,16},{16,20},{20,24},{24,28},{28,32},{32,36}... | collective-permute-start | bytes 196616 | tf_op jit(solution)/shard_map/ppermute | solution.py:73
  82.7 13.8 %copy-start = (bf16[3,4,128,512]{3,2,1,0:T(8,128)(2,1)S(1)}, bf16[3,4,128,512]{3,2,1,0:T(8,128)(2,1)}, u32[]{:S(2)}) copy-start(bf16[3,4,128,512]{3,2,1,0:T(8,128)(2,1)} %all-gather.2.cloned.1.call-done) | copy-start | bytes 4718596
  83.0 11.6 %collective-permute-start.9 = (bf16[64,512]{1,0:T(8,128)(2,1)S(1)}, bf16[64,512]{1,0:T(8,128)(2,1)S(1)}, u32[]{:S(2)}, u32[]{:S(2)}) collective-permute-start(bf16[64,512]{1,0:T(8,128)(2,1)S(1)} %get-tuple-element.75), channel_id=1, source_target_pairs={{0,4},{4,8},{8,12},{12,16},{16,20},{20,24},{24,28},{28,32},{32,36}... | collective-permute-start | bytes 196616 | tf_op jit(solution)/shard_map/ppermute | solution.py:73
  85.0 10.1 %collective-permute-start.11 = (bf16[64,512]{1,0:T(8,128)(2,1)S(1)}, bf16[64,512]{1,0:T(8,128)(2,1)S(1)}, u32[]{:S(2)}, u32[]{:S(2)}) collective-permute-start(bf16[64,512]{1,0:T(8,128)(2,1)S(1)} %get-tuple-element.76), channel_id=1, source_target_pairs={{0,256},{4,260},{8,264},{12,268},{16,272},{20,276},{24,280},{28,28... | collective-permute-start | bytes 196616 | tf_op jit(solution)/shard_map/ppermute | solution.py:73
  87.8 8.6 %collective-permute-start.10 = (bf16[64,512]{1,0:T(8,128)(2,1)S(1)}, bf16[64,512]{1,0:T(8,128)(2,1)S(1)}, u32[]{:S(2)}, u32[]{:S(2)}) collective-permute-start(bf16[64,512]{1,0:T(8,128)(2,1)S(1)} %get-tuple-element.77), channel_id=1, source_target_pairs={{0,508},{4,0},{8,4},{12,8},{16,12},{20,16},{24,20},{28,24},{32,28}... | collective-permute-start | bytes 196616 | tf_op jit(solution)/shard_map/ppermute | solution.py:73
  98.1 15.8 %collective-permute-start.12 = (bf16[64,512]{1,0:T(8,128)(2,1)S(1)}, bf16[64,512]{1,0:T(8,128)(2,1)S(1)}, u32[]{:S(2)}, u32[]{:S(2)}) collective-permute-start(bf16[64,512]{1,0:T(8,128)(2,1)S(1)} %get-tuple-element.72), channel_id=1, source_target_pairs={{0,4},{4,8},{8,12},{12,16},{16,20},{20,24},{24,28},{28,32},{32,36}... | collective-permute-start | bytes 196616 | tf_op jit(solution)/shard_map/ppermute | solution.py:73
  100.1 13.9 %collective-permute-start.14 = (bf16[64,512]{1,0:T(8,128)(2,1)S(1)}, bf16[64,512]{1,0:T(8,128)(2,1)S(1)}, u32[]{:S(2)}, u32[]{:S(2)}) collective-permute-start(bf16[64,512]{1,0:T(8,128)(2,1)S(1)} %get-tuple-element.73), channel_id=1, source_target_pairs={{0,256},{4,260},{8,264},{12,268},{16,272},{20,276},{24,280},{28,28... | collective-permute-start | bytes 196616 | tf_op jit(solution)/shard_map/ppermute | solution.py:73
  107.0 8.6 %collective-permute-start.13 = (bf16[64,512]{1,0:T(8,128)(2,1)S(1)}, bf16[64,512]{1,0:T(8,128)(2,1)S(1)}, u32[]{:S(2)}, u32[]{:S(2)}) collective-permute-start(bf16[64,512]{1,0:T(8,128)(2,1)S(1)} %get-tuple-element.74), channel_id=1, source_target_pairs={{0,508},{4,0},{8,4},{12,8},{16,12},{20,16},{24,20},{28,24},{32,28}... | collective-permute-start | bytes 196616 | tf_op jit(solution)/shard_map/ppermute | solution.py:73
  116.3 11.5 %collective-permute-start.15 = (bf16[64,512]{1,0:T(8,128)(2,1)S(1)}, bf16[64,512]{1,0:T(8,128)(2,1)S(1)}, u32[]{:S(2)}, u32[]{:S(2)}) collective-permute-start(bf16[64,512]{1,0:T(8,128)(2,1)S(1)} %get-tuple-element.69), channel_id=1, source_target_pairs={{0,4},{4,8},{8,12},{12,16},{16,20},{20,24},{24,28},{28,32},{32,36}... | collective-permute-start | bytes 196616 | tf_op jit(solution)/shard_map/ppermute | solution.py:73
  118.3 10.1 %collective-permute-start.17 = (bf16[64,512]{1,0:T(8,128)(2,1)S(1)}, bf16[64,512]{1,0:T(8,128)(2,1)S(1)}, u32[]{:S(2)}, u32[]{:S(2)}) collective-permute-start(bf16[64,512]{1,0:T(8,128)(2,1)S(1)} %get-tuple-element.70), channel_id=1, source_target_pairs={{0,256},{4,260},{8,264},{12,268},{16,272},{20,276},{24,280},{28,28... | collective-permute-start | bytes 196616 | tf_op jit(solution)/shard_map/ppermute | solution.py:73
  121.1 8.6 %collective-permute-start.16 = (bf16[64,512]{1,0:T(8,128)(2,1)S(1)}, bf16[64,512]{1,0:T(8,128)(2,1)S(1)}, u32[]{:S(2)}, u32[]{:S(2)}) collective-permute-start(bf16[64,512]{1,0:T(8,128)(2,1)S(1)} %get-tuple-element.71), channel_id=1, source_target_pairs={{0,508},{4,0},{8,4},{12,8},{16,12},{20,16},{24,20},{28,24},{32,28}... | collective-permute-start | bytes 196616 | tf_op jit(solution)/shard_map/ppermute | solution.py:73
  (3 other events, 1.9 us)
Sparse Core Ops, SparseCore 0:
  22.4 31.8 all-gather.1

commit v9 on v8

--- a/solution.py
+++ b/solution.py
@@ -34,16 +34,14 @@
         perm = [(i, (i + offsets[k]) % n_areas) for i in range(n_areas)]
         provide.append(lax.ppermute(wanted[k], "area", perm))
     provide = jnp.stack(provide)
-    select_provided = jnp.take(select, provide, axis=1)
+    select_provided = ((slot_dst[:, None] == provide[None, :]) & occupied[:, None]).astype(jnp.float32)
 
-    w_full = lax.all_gather(weights[:, 0], "blk", axis=1, tiled=False)
-    w_full = w_full.reshape(slot_cap, sub_width, sub_width)
     own_state = jnp.stack([activity[:, 0], ext_input[:, 0].astype(jnp.float32)])
     by_shift = [own_state] + [
         lax.ppermute(own_state, "blk", [((b + s) % n_blk, b) for b in range(n_blk)]) for s in range(1, n_blk)
     ]
 
-    def in_part_order(pieces):
+    def in_part_order(pieces, axis=-2):
         ordered = []
         for j in range(n_blk):
             shift_j = (j - my_blk) % n_blk
@@ -51,7 +49,13 @@
             for s in range(1, n_blk):
                 out = jnp.where(shift_j == s, pieces[s], out)
             ordered.append(out)
-        return jnp.stack(ordered, axis=-2)
+        return jnp.stack(ordered, axis=axis)
+
+    own_w = weights[:, 0]
+    w_pieces = [own_w] + [
+        lax.ppermute(own_w, "blk", [((b + s) % n_blk, b) for b in range(n_blk)]) for s in range(1, n_blk)
+    ]
+    w_full = in_part_order(w_pieces, axis=1).reshape(slot_cap, sub_width, sub_width)
 
     def pick(x, idx):
         return jnp.stack([lax.dynamic_index_in_dim(x, idx[k], 0, keepdims=False) for k in range(slot_cap)])

time: 142 us -> 153 us (1.077); the launches traced: 140 us -> 150 us
  between operations: 26.2 us -> 13.2 us
  starting transfers between devices: 76.6 us -> 87.1 us
  waiting for transfers between devices: 13.3 us -> 19.2 us
  local copies, waits for them, and re-layouts: 9.24 us -> 15.1 us
    ppermute x0 -> x3, starting transfers between devices: none -> 13.2 us  [body(): lax.ppermute(own_w, 'blk', [((b + s) % n_blk, b) for b in range(n_blk)])]
    ppermute x3, waiting for transfers between devices: 0.01 us -> 9.63 us  [body(): lax.ppermute(own_state, 'blk', [((b + s) % n_blk, b) for b in range(n_blk)])]
    ppermute x3, starting transfers between devices: 13 us -> 9.08 us  [body(): lax.ppermute(own_state, 'blk', [((b + s) % n_blk, b) for b in range(n_blk)])]
    another operation x3 -> x6, other arithmetic: 0.62 us -> 2.93 us  [the longest x1 1.88 us: body(): provide = jnp.stack(provide)]
    ppermute x3, waiting for transfers between devices: 6.44 us -> 4.17 us  [body(): provide.append(lax.ppermute(wanted[k], 'area', perm))]
    select_n x2 -> x0, other arithmetic: 1.92 us -> none  [body(): select_provided = jnp.take(select, provide, axis=1)]
    and x1 -> x0, other arithmetic: 1.85 us -> none  [body(): select_provided = jnp.take(select, provide, axis=1)]
  transfers between devices with their start and end apart: 19 -> 21, of which waited for: 7 -> 8; matrix products, arithmetic and copies ran while one was open for 10% -> 14% of each run, Pallas kernels for 0% -> 0%
where the time goes in v9:
time: 153 us; the launch traced here: 150 us
  starting transfers between devices  87.1 us (57%)
  waiting for transfers between devices  19.2 us (13%)
  local copies, waits for them, and re-layouts  15.1 us (10%)
  between operations  13.2 us (9%)
  other arithmetic  12.4 us (8%)
  matrix products  2.68 us (2%)
    ppermute x12, starting transfers between devices, exchange(): got.append(lax.ppermute(payload[k], 'area', perm))  51.9 us
    ppermute x3, starting transfers between devices, body(): lax.ppermute(own_w, 'blk', [((b + s) % n_blk, b) for b in range(n_blk)])  13.2 us
    ppermute x3, starting transfers between devices, body(): provide.append(lax.ppermute(wanted[k], 'area', perm))  13 us
    ppermute x3, waiting for transfers between devices, body(): lax.ppermute(own_state, 'blk', [((b + s) % n_blk, b) for b in range(n_blk)])  9.63 us
    ppermute x3, starting transfers between devices, body(): lax.ppermute(own_state, 'blk', [((b + s) % n_blk, b) for b in range(n_blk)])  9.08 us
    ppermute x12, waiting for transfers between devices, exchange(): got.append(lax.ppermute(payload[k], 'area', perm))  5.4 us
    ppermute x3, waiting for transfers between devices, body(): provide.append(lax.ppermute(wanted[k], 'area', perm))  4.17 us
  transfers between devices with their start and end apart: 21, of which 8 were waited for; matrix products, arithmetic and copies ran while one was open for 14% of the time, Pallas kernels for 0%

profile of v9, /device:TPU:6, one launch (start us, length us, event | category | flops | bytes accessed | tf_op | source)
XLA Modules:
  0.0 149.7 jit_solution(10301318583731109687)
XLA Ops:
  0.7 2.9 %collective-permute-start.11 = (bf16[3,128,512]{2,1,0:T(8,128)(2,1)}, bf16[3,128,512]{2,1,0:T(8,128)(2,1)S(1)}, u32[]{:S(2)}, u32[]{:S(2)}) collective-permute-start(bf16[3,128,512]{2,1,0:T(8,128)(2,1)} %bitcast.239), channel_id=1, source_target_pairs={{1,0},{2,1},{3,2},{0,3},{5,4},{6,5},{7,6},{4,7},{9,8},{10,9},{11,1... | collective-permute-start | bytes 1179656 | tf_op jit(solution)/shard_map/ppermute | solution.py:56
  3.5 8.4 %collective-permute-start.10 = (bf16[3,128,512]{2,1,0:T(8,128)(2,1)}, bf16[3,128,512]{2,1,0:T(8,128)(2,1)S(1)}, u32[]{:S(2)}, u32[]{:S(2)}) collective-permute-start(bf16[3,128,512]{2,1,0:T(8,128)(2,1)} %bitcast.240), channel_id=1, source_target_pairs={{2,0},{3,1},{0,2},{1,3},{6,4},{7,5},{4,6},{5,7},{10,8},{11,9},{8,1... | collective-permute-start | bytes 1179656 | tf_op jit(solution)/shard_map/ppermute | solution.py:56
  11.9 1.9 %collective-permute-start.9 = (bf16[3,128,512]{2,1,0:T(8,128)(2,1)}, bf16[3,128,512]{2,1,0:T(8,128)(2,1)S(1)}, u32[]{:S(2)}, u32[]{:S(2)}) collective-permute-start(bf16[3,128,512]{2,1,0:T(8,128)(2,1)} %bitcast.241), channel_id=1, source_target_pairs={{3,0},{0,1},{1,2},{2,3},{7,4},{4,5},{5,6},{6,7},{11,8},{8,9},{9,10... | collective-permute-start | bytes 1179656 | tf_op jit(solution)/shard_map/ppermute | solution.py:56
  15.1 9.2 %collective-permute-start.3 = (s32[]{:T(128)}, s32[]{:T(128)}, u32[]{:S(2)}, u32[]{:S(2)}) collective-permute-start(s32[]{:T(128)} %bitcast.8), channel_id=1, source_target_pairs={{0,508},{4,0},{8,4},{12,8},{16,12},{20,16},{24,20},{28,24},{32,28}... | collective-permute-start | bytes 20 | tf_op jit(solution)/shard_map/ppermute | solution.py:35
  24.3 1.9 %collective-permute-start.5 = (s32[]{:T(128)}, s32[]{:T(128)}, u32[]{:S(2)}, u32[]{:S(2)}) collective-permute-start(s32[]{:T(128)} %bitcast.12), channel_id=1, source_target_pairs={{0,256},{4,260},{8,264},{12,268},{16,272},{20,276},{24,280},{28,28... | collective-permute-start | bytes 20 | tf_op jit(solution)/shard_map/ppermute | solution.py:35
  41.2 2.3 %collective-permute-start.2 = (f32[2,8,64,128]{3,2,1,0:T(8,128)}, f32[2,8,64,128]{3,2,1,0:T(8,128)S(1)}, u32[]{:S(2)}, u32[]{:S(2)}) collective-permute-start(f32[2,8,64,128]{3,2,1,0:T(8,128)} %pad_maximum_fusion.3), channel_id=1, source_target_pairs={{1,0},{2,1},{3,2},{0,3},{5,4},{6,5},{7,6},{4,7},{9,8},{10,9},{11,1... | collective-permute-start | bytes 1572872 | tf_op jit(solution)/shard_map/ppermute | solution.py:41
  43.4 4.2 %collective-permute-done.4 = s32[]{:T(128)} collective-permute-done((s32[]{:T(128)}, s32[]{:T(128)}, u32[]{:S(2)}, u32[]{:S(2)}) %collective-permute-start.4) | collective-permute-done | bytes 36 | tf_op jit(solution)/shard_map/ppermute | solution.py:35
  47.6 4.0 %collective-permute-start.1 = (f32[2,8,64,128]{3,2,1,0:T(8,128)}, f32[2,8,64,128]{3,2,1,0:T(8,128)S(1)}, u32[]{:S(2)}, u32[]{:S(2)}) collective-permute-start(f32[2,8,64,128]{3,2,1,0:T(8,128)} %pad_maximum_fusion.3), channel_id=1, source_target_pairs={{2,0},{3,1},{0,2},{1,3},{6,4},{7,5},{4,6},{5,7},{10,8},{11,9},{8,1... | collective-permute-start | bytes 1572872 | tf_op jit(solution)/shard_map/ppermute | solution.py:41
  59.1 2.8 %collective-permute-start = (f32[2,8,64,128]{3,2,1,0:T(8,128)}, f32[2,8,64,128]{3,2,1,0:T(8,128)S(1)}, u32[]{:S(2)}, u32[]{:S(2)}) collective-permute-start(f32[2,8,64,128]{3,2,1,0:T(8,128)} %pad_maximum_fusion.3), channel_id=1, source_target_pairs={{3,0},{0,1},{1,2},{2,3},{7,4},{4,5},{5,6},{6,7},{11,8},{8,9},{9,10... | collective-permute-start | bytes 1572872 | tf_op jit(solution)/shard_map/ppermute | solution.py:41
  62.5 7.2 %collective-permute-done.2 = f32[2,8,64,128]{3,2,1,0:T(8,128)S(1)} collective-permute-done((f32[2,8,64,128]{3,2,1,0:T(8,128)}, f32[2,8,64,128]{3,2,1,0:T(8,128)S(1)}, u32[]{:S(2)}, u32[]{:S(2)}) %collective-permute-start.2) | collective-permute-done | bytes 524320 | tf_op jit(solution)/shard_map/ppermute | solution.py:41
  69.8 2.4 %collective-permute-done = f32[2,8,64,128]{3,2,1,0:T(8,128)S(1)} collective-permute-done((f32[2,8,64,128]{3,2,1,0:T(8,128)}, f32[2,8,64,128]{3,2,1,0:T(8,128)S(1)}, u32[]{:S(2)}, u32[]{:S(2)}) %collective-permute-start) | collective-permute-done | bytes 524320 | tf_op jit(solution)/shard_map/ppermute | solution.py:41
  73.9 4.3 %collective-permute-start.7 = (bf16[64,512]{1,0:T(8,128)(2,1)S(1)}, bf16[64,512]{1,0:T(8,128)(2,1)S(1)}, u32[]{:S(2)}, u32[]{:S(2)}) collective-permute-start(bf16[64,512]{1,0:T(8,128)(2,1)S(1)} %bitcast.271), channel_id=1, source_target_pairs={{0,508},{4,0},{8,4},{12,8},{16,12},{20,16},{24,20},{28,24},{32,28}... | collective-permute-start | bytes 196616 | tf_op jit(solution)/shard_map/ppermute | solution.py:77
  78.2 7.5 %collective-permute-start.8 = (bf16[64,512]{1,0:T(8,128)(2,1)S(1)}, bf16[64,512]{1,0:T(8,128)(2,1)S(1)}, u32[]{:S(2)}, u32[]{:S(2)}) collective-permute-start(bf16[64,512]{1,0:T(8,128)(2,1)S(1)} %bitcast.270), channel_id=1, source_target_pairs={{0,256},{4,260},{8,264},{12,268},{16,272},{20,276},{24,280},{28,28... | collective-permute-start | bytes 196616 | tf_op jit(solution)/shard_map/ppermute | solution.py:77
  85.8 1.9 %collective-permute-start.6 = (bf16[64,512]{1,0:T(8,128)(2,1)S(1)}, bf16[64,512]{1,0:T(8,128)(2,1)S(1)}, u32[]{:S(2)}, u32[]{:S(2)}) collective-permute-start(bf16[64,512]{1,0:T(8,128)(2,1)S(1)} %bitcast.269), channel_id=1, source_target_pairs={{0,4},{4,8},{8,12},{12,16},{16,20},{20,24},{24,28},{28,32},{32,36}... | collective-permute-start | bytes 196616 | tf_op jit(solution)/shard_map/ppermute | solution.py:77
  93.9 2.9 %copy.11 = f32[1,8,64,4,128]{4,3,2,1,0:T(4,128)} copy(f32[1,8,64,4,128]{4,2,1,0,3:T(8,128)} %get-tuple-element.9) | data formatting | bytes 2097152 | tf_op jit(solution)/shard_map/slice | solution.py:65
  99.1 1.9 %collective-permute-start.12 = (bf16[64,512]{1,0:T(8,128)(2,1)S(1)}, bf16[64,512]{1,0:T(8,128)(2,1)S(1)}, u32[]{:S(2)}, u32[]{:S(2)}) collective-permute-start(bf16[64,512]{1,0:T(8,128)(2,1)S(1)} %get-tuple-element.71), channel_id=1, source_target_pairs={{0,4},{4,8},{8,12},{12,16},{16,20},{20,24},{24,28},{28,32},{32,36}... | collective-permute-start | bytes 196616 | tf_op jit(solution)/shard_map/ppermute | solution.py:77
  101.1 2.2 %collective-permute-start.14 = (bf16[64,512]{1,0:T(8,128)(2,1)S(1)}, bf16[64,512]{1,0:T(8,128)(2,1)S(1)}, u32[]{:S(2)}, u32[]{:S(2)}) collective-permute-start(bf16[64,512]{1,0:T(8,128)(2,1)S(1)} %get-tuple-element.72), channel_id=1, source_target_pairs={{0,256},{4,260},{8,264},{12,268},{16,272},{20,276},{24,280},{28,28... | collective-permute-start | bytes 196616 | tf_op jit(solution)/shard_map/ppermute | solution.py:77
  103.3 6.7 %collective-permute-start.13 = (bf16[64,512]{1,0:T(8,128)(2,1)S(1)}, bf16[64,512]{1,0:T(8,128)(2,1)S(1)}, u32[]{:S(2)}, u32[]{:S(2)}) collective-permute-start(bf16[64,512]{1,0:T(8,128)(2,1)S(1)} %get-tuple-element.73), channel_id=1, source_target_pairs={{0,508},{4,0},{8,4},{12,8},{16,12},{20,16},{24,20},{28,24},{32,28}... | collective-permute-start | bytes 196616 | tf_op jit(solution)/shard_map/ppermute | solution.py:77
  114.2 1.9 %collective-permute-start.15 = (bf16[64,512]{1,0:T(8,128)(2,1)S(1)}, bf16[64,512]{1,0:T(8,128)(2,1)S(1)}, u32[]{:S(2)}, u32[]{:S(2)}) collective-permute-start(bf16[64,512]{1,0:T(8,128)(2,1)S(1)} %get-tuple-element.68), channel_id=1, source_target_pairs={{0,4},{4,8},{8,12},{12,16},{16,20},{20,24},{24,28},{28,32},{32,36}... | collective-permute-start | bytes 196616 | tf_op jit(solution)/shard_map/ppermute | solution.py:77
  116.1 7.5 %collective-permute-start.17 = (bf16[64,512]{1,0:T(8,128)(2,1)S(1)}, bf16[64,512]{1,0:T(8,128)(2,1)S(1)}, u32[]{:S(2)}, u32[]{:S(2)}) collective-permute-start(bf16[64,512]{1,0:T(8,128)(2,1)S(1)} %get-tuple-element.69), channel_id=1, source_target_pairs={{0,256},{4,260},{8,264},{12,268},{16,272},{20,276},{24,280},{28,28... | collective-permute-start | bytes 196616 | tf_op jit(solution)/shard_map/ppermute | solution.py:77
  123.7 6.7 %collective-permute-start.16 = (bf16[64,512]{1,0:T(8,128)(2,1)S(1)}, bf16[64,512]{1,0:T(8,128)(2,1)S(1)}, u32[]{:S(2)}, u32[]{:S(2)}) collective-permute-start(bf16[64,512]{1,0:T(8,128)(2,1)S(1)} %get-tuple-element.70), channel_id=1, source_target_pairs={{0,508},{4,0},{8,4},{12,8},{16,12},{20,16},{24,20},{28,24},{32,28}... | collective-permute-start | bytes 196616 | tf_op jit(solution)/shard_map/ppermute | solution.py:77
  133.0 1.9 %collective-permute-start.18 = (bf16[64,512]{1,0:T(8,128)(2,1)S(1)}, bf16[64,512]{1,0:T(8,128)(2,1)S(1)}, u32[]{:S(2)}, u32[]{:S(2)}) collective-permute-start(bf16[64,512]{1,0:T(8,128)(2,1)S(1)} %get-tuple-element.65), channel_id=1, source_target_pairs={{0,4},{4,8},{8,12},{12,16},{16,20},{20,24},{24,28},{28,32},{32,36}... | collective-permute-start | bytes 196616 | tf_op jit(solution)/shard_map/ppermute | solution.py:77
  134.9 2.2 %collective-permute-start.20 = (bf16[64,512]{1,0:T(8,128)(2,1)S(1)}, bf16[64,512]{1,0:T(8,128)(2,1)S(1)}, u32[]{:S(2)}, u32[]{:S(2)}) collective-permute-start(bf16[64,512]{1,0:T(8,128)(2,1)S(1)} %get-tuple-element.66), channel_id=1, source_target_pairs={{0,256},{4,260},{8,264},{12,268},{16,272},{20,276},{24,280},{28,28... | collective-permute-start | bytes 196616 | tf_op jit(solution)/shard_map/ppermute | solution.py:77
  137.1 6.9 %collective-permute-start.19 = (bf16[64,512]{1,0:T(8,128)(2,1)S(1)}, bf16[64,512]{1,0:T(8,128)(2,1)S(1)}, u32[]{:S(2)}, u32[]{:S(2)}) collective-permute-start(bf16[64,512]{1,0:T(8,128)(2,1)S(1)} %get-tuple-element.67), channel_id=1, source_target_pairs={{0,508},{4,0},{8,4},{12,8},{16,12},{20,16},{24,20},{28,24},{32,28}... | collective-permute-start | bytes 196616 | tf_op jit(solution)/shard_map/ppermute | solution.py:77
  (111 shorter events, 34.6 us)
Async XLA Ops:
  0.6 61.3 %copy-start.3 = (bf16[3,1,128,512]{3,2,1,0:T(8,128)(2,1)S(1)}, bf16[3,1,128,512]{3,2,1,0:T(8,128)(2,1)}, u32[]{:S(2)}) copy-start(bf16[3,1,128,512]{3,2,1,0:T(8,128)(2,1)} %param.9) | copy-start | bytes 1179652
  0.6 52.9 %copy-start.4 = (s32[3]{0:T(128)S(1)}, s32[3]{0:T(128)}, u32[]{:S(2)}) copy-start(s32[3]{0:T(128)} %param.10) | copy-start | bytes 40
  0.7 58.4 %copy-start.2 = (f32[8,1,64,128]{3,2,1,0:T(8,128)S(1)}, f32[8,1,64,128]{3,2,1,0:T(8,128)}, u32[]{:S(2)}) copy-start(f32[8,1,64,128]{3,2,1,0:T(8,128)} %param.7) | copy-start | bytes 786436
  0.7 58.4 %collective-permute-start.11 = (bf16[3,128,512]{2,1,0:T(8,128)(2,1)}, bf16[3,128,512]{2,1,0:T(8,128)(2,1)S(1)}, u32[]{:S(2)}, u32[]{:S(2)}) collective-permute-start(bf16[3,128,512]{2,1,0:T(8,128)(2,1)} %bitcast.239), channel_id=1, source_target_pairs={{1,0},{2,1},{3,2},{0,3},{5,4},{6,5},{7,6},{4,7},{9,8},{10,9},{11,1... | collective-permute-start | bytes 1179656 | tf_op jit(solution)/shard_map/ppermute | solution.py:56
  3.5 58.4 %collective-permute-start.10 = (bf16[3,128,512]{2,1,0:T(8,128)(2,1)}, bf16[3,128,512]{2,1,0:T(8,128)(2,1)S(1)}, u32[]{:S(2)}, u32[]{:S(2)}) collective-permute-start(bf16[3,128,512]{2,1,0:T(8,128)(2,1)} %bitcast.240), channel_id=1, source_target_pairs={{2,0},{3,1},{0,2},{1,3},{6,4},{7,5},{4,6},{5,7},{10,8},{11,9},{8,1... | collective-permute-start | bytes 1179656 | tf_op jit(solution)/shard_map/ppermute | solution.py:56
  11.9 50.0 %collective-permute-start.9 = (bf16[3,128,512]{2,1,0:T(8,128)(2,1)}, bf16[3,128,512]{2,1,0:T(8,128)(2,1)S(1)}, u32[]{:S(2)}, u32[]{:S(2)}) collective-permute-start(bf16[3,128,512]{2,1,0:T(8,128)(2,1)} %bitcast.241), channel_id=1, source_target_pairs={{3,0},{0,1},{1,2},{2,3},{7,4},{4,5},{5,6},{6,7},{11,8},{8,9},{9,10... | collective-permute-start | bytes 1179656 | tf_op jit(solution)/shard_map/ppermute | solution.py:56
  15.1 24.2 %collective-permute-start.3 = (s32[]{:T(128)}, s32[]{:T(128)}, u32[]{:S(2)}, u32[]{:S(2)}) collective-permute-start(s32[]{:T(128)} %bitcast.8), channel_id=1, source_target_pairs={{0,508},{4,0},{8,4},{12,8},{16,12},{20,16},{24,20},{28,24},{32,28}... | collective-permute-start | bytes 20 | tf_op jit(solution)/shard_map/ppermute | solution.py:35
  24.3 16.9 %collective-permute-start.5 = (s32[]{:T(128)}, s32[]{:T(128)}, u32[]{:S(2)}, u32[]{:S(2)}) collective-permute-start(s32[]{:T(128)} %bitcast.12), channel_id=1, source_target_pairs={{0,256},{4,260},{8,264},{12,268},{16,272},{20,276},{24,280},{28,28... | collective-permute-start | bytes 20 | tf_op jit(solution)/shard_map/ppermute | solution.py:35
  39.3 8.4 %collective-permute-start.4 = (s32[]{:T(128)}, s32[]{:T(128)}, u32[]{:S(2)}, u32[]{:S(2)}) collective-permute-start(s32[]{:T(128)} %bitcast.10), channel_id=1, source_target_pairs={{0,4},{4,8},{8,12},{12,16},{16,20},{20,24},{24,28},{28,32},{32,36}... | collective-permute-start | bytes 20 | tf_op jit(solution)/shard_map/ppermute | solution.py:35
  41.2 28.5 %collective-permute-start.2 = (f32[2,8,64,128]{3,2,1,0:T(8,128)}, f32[2,8,64,128]{3,2,1,0:T(8,128)S(1)}, u32[]{:S(2)}, u32[]{:S(2)}) collective-permute-start(f32[2,8,64,128]{3,2,1,0:T(8,128)} %pad_maximum_fusion.3), channel_id=1, source_target_pairs={{1,0},{2,1},{3,2},{0,3},{5,4},{6,5},{7,6},{4,7},{9,8},{10,9},{11,1... | collective-permute-start | bytes 1572872 | tf_op jit(solution)/shard_map/ppermute | solution.py:41
  47.6 22.1 %collective-permute-start.1 = (f32[2,8,64,128]{3,2,1,0:T(8,128)}, f32[2,8,64,128]{3,2,1,0:T(8,128)S(1)}, u32[]{:S(2)}, u32[]{:S(2)}) collective-permute-start(f32[2,8,64,128]{3,2,1,0:T(8,128)} %pad_maximum_fusion.3), channel_id=1, source_target_pairs={{2,0},{3,1},{0,2},{1,3},{6,4},{7,5},{4,6},{5,7},{10,8},{11,9},{8,1... | collective-permute-start | bytes 1572872 | tf_op jit(solution)/shard_map/ppermute | solution.py:41
  59.1 13.1 %collective-permute-start = (f32[2,8,64,128]{3,2,1,0:T(8,128)}, f32[2,8,64,128]{3,2,1,0:T(8,128)S(1)}, u32[]{:S(2)}, u32[]{:S(2)}) collective-permute-start(f32[2,8,64,128]{3,2,1,0:T(8,128)} %pad_maximum_fusion.3), channel_id=1, source_target_pairs={{3,0},{0,1},{1,2},{2,3},{7,4},{4,5},{5,6},{6,7},{11,8},{8,9},{9,10... | collective-permute-start | bytes 1572872 | tf_op jit(solution)/shard_map/ppermute | solution.py:41
  73.9 24.6 %collective-permute-start.7 = (bf16[64,512]{1,0:T(8,128)(2,1)S(1)}, bf16[64,512]{1,0:T(8,128)(2,1)S(1)}, u32[]{:S(2)}, u32[]{:S(2)}) collective-permute-start(bf16[64,512]{1,0:T(8,128)(2,1)S(1)} %bitcast.271), channel_id=1, source_target_pairs={{0,508},{4,0},{8,4},{12,8},{16,12},{20,16},{24,20},{28,24},{32,28}... | collective-permute-start | bytes 196616 | tf_op jit(solution)/shard_map/ppermute | solution.py:77
  78.2 20.2 %collective-permute-start.8 = (bf16[64,512]{1,0:T(8,128)(2,1)S(1)}, bf16[64,512]{1,0:T(8,128)(2,1)S(1)}, u32[]{:S(2)}, u32[]{:S(2)}) collective-permute-start(bf16[64,512]{1,0:T(8,128)(2,1)S(1)} %bitcast.270), channel_id=1, source_target_pairs={{0,256},{4,260},{8,264},{12,268},{16,272},{20,276},{24,280},{28,28... | collective-permute-start | bytes 196616 | tf_op jit(solution)/shard_map/ppermute | solution.py:77
  85.8 12.7 %collective-permute-start.6 = (bf16[64,512]{1,0:T(8,128)(2,1)S(1)}, bf16[64,512]{1,0:T(8,128)(2,1)S(1)}, u32[]{:S(2)}, u32[]{:S(2)}) collective-permute-start(bf16[64,512]{1,0:T(8,128)(2,1)S(1)} %bitcast.269), channel_id=1, source_target_pairs={{0,4},{4,8},{8,12},{12,16},{16,20},{20,24},{24,28},{28,32},{32,36}... | collective-permute-start | bytes 196616 | tf_op jit(solution)/shard_map/ppermute | solution.py:77
  99.1 10.9 %collective-permute-start.12 = (bf16[64,512]{1,0:T(8,128)(2,1)S(1)}, bf16[64,512]{1,0:T(8,128)(2,1)S(1)}, u32[]{:S(2)}, u32[]{:S(2)}) collective-permute-start(bf16[64,512]{1,0:T(8,128)(2,1)S(1)} %get-tuple-element.71), channel_id=1, source_target_pairs={{0,4},{4,8},{8,12},{12,16},{16,20},{20,24},{24,28},{28,32},{32,36}... | collective-permute-start | bytes 196616 | tf_op jit(solution)/shard_map/ppermute | solution.py:77
  101.1 10.4 %collective-permute-start.14 = (bf16[64,512]{1,0:T(8,128)(2,1)S(1)}, bf16[64,512]{1,0:T(8,128)(2,1)S(1)}, u32[]{:S(2)}, u32[]{:S(2)}) collective-permute-start(bf16[64,512]{1,0:T(8,128)(2,1)S(1)} %get-tuple-element.72), channel_id=1, source_target_pairs={{0,256},{4,260},{8,264},{12,268},{16,272},{20,276},{24,280},{28,28... | collective-permute-start | bytes 196616 | tf_op jit(solution)/shard_map/ppermute | solution.py:77
  103.3 8.6 %collective-permute-start.13 = (bf16[64,512]{1,0:T(8,128)(2,1)S(1)}, bf16[64,512]{1,0:T(8,128)(2,1)S(1)}, u32[]{:S(2)}, u32[]{:S(2)}) collective-permute-start(bf16[64,512]{1,0:T(8,128)(2,1)S(1)} %get-tuple-element.73), channel_id=1, source_target_pairs={{0,508},{4,0},{8,4},{12,8},{16,12},{20,16},{24,20},{28,24},{32,28}... | collective-permute-start | bytes 196616 | tf_op jit(solution)/shard_map/ppermute | solution.py:77
  114.2 16.4 %collective-permute-start.15 = (bf16[64,512]{1,0:T(8,128)(2,1)S(1)}, bf16[64,512]{1,0:T(8,128)(2,1)S(1)}, u32[]{:S(2)}, u32[]{:S(2)}) collective-permute-start(bf16[64,512]{1,0:T(8,128)(2,1)S(1)} %get-tuple-element.68), channel_id=1, source_target_pairs={{0,4},{4,8},{8,12},{12,16},{16,20},{20,24},{24,28},{28,32},{32,36}... | collective-permute-start | bytes 196616 | tf_op jit(solution)/shard_map/ppermute | solution.py:77
  116.1 14.5 %collective-permute-start.17 = (bf16[64,512]{1,0:T(8,128)(2,1)S(1)}, bf16[64,512]{1,0:T(8,128)(2,1)S(1)}, u32[]{:S(2)}, u32[]{:S(2)}) collective-permute-start(bf16[64,512]{1,0:T(8,128)(2,1)S(1)} %get-tuple-element.69), channel_id=1, source_target_pairs={{0,256},{4,260},{8,264},{12,268},{16,272},{20,276},{24,280},{28,28... | collective-permute-start | bytes 196616 | tf_op jit(solution)/shard_map/ppermute | solution.py:77
  123.7 8.6 %collective-permute-start.16 = (bf16[64,512]{1,0:T(8,128)(2,1)S(1)}, bf16[64,512]{1,0:T(8,128)(2,1)S(1)}, u32[]{:S(2)}, u32[]{:S(2)}) collective-permute-start(bf16[64,512]{1,0:T(8,128)(2,1)S(1)} %get-tuple-element.70), channel_id=1, source_target_pairs={{0,508},{4,0},{8,4},{12,8},{16,12},{20,16},{24,20},{28,24},{32,28}... | collective-permute-start | bytes 196616 | tf_op jit(solution)/shard_map/ppermute | solution.py:77
  133.0 11.1 %collective-permute-start.18 = (bf16[64,512]{1,0:T(8,128)(2,1)S(1)}, bf16[64,512]{1,0:T(8,128)(2,1)S(1)}, u32[]{:S(2)}, u32[]{:S(2)}) collective-permute-start(bf16[64,512]{1,0:T(8,128)(2,1)S(1)} %get-tuple-element.65), channel_id=1, source_target_pairs={{0,4},{4,8},{8,12},{12,16},{16,20},{20,24},{24,28},{28,32},{32,36}... | collective-permute-start | bytes 196616 | tf_op jit(solution)/shard_map/ppermute | solution.py:77
  134.9 10.1 %collective-permute-start.20 = (bf16[64,512]{1,0:T(8,128)(2,1)S(1)}, bf16[64,512]{1,0:T(8,128)(2,1)S(1)}, u32[]{:S(2)}, u32[]{:S(2)}) collective-permute-start(bf16[64,512]{1,0:T(8,128)(2,1)S(1)} %get-tuple-element.66), channel_id=1, source_target_pairs={{0,256},{4,260},{8,264},{12,268},{16,272},{20,276},{24,280},{28,28... | collective-permute-start | bytes 196616 | tf_op jit(solution)/shard_map/ppermute | solution.py:77
  137.1 8.8 %collective-permute-start.19 = (bf16[64,512]{1,0:T(8,128)(2,1)S(1)}, bf16[64,512]{1,0:T(8,128)(2,1)S(1)}, u32[]{:S(2)}, u32[]{:S(2)}) collective-permute-start(bf16[64,512]{1,0:T(8,128)(2,1)S(1)} %get-tuple-element.67), channel_id=1, source_target_pairs={{0,508},{4,0},{8,4},{12,8},{16,12},{20,16},{24,20},{28,24},{32,28}... | collective-permute-start | bytes 196616 | tf_op jit(solution)/shard_map/ppermute | solution.py:77
  (5 other events, 5.3 us)
